TPU v7x, 32 devices: a whole 2x2x4 slice. The times are simulated.
32 devices in a mesh: dp: 2 (over x), seq: 8 (over z, y), tensor: 2 (over core).
Axes of the slice: x: 2, y: 2, z: 4, core: 2. Of those that a mesh axis runs over, the one named last changes fastest.
Arguments:
- queries: bfloat16 [2, 1024, 1536], P('dp', 'seq', 'tensor')
- keys: bfloat16 [2, 1024, 1536], P('dp', 'seq', 'tensor')
- values: bfloat16 [2, 1024, 1536], P('dp', 'seq', 'tensor'), may hold values from -6 to 6
- out_weight: bfloat16 [1536, 1536], P('tensor'), may hold values from -0.15625 to 0.15625
- residual: bfloat16 [2, 1024, 1536], P('dp', 'seq', 'tensor'), may hold values from -1.1953125 to 1.1953125
- lengths: int32 [2], P('dp'), may hold values from 512 to 1024
- grad_out: bfloat16 [2, 1024, 1536], P('dp', 'seq', 'tensor'), may hold values from -6 to 6
Outputs:
- block_out: bfloat16 [2, 1024, 1536], P('dp', 'seq', 'tensor')
- grad_queries: bfloat16 [2, 1024, 1536], P('dp', 'seq', 'tensor')
- grad_keys: bfloat16 [2, 1024, 1536], P('dp', 'seq', 'tensor')
- grad_values: bfloat16 [2, 1024, 1536], P('dp', 'seq', 'tensor')
- grad_weight: float32 [1536, 1536], P('tensor', ('dp', 'seq'))
Inputs may be any that keep to these rules, and one draw needn't show every extreme that they name: Frames at positions from lengths[b] on are padding.
All inputs are finite; a program needn't handle non-finite values.
Results may differ from a plain program's by a relative error of at most 0.014.
Values may be sent and summed in bfloat16 or wider, within the bound.
No kernel may reach another device: no remote copies, remote signals or barrier semaphores. Data moves between devices by JAX's collectives and lax.ppermute only.
A program may use at most 64 MiB of HBM per device.

v0:
```python
import math

import jax
import jax.numpy as jnp
from jax import lax
from jax.sharding import PartitionSpec as P


HEAD_DIM = 96


block_rows = 1024


def split_heads(rows):
    return rows.reshape(rows.shape[0], -1, HEAD_DIM)


def join_heads(blocks):
    return jnp.transpose(blocks, (1, 0, 2)).reshape(blocks.shape[1], -1)


def gather_rows(x, axis_name):
    n = lax.axis_size(axis_name)
    spread = jnp.broadcast_to(x[None], (n,) + x.shape)
    return lax.all_to_all(spread, axis_name, 0, 0, tiled=True)


def ring_gather(x, axis_name, flat=False):
    n = lax.axis_size(axis_name)
    me = lax.axis_index(axis_name)
    if n % 2 == 0:
        ring = list(range(0, n, 2)) + list(range(n - 1, 0, -2))
    else:
        ring = list(range(n))
    place = [0] * n
    for i, d in enumerate(ring):
        place[d] = i
    ring_ids = jnp.array(ring, jnp.int32)
    here = jnp.array(place, jnp.int32)[me]
    to_next = [(ring[i], ring[(i + 1) % n]) for i in range(n)]
    to_prev = [(ring[(i + 1) % n], ring[i]) for i in range(n)]
    if flat:
        gathered = jnp.zeros((n * x.shape[0],) + x.shape[1:], x.dtype)

        def put(buffer, block, source):
            return lax.dynamic_update_slice_in_dim(buffer, block, source * x.shape[0], 0)
    else:
        gathered = jnp.zeros((n,) + x.shape, x.dtype)

        def put(buffer, block, source):
            return lax.dynamic_update_index_in_dim(buffer, block, source, 0)
    gathered = put(gathered, x, me)
    ahead = x
    behind = x
    for step in range(1, n // 2 + 1):
        ahead = lax.ppermute(ahead, axis_name, to_next)
        source = ring_ids[(here - step + n) % n]
        gathered = put(gathered, ahead, source)
        if step <= (n - 1) // 2:
            behind = lax.ppermute(behind, axis_name, to_prev)
            source = ring_ids[(here + step) % n]
            gathered = put(gathered, behind, source)
    return gathered


def scatter_sum(x, axis_name, axis):
    n = lax.axis_size(axis_name)
    shape = x.shape[:axis] + (n, x.shape[axis] // n) + x.shape[axis + 1:]
    pieces = jnp.moveaxis(x.reshape(shape), axis, 0)
    return jnp.sum(lax.all_to_all(pieces, axis_name, 0, 0, tiled=True), axis=0)


def by_blocks(step_fn, carry, piece):
    count = piece[0].shape[0]
    size = count if count <= block_rows else math.gcd(count, block_rows)

    def one(index, state):
        first = index * size
        part = tuple((lax.dynamic_slice_in_dim(item, first, size, 0) for item in piece))
        return step_fn(state, part, first)

    return lax.fori_loop(0, count // size, one, carry)


def shards_body(queries, keys, values, out_weight, residual, lengths, grad_out):
    scale = 1.0 / math.sqrt(HEAD_DIM)
    highest = lax.Precision.HIGHEST
    own_q = queries[0]
    own_k = keys[0]
    own_v = values[0]
    frames_here = own_q.shape[0]
    length = lengths[0]
    q_heads = split_heads(own_q)
    k_heads = split_heads(own_k)
    v_heads = split_heads(own_v)
    heads_here = q_heads.shape[1]
    key_pos = lax.axis_index("seq") * frames_here + jnp.arange(frames_here, dtype=jnp.int32)

    def masked_scores(left, right, positions):
        s = jnp.einsum("ihc,jhc->hij", left, right, preferred_element_type=jnp.float32) * scale
        return jnp.where(positions[None, None, :] < length, s, -1e30)

    def forward_step(state, part, start):
        run_max, run_sum, total = state
        k_rows, v_rows = part
        positions = start + jnp.arange(k_rows.shape[0], dtype=jnp.int32)
        s = masked_scores(q_heads, split_heads(k_rows), positions)
        new_max = jnp.maximum(run_max, jnp.max(s, axis=2))
        factor = jnp.exp(run_max - new_max)
        weights = jnp.exp(s - new_max[:, :, None])
        run_sum = run_sum * factor + jnp.sum(weights, axis=2)
        total = total * factor[:, :, None] + jnp.einsum(
            "hij,jhc->hic", weights, split_heads(v_rows).astype(jnp.float32), precision=highest
        )
        return (new_max, run_sum, total)

    start_state = (
        jnp.full((heads_here, frames_here), -1e30, jnp.float32),
        jnp.zeros((heads_here, frames_here), jnp.float32),
        jnp.zeros((heads_here, frames_here, HEAD_DIM), jnp.float32),
    )
    grad_full = lax.all_gather(grad_out[0], "tensor", axis=1, tiled=True)
    grad_attn = lax.dot_general(
        grad_full, out_weight, (((1,), (1,)), ((), ())), preferred_element_type=jnp.float32
    ).astype(jnp.bfloat16)
    width = own_k.shape[1]
    kv_rows = jnp.concatenate([own_k, own_v], axis=1)
    kv_all = ring_gather(kv_rows, "seq").reshape(-1, 2 * width)
    n_seq = lax.axis_size("seq")
    n_dp = lax.axis_size("dp")
    col_width = grad_full.shape[1] // (n_dp * n_seq)
    g_cols = jnp.transpose(grad_full.reshape(frames_here, n_dp, n_seq, col_width), (2, 0, 1, 3))
    g_cols = g_cols.reshape(n_seq, frames_here, n_dp * col_width)
    g_mine = lax.all_to_all(g_cols, "seq", 0, 0, tiled=True).reshape(-1, n_dp * col_width)
    qg_rows = jnp.concatenate([own_q, grad_attn], axis=1)
    qg_all = ring_gather(qg_rows, "seq", flat=True)
    k_all = kv_all[:, :width]
    v_all = kv_all[:, width:]
    run_max, run_sum, total = by_blocks(forward_step, start_state, (k_all, v_all))
    log_sum = run_max + jnp.log(run_sum)
    attn_full = total / run_sum[:, :, None]
    attn = join_heads(attn_full).astype(jnp.bfloat16)
    partial_out = jnp.dot(attn, out_weight, preferred_element_type=jnp.float32)
    mixed = scatter_sum(partial_out, "tensor", 1)
    block_out = (residual[0].astype(jnp.float32) + mixed).astype(jnp.bfloat16)
    attn_all = lax.all_gather(attn, "seq", axis=0, tiled=True)
    weight_term = lax.dot_general(
        attn_all, g_mine, (((0,), (0,)), ((), ())), preferred_element_type=jnp.float32
    )
    grad_weight = scatter_sum(weight_term, "dp", 1)
    g_heads = split_heads(grad_attn)
    delta = jnp.sum(jnp.transpose(g_heads, (1, 0, 2)).astype(jnp.float32) * attn_full, axis=2)

    def query_step(grad_q, part, start):
        k_rows, v_rows = part
        positions = start + jnp.arange(k_rows.shape[0], dtype=jnp.int32)
        s = masked_scores(q_heads, split_heads(k_rows), positions)
        probs = jnp.exp(s - log_sum[:, :, None])
        dots = jnp.einsum(
            "ihc,jhc->hij", g_heads, split_heads(v_rows), preferred_element_type=jnp.float32
        )
        dscores = (probs * (dots - delta[:, :, None]) * scale).astype(jnp.bfloat16)
        return grad_q + jnp.einsum(
            "hij,jhc->hic", dscores, split_heads(k_rows), preferred_element_type=jnp.float32
        )

    empty_q = jnp.zeros((heads_here, frames_here, HEAD_DIM), jnp.float32)
    grad_q = by_blocks(query_step, empty_q, (k_all, v_all))
    stats = gather_rows(jnp.concatenate([log_sum, delta], axis=0), "seq")
    stats = jnp.transpose(stats, (1, 0, 2)).reshape(2 * heads_here, -1)

    def key_step(state, part, start):
        grad_k, grad_v = state
        q_rows, g_rows, lse_rows, delta_rows = part
        q_part = split_heads(q_rows.astype(jnp.bfloat16))
        g_part = split_heads(g_rows.astype(jnp.bfloat16))
        s = masked_scores(q_part, k_heads, key_pos)
        probs = jnp.exp(s - lse_rows.T[:, :, None])
        dots = jnp.einsum("ihc,jhc->hij", g_part, v_heads, preferred_element_type=jnp.float32)
        dscores = (probs * (dots - delta_rows.T[:, :, None]) * scale).astype(jnp.bfloat16)
        grad_k = grad_k + jnp.einsum(
            "hij,ihc->hjc", dscores, q_part, preferred_element_type=jnp.float32
        )
        grad_v = grad_v + jnp.einsum(
            "hij,ihc->hjc", probs.astype(jnp.bfloat16), g_part, preferred_element_type=jnp.float32
        )
        return (grad_k, grad_v)

    grad_k, grad_v = by_blocks(
        key_step,
        (empty_q, empty_q),
        (
            qg_all[:, :width],
            qg_all[:, width:],
            stats[:heads_here].T,
            stats[heads_here:].T,
        ),
    )
    return (
        block_out[None],
        join_heads(grad_q).astype(jnp.bfloat16)[None],
        join_heads(grad_k).astype(jnp.bfloat16)[None],
        join_heads(grad_v).astype(jnp.bfloat16)[None],
        grad_weight,
    )


def solution(mesh):
    in_specs = (
        P("dp", "seq", "tensor"),
        P("dp", "seq", "tensor"),
        P("dp", "seq", "tensor"),
        P("tensor", None),
        P("dp", "seq", "tensor"),
        P("dp"),
        P("dp", "seq", "tensor"),
    )
    out_specs = (
        P("dp", "seq", "tensor"),
        P("dp", "seq", "tensor"),
        P("dp", "seq", "tensor"),
        P("dp", "seq", "tensor"),
        P("tensor", ("dp", "seq")),
    )
    return jax.shard_map(shards_body, mesh=mesh, in_specs=in_specs, out_specs=out_specs, check_vma=False)
```

profile of v0, /device:TPU:0, one launch (start us, length us, event | category | flops | bytes accessed | tf_op | source)
XLA Modules:
  0.0 249.4 jit_solution(13673011330421552073)
XLA Ops:
  9.0 3.1 %collective-permute-start = (bf16[128,1536]{1,0:T(8,128)(2,1)}, bf16[128,1536]{1,0:T(8,128)(2,1)}, u32[]{:S(2)}, u32[]{:S(2)}) collective-permute-start(bf16[128,1536]{1,0:T(8,128)(2,1)} %pad_maximum_fusion), channel_id=1, source_target_pairs={{0,4},{4,8},{8,12},{12,14},{14,10},{10,6},{6,2},{2,0},{1,5},{5,9},... | collective-permute-start | bytes 1179656 | tf_op jit(solution)/shard_map/ppermute | solution.py:57
  13.2 2.1 all-gather
  15.2 2.6 %convolution_convert_fusion = bf16[128,768]{1,0:T(8,128)(2,1)S(1)} fusion(bf16[768,1536]{1,0:T(8,128)(2,1)} %param.14, bf16[1,128,1536]{1,2,0:T(8,128)(2,1)S(1)} %all-gather), kind=kOutput, calls=%fused_computation.33 | convolution fusion | flops 302088192 | bytes 2949120 | tf_op jit(solution)/shard_map/dot_general | solution.py:124
  18.7 2.0 collective-permute-start.7
  21.5 6.3 %all-to-all-start.2 = ((bf16[8,128,192]{1,2,0:T(8,128)(2,1)}), bf16[8,128,192]{1,2,0:T(8,128)(2,1)}, u32[]{:S(2)}, u32[]{:S(2)}) async-start(bf16[8,128,192]{1,2,0:T(8,128)(2,1)} %bitcast.65), calls=%async_computation.2 | async-start | bytes 786432 | tf_op jit(solution)/shard_map/all_to_all | solution.py:135
  59.3 4.3 %copy.95 = bf16[1536,768]{1,0:T(8,128)(2,1)} copy(bf16[1536,768]{0,1:T(8,128)(2,1)} %bitcast.158) | data formatting | bytes 4718592 | tf_op jit(solution)/shard_map/dot_general | solution.py:144
  68.0 1.9 copy.75
  69.9 2.0 collective-permute-start.9
  73.2 2.0 collective-permute-start.2
  83.4 2.1 collective-permute-start.11
  87.5 3.2 %collective-permute-done.2 = bf16[128,1536]{1,0:T(8,128)(2,1)} collective-permute-done((bf16[128,1536]{1,0:T(8,128)(2,1)}, bf16[128,1536]{1,0:T(8,128)(2,1)}, u32[]{:S(2)}, u32[]{:S(2)}) %collective-permute-start.2) | collective-permute-done | bytes 393248 | tf_op jit(solution)/shard_map/ppermute | solution.py:57
  90.6 2.0 collective-permute-start.4
  94.0 2.1 bitcast_dynamic-update-slice_fusion.2
  97.9 7.9 %collective-permute-done.4 = bf16[128,1536]{1,0:T(8,128)(2,1)} collective-permute-done((bf16[128,1536]{1,0:T(8,128)(2,1)}, bf16[128,1536]{1,0:T(8,128)(2,1)}, u32[]{:S(2)}, u32[]{:S(2)}) %collective-permute-start.4) | collective-permute-done | bytes 393248 | tf_op jit(solution)/shard_map/ppermute | solution.py:57
  107.6 3.8 %copy.63 = bf16[8,128,1536]{1,0,2:T(8,128)(2,1)S(1)} copy(bf16[8,128,1536]{2,1,0:T(8,128)(2,1)} %bitcast_dynamic-update-slice_fusion) | data formatting | bytes 6291456 | tf_op jit(solution)/shard_map/jit(dynamic_update_index_in_dim)/dynamic_update_slice | solution.py:52
  113.2 17.8 %dynamic_update_slice.55 = bf16[8,128,1536]{1,0,2:T(8,128)(2,1)S(1)} dynamic-update-slice(bf16[8,128,1536]{1,0,2:T(8,128)(2,1)S(1)} %copy.63, bf16[1,128,1536]{1,0,2:T(2,128)(2,1)} %copy.64, s32[]{:T(128)S(6)} %select_n.196, s32[]{:T(128)} %constant.181.clone.1, s32[]{:T(128)} %constant.181.clone.1) | dynamic-update-slice | bytes 786436 | tf_op jit(solution)/shard_map/jit(dynamic_update_index_in_dim)/dynamic_update_slice | solution.py:52
  135.8 1.9 copy.80
  140.4 3.1 %collective-permute-done.6 = bf16[128,1536]{1,0:T(8,128)(2,1)} collective-permute-done((bf16[128,1536]{1,0:T(8,128)(2,1)}, bf16[128,1536]{1,0:T(8,128)(2,1)}, u32[]{:S(2)}, u32[]{:S(2)}) %collective-permute-start.6) | collective-permute-done | bytes 393248 | tf_op jit(solution)/shard_map/ppermute | solution.py:57
  143.4 3.0 %copy.65 = bf16[1,128,1536]{1,0,2:T(2,128)(2,1)} copy(bf16[1,128,1536]{2,1,0:T(8,128)(2,1)} %bitcast.22) | data formatting | bytes 786432 | tf_op jit(solution)/shard_map/jit(dynamic_update_index_in_dim)/broadcast_in_dim | solution.py:52
  146.4 17.8 %dynamic_update_slice.56 = bf16[8,128,1536]{1,0,2:T(8,128)(2,1)S(1)} dynamic-update-slice(bf16[8,128,1536]{1,0,2:T(8,128)(2,1)S(1)} %dynamic_update_slice.55, bf16[1,128,1536]{1,0,2:T(2,128)(2,1)} %copy.65, s32[]{:T(128)S(6)} %select_n.199, s32[]{:T(128)} %constant.181.clone.1, s32[]{:T(128)} %constant.181.clone.1) | dynamic-update-slice | bytes 786436 | tf_op jit(solution)/shard_map/jit(dynamic_update_index_in_dim)/dynamic_update_slice | solution.py:52
  168.3 4.5 %fusion.35 = (bf16[128,8,96]{0,2,1:T(8,128)(2,1)S(1)}, f32[8,128,96]{1,2,0:T(8,128)}) fusion(f32[128,8]{0,1:T(8,128)S(1)} %bitcast_add_fusion.2, f32[128,8]{0,1:T(8,128)S(1)} %get-tuple-element.109, bf16[1024,8,96]{0,2,1:T(8,128)(2,1)S(1)} %bitcast.169, f32[8,1024,128]{2,1,0:T(8,128)S(1)} %get-tuple-element.131, f32[8,128]{1,0:T(8,128)S(1)} %broadcast_maximum_fusion, ...), kind=kOutput, calls=%fused_computation.44 | convolution fusion | flops 1211400192 | bytes 6370304 | tf_op jit(solution)/shard_map/while/body/eval_jaxpr/hij,jhc->hic/dot_general | solution.py:113
  174.6 4.6 %all-to-all-start = ((f32[2,128,768]{2,1,0:T(8,128)}), f32[2,128,768]{2,1,0:T(8,128)}, u32[]{:S(2)}, u32[]{:S(2)}) async-start(f32[2,128,768]{2,1,0:T(8,128)} %convolution_bitcast_fusion), calls=%async_computation | async-start | bytes 1572864 | tf_op jit(solution)/shard_map/all_to_all | solution.py:71
  183.1 5.7 %all-to-all-start.1 = ((f32[8,16,128]{2,1,0:T(8,128)}), f32[8,16,128]{2,1,0:T(8,128)}, u32[]{:S(2)}, u32[]{:S(2)}) async-start(f32[8,16,128]{2,1,0:T(8,128)} %broadcast_in_dim.116), calls=%async_computation.1 | async-start | bytes 131072 | tf_op jit(solution)/shard_map/all_to_all | solution.py:26
  188.8 2.0 reduce_sum.43
  193.6 2.8 %fusion.49 = f32[8,1024,128]{2,1,0:T(8,128)} fusion(bf16[1024,8,96]{0,2,1:T(8,128)(2,1)S(1)} %bitcast.162, bf16[128,8,96]{0,2,1:T(8,128)(2,1)S(1)} %bitcast.173), kind=kOutput, calls=%fused_computation.81 | convolution fusion | flops 201326592 | bytes 5963776 | tf_op jit(solution)/shard_map/while/body/eval_jaxpr/ihc,jhc->hij/dot_general | solution.py:101
  196.4 6.0 %fusion.26 = bf16[8,128,96]{1,2,0:T(8,128)(2,1)} fusion(bf16[1024,8,96]{0,2,1:T(8,128)(2,1)S(1)} %bitcast.161, f32[8,1024,128]{2,1,0:T(8,128)} %copy-done, bf16[128,8,96]{0,2,1:T(8,128)(2,1)} %bitcast.178, bf16[1024,8,96]{0,2,1:T(8,128)(2,1)} %bitcast.170, f32[8,128]{1,0:T(8,128)S(1)} %fusion.31, f32[8,128]{1,0:T(8,128)S(1)} %get-tuple-element.107, ...), kind=kOutput, calls=%fused_computation.30 | convolution fusion | flops 410091520 | bytes 7742464 | tf_op jit(solution)/shard_map/while/body/eval_jaxpr/hij,jhc->hic/dot_general | solution.py:164
  206.6 5.9 %fusion.27 = bf16[8,128,96]{1,2,0:T(8,128)(2,1)S(1)} fusion(bf16[1024,8,96]{0,2,1:T(8,128)(2,1)S(1)} %bitcast.163, f32[8,1024,128]{2,1,0:T(8,128)} %fusion.49, bf16[1024,8,96]{0,2,1:T(8,128)(2,1)} %bitcast.171, bf16[128,8,96]{0,2,1:T(8,128)(2,1)} %bitcast.182, f32[8,1024]{1,0:T(8,128)S(1)} %get-tuple-element.106, f32[8,1024]{1,0:T(8,128)S(1)} %get-tuple-element.105, ...), kind=kOutput, calls=%fused_computation.31 | convolution fusion | flops 410091520 | bytes 7798912 | tf_op jit(solution)/shard_map/while/body/eval_jaxpr/hij,ihc->hjc/dot_general | solution.py:182
  213.3 14.3 %all-gather.3.cloned.1.call-done = bf16[1024,768]{1,0:T(8,128)(2,1)} async-done(((bf16[128,768]{1,0:T(8,128)(2,1)}), bf16[1024,768]{1,0:T(8,128)(2,1)}) %all-gather.3.cloned.1.call-update) | async-done | bytes 1572880 | tf_op jit(solution)/shard_map/all_gather | solution.py:147
  227.7 2.7 %fusion.23 = f32[2,768,96]{1,2,0:T(8,128)} fusion(bf16[2,96,1024]{2,1,0:T(8,128)(2,1)S(1)} %bitcast.180, bf16[1024,768]{1,0:T(8,128)(2,1)} %all-gather.3.cloned.1.call-done), kind=kOutput, calls=%fused_computation.29 | convolution fusion | flops 301989888 | bytes 2555904 | tf_op jit(solution)/shard_map/dot_general | solution.py:148
  230.4 3.5 %all-to-all-start.3 = ((f32[2,768,96]{1,2,0:T(8,128)}), f32[2,768,96]{1,2,0:T(8,128)S(1)}, u32[]{:S(2)}, u32[]{:S(2)}) async-start(f32[2,768,96]{1,2,0:T(8,128)} %fusion.23), calls=%async_computation.3 | async-start | bytes 1179648 | tf_op jit(solution)/shard_map/all_to_all | solution.py:71
  233.9 3.3 %fusion.28 = bf16[8,128,96]{1,2,0:T(8,128)(2,1)S(1)} fusion(bf16[1024,8,96]{0,2,1:T(8,128)(2,1)S(1)} %bitcast.172, f32[8,1024,128]{2,1,0:T(8,128)} %fusion.49, f32[8,1024]{1,0:T(8,128)S(1)} %get-tuple-element.105, pred[128]{0:T(512)(128)(4,1)S(1)} %copy-done.21), kind=kOutput, calls=%fused_computation.32 | convolution fusion | flops 205619200 | bytes 5996672 | tf_op jit(solution)/shard_map/while/body/eval_jaxpr/hij,ihc->hjc/dot_general | solution.py:185
  238.0 3.8 %all-to-all-done.3 = f32[2,768,96]{1,2,0:T(8,128)S(1)} async-done(((f32[2,768,96]{1,2,0:T(8,128)}), f32[2,768,96]{1,2,0:T(8,128)S(1)}, u32[]{:S(2)}, u32[]{:S(2)}) %all-to-all-start.3) | async-done | bytes 589856 | tf_op jit(solution)/shard_map/all_to_all | solution.py:71
  (124 shorter events, 61.9 us)
Async XLA Ops:
  7.2 10.7 %copy-start.15 = (bf16[1,128,768]{2,1,0:T(8,128)(2,1)S(1)}, bf16[1,128,768]{2,1,0:T(8,128)(2,1)}, u32[]{:S(2)}) copy-start(bf16[1,128,768]{2,1,0:T(8,128)(2,1)} %param.11) | copy-start | bytes 589828
  9.0 64.2 %collective-permute-start = (bf16[128,1536]{1,0:T(8,128)(2,1)}, bf16[128,1536]{1,0:T(8,128)(2,1)}, u32[]{:S(2)}, u32[]{:S(2)}) collective-permute-start(bf16[128,1536]{1,0:T(8,128)(2,1)} %pad_maximum_fusion), channel_id=1, source_target_pairs={{0,4},{4,8},{8,12},{12,14},{14,10},{10,6},{6,2},{2,0},{1,5},{5,9},... | collective-permute-start | bytes 1179656 | tf_op jit(solution)/shard_map/ppermute | solution.py:57
  12.1 64.3 %collective-permute-start.1 = (bf16[128,1536]{1,0:T(8,128)(2,1)}, bf16[128,1536]{1,0:T(8,128)(2,1)}, u32[]{:S(2)}, u32[]{:S(2)}) collective-permute-start(bf16[128,1536]{1,0:T(8,128)(2,1)} %pad_maximum_fusion), channel_id=1, source_target_pairs={{4,0},{8,4},{12,8},{14,12},{10,14},{6,10},{2,6},{0,2},{5,1},{9,5},... | collective-permute-start | bytes 1179656 | tf_op jit(solution)/shard_map/ppermute | solution.py:61
  17.9 14.4 %copy-start.8 = (bf16[1,128,768]{2,1,0:T(8,128)(2,1)S(1)}, bf16[1,128,768]{2,1,0:T(8,128)(2,1)}, u32[]{:S(2)}) copy-start(bf16[1,128,768]{2,1,0:T(8,128)(2,1)} %param.12) | copy-start | bytes 589828
  17.9 14.4 %copy-start.9 = (bf16[1,128,768]{2,1,0:T(8,128)(2,1)S(1)}, bf16[1,128,768]{2,1,0:T(8,128)(2,1)}, u32[]{:S(2)}) copy-start(bf16[1,128,768]{2,1,0:T(8,128)(2,1)} %param.13) | copy-start | bytes 589828
  18.7 49.3 %collective-permute-start.7 = (bf16[128,1536]{1,0:T(8,128)(2,1)}, bf16[128,1536]{1,0:T(8,128)(2,1)}, u32[]{:S(2)}, u32[]{:S(2)}) collective-permute-start(bf16[128,1536]{1,0:T(8,128)(2,1)} %pad_maximum_fusion.1), channel_id=1, source_target_pairs={{0,4},{4,8},{8,12},{12,14},{14,10},{10,6},{6,2},{2,0},{1,5},{5,9},... | collective-permute-start | bytes 1179656 | tf_op jit(solution)/shard_map/ppermute | solution.py:57
  20.7 51.2 %collective-permute-start.8 = (bf16[128,1536]{1,0:T(8,128)(2,1)}, bf16[128,1536]{1,0:T(8,128)(2,1)}, u32[]{:S(2)}, u32[]{:S(2)}) collective-permute-start(bf16[128,1536]{1,0:T(8,128)(2,1)} %pad_maximum_fusion.1), channel_id=1, source_target_pairs={{4,0},{8,4},{12,8},{14,12},{10,14},{6,10},{2,6},{0,2},{5,1},{9,5},... | collective-permute-start | bytes 1179656 | tf_op jit(solution)/shard_map/ppermute | solution.py:61
  21.5 58.7 %all-to-all-start.2 = ((bf16[8,128,192]{1,2,0:T(8,128)(2,1)}), bf16[8,128,192]{1,2,0:T(8,128)(2,1)}, u32[]{:S(2)}, u32[]{:S(2)}) async-start(bf16[8,128,192]{1,2,0:T(8,128)(2,1)} %bitcast.65), calls=%async_computation.2 | async-start | bytes 786432 | tf_op jit(solution)/shard_map/all_to_all | solution.py:135
  32.2 8.1 %copy-start.18 = (s32[8]{0:T(128)S(1)}, s32[8]{0:T(128)}, u32[]{:S(2)}) copy-start(s32[8]{0:T(128)} %constant.196.clone) | copy-start | bytes 100
  67.9 99.4 %copy-start.19 = (pred[1024]{0:T(1024)(128)(4,1)}, pred[1024]{0:T(1024)(128)(4,1)S(1)}, u32[]{:S(2)}) copy-start(pred[1024]{0:T(1024)(128)(4,1)S(1)} %iota_compare_fusion) | copy-start | bytes 3076
  69.9 12.3 %collective-permute-start.9 = (bf16[128,1536]{1,0:T(8,128)(2,1)}, bf16[128,1536]{1,0:T(8,128)(2,1)}, u32[]{:S(2)}, u32[]{:S(2)}) collective-permute-start(bf16[128,1536]{1,0:T(8,128)(2,1)} %collective-permute-done.7), channel_id=1, source_target_pairs={{0,4},{4,8},{8,12},{12,14},{14,10},{10,6},{6,2},{2,0},{1,5},{5,9},... | collective-permute-start | bytes 1179656 | tf_op jit(solution)/shard_map/ppermute | solution.py:57
  73.2 12.4 %collective-permute-start.10 = (bf16[128,1536]{1,0:T(8,128)(2,1)}, bf16[128,1536]{1,0:T(8,128)(2,1)}, u32[]{:S(2)}, u32[]{:S(2)}) collective-permute-start(bf16[128,1536]{1,0:T(8,128)(2,1)} %collective-permute-done.8), channel_id=1, source_target_pairs={{4,0},{8,4},{12,8},{14,12},{10,14},{6,10},{2,6},{0,2},{5,1},{9,5},... | collective-permute-start | bytes 1179656 | tf_op jit(solution)/shard_map/ppermute | solution.py:61
  73.2 17.4 %collective-permute-start.2 = (bf16[128,1536]{1,0:T(8,128)(2,1)}, bf16[128,1536]{1,0:T(8,128)(2,1)}, u32[]{:S(2)}, u32[]{:S(2)}) collective-permute-start(bf16[128,1536]{1,0:T(8,128)(2,1)} %collective-permute-done), channel_id=1, source_target_pairs={{0,4},{4,8},{8,12},{12,14},{14,10},{10,6},{6,2},{2,0},{1,5},{5,9},... | collective-permute-start | bytes 1179656 | tf_op jit(solution)/shard_map/ppermute | solution.py:57
  76.4 17.6 %collective-permute-start.3 = (bf16[128,1536]{1,0:T(8,128)(2,1)}, bf16[128,1536]{1,0:T(8,128)(2,1)}, u32[]{:S(2)}, u32[]{:S(2)}) collective-permute-start(bf16[128,1536]{1,0:T(8,128)(2,1)} %collective-permute-done.1), channel_id=1, source_target_pairs={{4,0},{8,4},{12,8},{14,12},{10,14},{6,10},{2,6},{0,2},{5,1},{9,5},... | collective-permute-start | bytes 1179656 | tf_op jit(solution)/shard_map/ppermute | solution.py:61
  83.4 49.5 %collective-permute-start.11 = (bf16[128,1536]{1,0:T(8,128)(2,1)}, bf16[128,1536]{1,0:T(8,128)(2,1)}, u32[]{:S(2)}, u32[]{:S(2)}) collective-permute-start(bf16[128,1536]{1,0:T(8,128)(2,1)} %collective-permute-done.9), channel_id=1, source_target_pairs={{0,4},{4,8},{8,12},{12,14},{14,10},{10,6},{6,2},{2,0},{1,5},{5,9},... | collective-permute-start | bytes 1179656 | tf_op jit(solution)/shard_map/ppermute | solution.py:57
  87.4 48.4 %collective-permute-start.12 = (bf16[128,1536]{1,0:T(8,128)(2,1)}, bf16[128,1536]{1,0:T(8,128)(2,1)}, u32[]{:S(2)}, u32[]{:S(2)}) collective-permute-start(bf16[128,1536]{1,0:T(8,128)(2,1)} %collective-permute-done.10), channel_id=1, source_target_pairs={{4,0},{8,4},{12,8},{14,12},{10,14},{6,10},{2,6},{0,2},{5,1},{9,5},... | collective-permute-start | bytes 1179656 | tf_op jit(solution)/shard_map/ppermute | solution.py:61
  90.6 15.2 %collective-permute-start.4 = (bf16[128,1536]{1,0:T(8,128)(2,1)}, bf16[128,1536]{1,0:T(8,128)(2,1)}, u32[]{:S(2)}, u32[]{:S(2)}) collective-permute-start(bf16[128,1536]{1,0:T(8,128)(2,1)} %collective-permute-done.2), channel_id=1, source_target_pairs={{0,4},{4,8},{8,12},{12,14},{14,10},{10,6},{6,2},{2,0},{1,5},{5,9},... | collective-permute-start | bytes 1179656 | tf_op jit(solution)/shard_map/ppermute | solution.py:57
  93.9 11.9 %copy-start.1 = (bf16[1024,1536]{0,1:T(8,128)(2,1)}, bf16[1024,1536]{0,1:T(8,128)(2,1)S(1)}, u32[]{:S(2)}) copy-start(bf16[1024,1536]{0,1:T(8,128)(2,1)S(1)} %constant_dynamic-update-slice_fusion.5) | copy-start | bytes 9437188
  94.0 17.5 %collective-permute-start.5 = (bf16[128,1536]{1,0:T(8,128)(2,1)}, bf16[128,1536]{1,0:T(8,128)(2,1)S(1)}, u32[]{:S(2)}, u32[]{:S(2)}) collective-permute-start(bf16[128,1536]{1,0:T(8,128)(2,1)} %collective-permute-done.3), channel_id=1, source_target_pairs={{4,0},{8,4},{12,8},{14,12},{10,14},{6,10},{2,6},{0,2},{5,1},{9,5},... | collective-permute-start | bytes 1179656 | tf_op jit(solution)/shard_map/ppermute | solution.py:61
  131.1 12.4 %collective-permute-start.6 = (bf16[128,1536]{1,0:T(8,128)(2,1)}, bf16[128,1536]{1,0:T(8,128)(2,1)}, u32[]{:S(2)}, u32[]{:S(2)}) collective-permute-start(bf16[128,1536]{1,0:T(8,128)(2,1)} %collective-permute-done.4), channel_id=1, source_target_pairs={{0,4},{4,8},{8,12},{12,14},{14,10},{10,6},{6,2},{2,0},{1,5},{5,9},... | collective-permute-start | bytes 1179656 | tf_op jit(solution)/shard_map/ppermute | solution.py:57
  134.1 47.1 %collective-permute-start.13 = (bf16[128,1536]{1,0:T(8,128)(2,1)}, bf16[128,1536]{1,0:T(8,128)(2,1)}, u32[]{:S(2)}, u32[]{:S(2)}) collective-permute-start(bf16[128,1536]{1,0:T(8,128)(2,1)} %collective-permute-done.11), channel_id=1, source_target_pairs={{0,4},{4,8},{8,12},{12,14},{14,10},{10,6},{6,2},{2,0},{1,5},{5,9},... | collective-permute-start | bytes 1179656 | tf_op jit(solution)/shard_map/ppermute | solution.py:57
  172.8 7.3 %copy-start.16 = (bf16[128,768]{0,1:T(8,128)(2,1)S(1)}, bf16[128,768]{0,1:T(8,128)(2,1)}, u32[]{:S(2)}) copy-start(bf16[128,768]{0,1:T(8,128)(2,1)} %copy.71) | copy-start | bytes 589828
  174.6 16.2 %copy-start.2 = (bf16[1024,1536]{0,1:T(8,128)(2,1)S(1)}, bf16[1024,1536]{0,1:T(8,128)(2,1)}, u32[]{:S(2)}) copy-start(bf16[1024,1536]{0,1:T(8,128)(2,1)} %constant_dynamic-update-slice_fusion.2) | copy-start | bytes 9437188
  174.6 7.8 %all-to-all-start = ((f32[2,128,768]{2,1,0:T(8,128)}), f32[2,128,768]{2,1,0:T(8,128)}, u32[]{:S(2)}, u32[]{:S(2)}) async-start(f32[2,128,768]{2,1,0:T(8,128)} %convolution_bitcast_fusion), calls=%async_computation | async-start | bytes 1572864 | tf_op jit(solution)/shard_map/all_to_all | solution.py:71
  179.2 48.5 %all-gather.3.cloned.1.call-start = ((), (), s32[]{:S(2)}) async-start(), calls=%async_computation.4 | async-start | bytes 1769472 | tf_op jit(solution)/shard_map/all_gather | solution.py:147
  183.1 22.8 %all-to-all-start.1 = ((f32[8,16,128]{2,1,0:T(8,128)}), f32[8,16,128]{2,1,0:T(8,128)}, u32[]{:S(2)}, u32[]{:S(2)}) async-start(f32[8,16,128]{2,1,0:T(8,128)} %broadcast_in_dim.116), calls=%async_computation.1 | async-start | bytes 131072 | tf_op jit(solution)/shard_map/all_to_all | solution.py:26
  196.4 6.1 %copy-start.10 = (f32[128,768]{1,0:T(8,128)S(1)}, f32[128,768]{1,0:T(8,128)}, u32[]{:S(2)}) copy-start(f32[128,768]{1,0:T(8,128)} %reduce_sum.43) | copy-start | bytes 1179652
  196.4 10.2 %copy-start.7 = (bf16[1024,768]{0,1:T(8,128)(2,1)S(1)}, bf16[1024,768]{0,1:T(8,128)(2,1)}, u32[]{:S(2)}) copy-start(bf16[1024,768]{0,1:T(8,128)(2,1)} %copy-done.6) | copy-start | bytes 4718596
  196.4 10.2 %copy-start.21 = (pred[128]{0:T(512)(128)(4,1)S(1)}, pred[128]{0:T(512)(128)(4,1)}, u32[]{:S(2)}) copy-start(pred[128]{0:T(512)(128)(4,1)} %add_compare_fusion) | copy-start | bytes 388
  206.6 21.0 %copy-start.17 = (bf16[1024,192]{0,1:T(8,128)(2,1)S(1)}, bf16[1024,192]{0,1:T(8,128)(2,1)}, u32[]{:S(2)}) copy-start(bf16[1024,192]{0,1:T(8,128)(2,1)} %copy_bitcast_fusion.1) | copy-start | bytes 1179652
  212.5 21.4 %copy-start.12 = (bf16[1024,768]{0,1:T(8,128)(2,1)S(1)}, bf16[1024,768]{0,1:T(8,128)(2,1)}, u32[]{:S(2)}) copy-start(bf16[1024,768]{0,1:T(8,128)(2,1)} %get-tuple-element.101) | copy-start | bytes 4718596
  230.4 11.4 %all-to-all-start.3 = ((f32[2,768,96]{1,2,0:T(8,128)}), f32[2,768,96]{1,2,0:T(8,128)S(1)}, u32[]{:S(2)}, u32[]{:S(2)}) async-start(f32[2,768,96]{1,2,0:T(8,128)} %fusion.23), calls=%async_computation.3 | async-start | bytes 1179648 | tf_op jit(solution)/shard_map/all_to_all | solution.py:71
  (10 other events, 31.3 us)
Sparse Core Ops, SparseCore 0:
  182.2 45.4 all-gather.2
where the time goes:
time: 254 us; the launch traced here: 249 us
  local copies, waits for them, and re-layouts  99.1 us (39%)
  between operations  37.3 us (15%)
  starting transfers between devices  37.1 us (15%)
  waiting for transfers between devices  32.5 us (13%)
  matrix products  30.9 us (12%)
  other arithmetic  10.3 us (4%)
    dynamic_update_slice x8, local copies, waits for them, and re-layouts, put(): return lax.dynamic_update_index_in_dim(buffer, block, source, 0)  48.7 us
    ppermute x8, starting transfers between devices, ring_gather(): ahead = lax.ppermute(ahead, axis_name, to_next)  16.7 us
    ppermute x8, waiting for transfers between devices, ring_gather(): ahead = lax.ppermute(ahead, axis_name, to_next)  14.4 us
    all_gather x1, waiting for transfers between devices, shards_body(): attn_all = lax.all_gather(attn, 'seq', axis=0, tiled=True)  14.3 us
    unnamed x54, local copies, waits for them, and re-layouts  11.4 us
    all_to_all x2, starting transfers between devices, scatter_sum(): return jnp.sum(lax.all_to_all(pieces, axis_name, 0, 0, tiled=True), axis=0)  8.1 us
    dynamic_update_slice x8, local copies, waits for them, and re-layouts, put(): lax.dynamic_update_slice_in_dim(buffer, block, source * x.shape[0], 0)  6.41 us
    all_to_all x1, starting transfers between devices, shards_body(): lax.all_to_all(g_cols, 'seq', 0, 0, tiled=True)  6.28 us
  transfers between devices with their start and end apart: 19, of which 6 were waited for; matrix products, arithmetic and copies ran while one was open for 53% of the time, Pallas kernels for 0%

commit v1 on v0

--- a/solution.py
+++ b/solution.py
@@ -26,7 +26,7 @@
     return lax.all_to_all(spread, axis_name, 0, 0, tiled=True)
 
 
-def ring_gather(x, axis_name, flat=False):
+def ring_gather(x, axis_name):
     n = lax.axis_size(axis_name)
     me = lax.axis_index(axis_name)
     if n % 2 == 0:
@@ -40,27 +40,18 @@
     here = jnp.array(place, jnp.int32)[me]
     to_next = [(ring[i], ring[(i + 1) % n]) for i in range(n)]
     to_prev = [(ring[(i + 1) % n], ring[i]) for i in range(n)]
-    if flat:
-        gathered = jnp.zeros((n * x.shape[0],) + x.shape[1:], x.dtype)
-
-        def put(buffer, block, source):
-            return lax.dynamic_update_slice_in_dim(buffer, block, source * x.shape[0], 0)
-    else:
-        gathered = jnp.zeros((n,) + x.shape, x.dtype)
-
-        def put(buffer, block, source):
-            return lax.dynamic_update_index_in_dim(buffer, block, source, 0)
-    gathered = put(gathered, x, me)
+    gathered = jnp.zeros((n,) + x.shape, x.dtype)
+    gathered = lax.dynamic_update_index_in_dim(gathered, x, me, 0)
     ahead = x
     behind = x
     for step in range(1, n // 2 + 1):
         ahead = lax.ppermute(ahead, axis_name, to_next)
         source = ring_ids[(here - step + n) % n]
-        gathered = put(gathered, ahead, source)
+        gathered = lax.dynamic_update_index_in_dim(gathered, ahead, source, 0)
         if step <= (n - 1) // 2:
             behind = lax.ppermute(behind, axis_name, to_prev)
             source = ring_ids[(here + step) % n]
-            gathered = put(gathered, behind, source)
+            gathered = lax.dynamic_update_index_in_dim(gathered, behind, source, 0)
     return gathered
 
 
@@ -134,7 +125,7 @@
     g_cols = g_cols.reshape(n_seq, frames_here, n_dp * col_width)
     g_mine = lax.all_to_all(g_cols, "seq", 0, 0, tiled=True).reshape(-1, n_dp * col_width)
     qg_rows = jnp.concatenate([own_q, grad_attn], axis=1)
-    qg_all = ring_gather(qg_rows, "seq", flat=True)
+    qg_all = lax.all_gather(qg_rows, "seq", axis=0, tiled=True)
     k_all = kv_all[:, :width]
     v_all = kv_all[:, width:]
     run_max, run_sum, total = by_blocks(forward_step, start_state, (k_all, v_all))

time: 254 us -> 255 us (level)
  waiting for transfers between devices: 32.5 us -> 79.8 us
  local copies, waits for them, and re-layouts: 99.1 us -> 79.1 us
  starting transfers between devices: 37.1 us -> 23.9 us
  matrix products: 30.9 us -> 26.2 us
  between operations: 37.3 us -> 32.7 us
  other arithmetic: 10.3 us -> 6.79 us
    all_gather x0 -> x1, waiting for transfers between devices: none -> 45.2 us  [shards_body(): qg_all = lax.all_gather(qg_rows, 'seq', axis=0, tiled=True)]
    all_to_all x1, waiting for transfers between devices: 0.01 us -> 11 us  [shards_body(): lax.all_to_all(g_cols, 'seq', 0, 0, tiled=True)]
    all_gather x1, waiting for transfers between devices: 14.3 us -> 3.51 us  [shards_body(): attn_all = lax.all_gather(attn, 'seq', axis=0, tiled=True)]
    ppermute x7 -> x0, local copies, waits for them, and re-layouts: 10.6 us -> none  [the longest x4 5.58 us: ring_gather(): ahead = lax.ppermute(ahead, axis_name, to_next)]
    dynamic_update_slice x16 -> x8, local copies, waits for them, and re-layouts: 55.1 us -> 45.4 us  [the longest x5 25 us: ring_gather(): gathered = lax.dynamic_update_index_in_dim(gathered, ahead, source, 0)]
    ppermute x8 -> x4, starting transfers between devices: 16.7 us -> 8.33 us  [ring_gather(): ahead = lax.ppermute(ahead, axis_name, to_next)]
    all_to_all x2, waiting for transfers between devices: 3.78 us -> 7.73 us  [scatter_sum(): return jnp.sum(lax.all_to_all(pieces, axis_name, 0, 0, tiled=True), axis=0)]
    slice x1 -> x2, local copies, waits for them, and re-layouts: 1.47 us -> 4.96 us  [shards_body(): qg_all[:, width:]]
  transfers between devices with their start and end apart: 19 -> 13, of which waited for: 6 -> 7; matrix products, arithmetic and copies ran while one was open for 53% -> 25% of each run, Pallas kernels for 0% -> 0%
where the time goes in v1:
time: 255 us; the launch traced here: 251 us
  waiting for transfers between devices  79.8 us (31%)
  local copies, waits for them, and re-layouts  79.1 us (31%)
  between operations  32.7 us (13%)
  matrix products  26.2 us (10%)
  starting transfers between devices  23.9 us (9%)
  other arithmetic  6.79 us (3%)
    all_gather x1, waiting for transfers between devices, shards_body(): qg_all = lax.all_gather(qg_rows, 'seq', axis=0, tiled=True)  45.2 us
    dynamic_update_slice x5, local copies, waits for them, and re-layouts, ring_gather(): gathered = lax.dynamic_update_index_in_dim(gathered, ahead, source, 0)  25 us
    dynamic_update_slice x3, local copies, waits for them, and re-layouts, ring_gather(): gathered = lax.dynamic_update_index_in_dim(gathered, behind, source, 0)  20.4 us
    ppermute x4, waiting for transfers between devices, ring_gather(): ahead = lax.ppermute(ahead, axis_name, to_next)  12.3 us
    all_to_all x1, waiting for transfers between devices, shards_body(): lax.all_to_all(g_cols, 'seq', 0, 0, tiled=True)  11 us
    unnamed x46, local copies, waits for them, and re-layouts  8.97 us
    ppermute x4, starting transfers between devices, ring_gather(): ahead = lax.ppermute(ahead, axis_name, to_next)  8.33 us
    all_to_all x2, waiting for transfers between devices, scatter_sum(): return jnp.sum(lax.all_to_all(pieces, axis_name, 0, 0, tiled=True), axis=0)  7.73 us
  transfers between devices with their start and end apart: 13, of which 7 were waited for; matrix products, arithmetic and copies ran while one was open for 25% of the time, Pallas kernels for 0%

profile of v1, /device:TPU:0, one launch (start us, length us, event | category | flops | bytes accessed | tf_op | source)
XLA Modules:
  0.0 250.6 jit_solution(16650836356404707948)
XLA Ops:
  8.4 3.1 %collective-permute-start = (bf16[128,1536]{1,0:T(8,128)(2,1)S(1)}, bf16[128,1536]{1,0:T(8,128)(2,1)S(1)}, u32[]{:S(2)}, u32[]{:S(2)}) collective-permute-start(bf16[128,1536]{1,0:T(8,128)(2,1)S(1)} %pad_maximum_fusion), channel_id=1, source_target_pairs={{0,4},{4,8},{8,12},{12,14},{14,10},{10,6},{6,2},{2,0},{1,5},{5,9},... | collective-permute-start | bytes 1179656 | tf_op jit(solution)/shard_map/ppermute | solution.py:48
  28.3 1.7 copy.53
  34.3 1.9 broadcast_in_dim.101
  37.0 2.0 collective-permute-start.2
  40.7 7.0 %collective-permute-done.2 = bf16[128,1536]{1,0:T(8,128)(2,1)S(1)} collective-permute-done((bf16[128,1536]{1,0:T(8,128)(2,1)S(1)}, bf16[128,1536]{1,0:T(8,128)(2,1)S(1)}, u32[]{:S(2)}, u32[]{:S(2)}) %collective-permute-start.2) | collective-permute-done | bytes 393248 | tf_op jit(solution)/shard_map/ppermute | solution.py:48
  50.4 1.8 bitcast_dynamic-update-slice_fusion.1
  52.2 5.3 %collective-permute-done.4 = bf16[128,1536]{1,0:T(8,128)(2,1)} collective-permute-done((bf16[128,1536]{1,0:T(8,128)(2,1)S(1)}, bf16[128,1536]{1,0:T(8,128)(2,1)}, u32[]{:S(2)}, u32[]{:S(2)}) %collective-permute-start.4) | collective-permute-done | bytes 393248 | tf_op jit(solution)/shard_map/ppermute | solution.py:48
  59.0 1.8 bitcast_dynamic-update-slice_fusion
  60.8 3.8 %copy.50 = bf16[8,128,1536]{1,0,2:T(8,128)(2,1)S(1)} copy(bf16[8,128,1536]{2,1,0:T(8,128)(2,1)} %bitcast_dynamic-update-slice_fusion) | data formatting | bytes 6291456 | tf_op jit(solution)/shard_map/jit(dynamic_update_index_in_dim)/dynamic_update_slice | solution.py:50
  64.7 3.0 %copy.51 = bf16[1,128,1536]{1,0,2:T(2,128)(2,1)} copy(bf16[1,128,1536]{2,1,0:T(8,128)(2,1)} %bitcast.19) | data formatting | bytes 786432 | tf_op jit(solution)/shard_map/jit(dynamic_update_index_in_dim)/broadcast_in_dim | solution.py:54
  67.6 17.8 %dynamic_update_slice.31 = bf16[8,128,1536]{1,0,2:T(8,128)(2,1)S(1)} dynamic-update-slice(bf16[8,128,1536]{1,0,2:T(8,128)(2,1)S(1)} %copy.50, bf16[1,128,1536]{1,0,2:T(2,128)(2,1)} %copy.51, s32[]{:T(128)S(6)} %select_n.122, s32[]{:T(128)} %constant.129.clone.1, s32[]{:T(128)} %constant.129.clone.1) | dynamic-update-slice | bytes 786436 | tf_op jit(solution)/shard_map/jit(dynamic_update_index_in_dim)/dynamic_update_slice | solution.py:54
  85.5 3.0 %copy.52 = bf16[1,128,1536]{1,0,2:T(2,128)(2,1)} copy(bf16[1,128,1536]{2,1,0:T(8,128)(2,1)} %bitcast.22) | data formatting | bytes 786432 | tf_op jit(solution)/shard_map/jit(dynamic_update_index_in_dim)/broadcast_in_dim | solution.py:50
  88.4 17.8 %dynamic_update_slice.32 = bf16[8,128,1536]{1,0,2:T(8,128)(2,1)S(1)} dynamic-update-slice(bf16[8,128,1536]{1,0,2:T(8,128)(2,1)S(1)} %dynamic_update_slice.31, bf16[1,128,1536]{1,0,2:T(2,128)(2,1)} %copy.52, s32[]{:T(128)S(6)} %select_n.125, s32[]{:T(128)} %constant.129.clone.1, s32[]{:T(128)} %constant.129.clone.1) | dynamic-update-slice | bytes 786436 | tf_op jit(solution)/shard_map/jit(dynamic_update_index_in_dim)/dynamic_update_slice | solution.py:50
  110.3 3.6 %fusion.35 = (bf16[128,8,96]{0,2,1:T(8,128)(2,1)S(1)}, f32[8,128,96]{1,2,0:T(8,128)}) fusion(f32[128,8]{0,1:T(8,128)S(1)} %bitcast_add_fusion.2, f32[128,8]{0,1:T(8,128)S(1)} %get-tuple-element.109, bf16[1024,8,96]{0,2,1:T(8,128)(2,1)S(1)} %bitcast.165, f32[8,1024,128]{2,1,0:T(8,128)S(1)} %get-tuple-element.131, f32[8,128]{1,0:T(8,128)S(1)} %broadcast_maximum_fusion, ...), kind=kOutput, calls=%fused_computation.44 | convolution fusion | flops 1211400192 | bytes 6370304 | tf_op jit(solution)/shard_map/while/body/eval_jaxpr/hij,jhc->hic/dot_general | solution.py:104
  115.0 2.1 all-gather
  120.5 4.8 %all-to-all-start.2 = ((bf16[8,128,192]{1,2,0:T(8,128)(2,1)}), bf16[8,128,192]{1,2,0:T(8,128)(2,1)S(1)}, u32[]{:S(2)}, u32[]{:S(2)}) async-start(bf16[8,128,192]{1,2,0:T(8,128)(2,1)} %bitcast.164), calls=%async_computation.2 | async-start | bytes 786432 | tf_op jit(solution)/shard_map/all_to_all | solution.py:126
  127.8 2.5 %copy.76 = bf16[1536,768]{1,0:T(8,128)(2,1)} copy(bf16[1536,768]{0,1:T(8,128)(2,1)S(1)} %bitcast.151) | data formatting | bytes 4718592 | tf_op jit(solution)/shard_map/dot_general | solution.py:135
  130.9 11.0 %all-to-all-done.2 = bf16[8,128,192]{1,2,0:T(8,128)(2,1)S(1)} async-done(((bf16[8,128,192]{1,2,0:T(8,128)(2,1)}), bf16[8,128,192]{1,2,0:T(8,128)(2,1)S(1)}, u32[]{:S(2)}, u32[]{:S(2)}) %all-to-all-start.2) | async-done | bytes 393248 | tf_op jit(solution)/shard_map/all_to_all | solution.py:126
  142.7 3.6 %convolution_bitcast_fusion = f32[2,128,768]{2,1,0:T(8,128)} fusion(bf16[128,768,1]{0,1,2:T(8,128)(2,1)S(1)} %bitcast.170, bf16[2,768,768]{2,1,0:T(8,128)(2,1)} %bitcast.152), kind=kOutput, calls=%fused_computation.28 | convolution fusion | flops 301989888 | bytes 3342336 | tf_op jit(solution)/shard_map/dot_general | solution.py:135
  146.3 3.5 %all-to-all-start = ((f32[2,128,768]{2,1,0:T(8,128)}), f32[2,128,768]{2,1,0:T(8,128)S(1)}, u32[]{:S(2)}, u32[]{:S(2)}) async-start(f32[2,128,768]{2,1,0:T(8,128)} %convolution_bitcast_fusion), calls=%async_computation | async-start | bytes 1572864 | tf_op jit(solution)/shard_map/all_to_all | solution.py:62
  150.0 1.8 all-to-all-done
  152.4 3.4 %all-to-all-start.1 = ((f32[8,16,128]{2,1,0:T(8,128)}), f32[8,16,128]{2,1,0:T(8,128)S(1)}, u32[]{:S(2)}, u32[]{:S(2)}) async-start(f32[8,16,128]{2,1,0:T(8,128)} %broadcast_in_dim.112), calls=%async_computation.1 | async-start | bytes 131072 | tf_op jit(solution)/shard_map/all_to_all | solution.py:26
  155.9 5.2 %fusion.26 = bf16[8,128,96]{1,2,0:T(8,128)(2,1)S(1)} fusion(bf16[1024,8,96]{0,2,1:T(8,128)(2,1)S(1)} %bitcast.156, f32[8,1024,128]{2,1,0:T(8,128)} %copy-done, bf16[128,8,96]{0,2,1:T(8,128)(2,1)S(1)} %bitcast.173, bf16[1024,8,96]{0,2,1:T(8,128)(2,1)} %bitcast.166, f32[8,128]{1,0:T(8,128)S(1)} %fusion.31, f32[8,128]{1,0:T(8,128)S(1)} %get-tuple-element.107, ...), kind=kOutput, calls=%fused_computation.30 | convolution fusion | flops 410091520 | bytes 7742464 | tf_op jit(solution)/shard_map/while/body/eval_jaxpr/hij,jhc->hic/dot_general | solution.py:155
  161.1 3.5 %all-gather.6.cloned.1.call-done = bf16[1024,768]{1,0:T(8,128)(2,1)} async-done(((bf16[128,768]{1,0:T(8,128)(2,1)}), bf16[1024,768]{1,0:T(8,128)(2,1)}) %all-gather.6.cloned.1.call-update) | async-done | bytes 1572880 | tf_op jit(solution)/shard_map/all_gather | solution.py:138
  164.6 2.7 %fusion.23 = f32[2,768,96]{1,2,0:T(8,128)} fusion(bf16[2,96,1024]{2,1,0:T(8,128)(2,1)S(1)} %bitcast.174, bf16[1024,768]{1,0:T(8,128)(2,1)} %all-gather.6.cloned.1.call-done), kind=kOutput, calls=%fused_computation.29 | convolution fusion | flops 301989888 | bytes 2555904 | tf_op jit(solution)/shard_map/dot_general | solution.py:139
  167.3 3.5 %all-to-all-start.3 = ((f32[2,768,96]{1,2,0:T(8,128)}), f32[2,768,96]{1,2,0:T(8,128)S(1)}, u32[]{:S(2)}, u32[]{:S(2)}) async-start(f32[2,768,96]{1,2,0:T(8,128)} %fusion.23), calls=%async_computation.3 | async-start | bytes 1179648 | tf_op jit(solution)/shard_map/all_to_all | solution.py:62
  173.0 5.9 %all-to-all-done.3 = f32[2,768,96]{1,2,0:T(8,128)S(1)} async-done(((f32[2,768,96]{1,2,0:T(8,128)}), f32[2,768,96]{1,2,0:T(8,128)S(1)}, u32[]{:S(2)}, u32[]{:S(2)}) %all-to-all-start.3) | async-done | bytes 589856 | tf_op jit(solution)/shard_map/all_to_all | solution.py:62
  179.7 45.2 %all-gather.4.cloned.1.call-done = bf16[1024,1536]{1,0:T(8,128)(2,1)} async-done(((bf16[128,1536]{1,0:T(8,128)(2,1)}), bf16[1024,1536]{1,0:T(8,128)(2,1)}) %all-gather.4.cloned.1.call-update) | async-done | bytes 3145744 | tf_op jit(solution)/shard_map/all_gather | solution.py:128
  224.9 3.3 %fusion.46 = (bf16[1024,768]{1,0:T(8,128)(2,1)S(1)}, bf16[1024,768]{1,0:T(8,128)(2,1)}) fusion(bf16[1024,1536]{1,0:T(8,128)(2,1)} %all-gather.4.cloned.1.call-done), kind=kLoop, calls=%fused_computation.70 | loop fusion | bytes 6291456 | tf_op jit(solution)/shard_map/slice | solution.py:186
  228.2 1.7 copy.61
  233.0 2.2 fusion.28
  235.2 5.9 %fusion.27 = bf16[8,128,96]{1,2,0:T(8,128)(2,1)} fusion(bf16[1024,8,96]{0,2,1:T(8,128)(2,1)S(1)} %bitcast.154, f32[8,1024,128]{2,1,0:T(8,128)} %copy-done.4, bf16[1024,8,96]{0,2,1:T(8,128)(2,1)S(1)} %bitcast.163, bf16[128,8,96]{0,2,1:T(8,128)(2,1)S(1)} %bitcast.176, f32[8,1024]{1,0:T(8,128)} %get-tuple-element.106, f32[8,1024]{1,0:T(8,128)} %get-tuple-element.105, ...), kind=kOutput, calls=%fused_computation.31 | convolution fusion | flops 410091520 | bytes 7798912 | tf_op jit(solution)/shard_map/while/body/eval_jaxpr/hij,ihc->hjc/dot_general | solution.py:173
  (90 shorter events, 32.3 us)
Async XLA Ops:
  7.2 29.1 %copy-start.6 = (bf16[1,128,768]{2,1,0:T(8,128)(2,1)S(1)}, bf16[1,128,768]{2,1,0:T(8,128)(2,1)}, u32[]{:S(2)}) copy-start(bf16[1,128,768]{2,1,0:T(8,128)(2,1)} %param.11) | copy-start | bytes 589828
  7.2 29.1 %copy-start.5 = (bf16[1,128,768]{2,1,0:T(8,128)(2,1)S(1)}, bf16[1,128,768]{2,1,0:T(8,128)(2,1)}, u32[]{:S(2)}) copy-start(bf16[1,128,768]{2,1,0:T(8,128)(2,1)} %param.10) | copy-start | bytes 589828
  7.2 157.4 %all-gather.6.cloned.1.call-start = ((), (), s32[]{:S(2)}) async-start(), calls=%async_computation.5 | async-start | bytes 1769472 | tf_op jit(solution)/shard_map/all_gather | solution.py:138
  8.4 28.7 %collective-permute-start = (bf16[128,1536]{1,0:T(8,128)(2,1)S(1)}, bf16[128,1536]{1,0:T(8,128)(2,1)S(1)}, u32[]{:S(2)}, u32[]{:S(2)}) collective-permute-start(bf16[128,1536]{1,0:T(8,128)(2,1)S(1)} %pad_maximum_fusion), channel_id=1, source_target_pairs={{0,4},{4,8},{8,12},{12,14},{14,10},{10,6},{6,2},{2,0},{1,5},{5,9},... | collective-permute-start | bytes 1179656 | tf_op jit(solution)/shard_map/ppermute | solution.py:48
  11.5 27.6 %collective-permute-start.1 = (bf16[128,1536]{1,0:T(8,128)(2,1)S(1)}, bf16[128,1536]{1,0:T(8,128)(2,1)S(1)}, u32[]{:S(2)}, u32[]{:S(2)}) collective-permute-start(bf16[128,1536]{1,0:T(8,128)(2,1)S(1)} %pad_maximum_fusion), channel_id=1, source_target_pairs={{4,0},{8,4},{12,8},{14,12},{10,14},{6,10},{2,6},{0,2},{5,1},{9,5},... | collective-permute-start | bytes 1179656 | tf_op jit(solution)/shard_map/ppermute | solution.py:52
  37.0 10.6 %collective-permute-start.2 = (bf16[128,1536]{1,0:T(8,128)(2,1)S(1)}, bf16[128,1536]{1,0:T(8,128)(2,1)S(1)}, u32[]{:S(2)}, u32[]{:S(2)}) collective-permute-start(bf16[128,1536]{1,0:T(8,128)(2,1)S(1)} %collective-permute-done), channel_id=1, source_target_pairs={{0,4},{4,8},{8,12},{12,14},{14,10},{10,6},{6,2},{2,0},{1,5},{5,9},... | collective-permute-start | bytes 1179656 | tf_op jit(solution)/shard_map/ppermute | solution.py:48
  39.1 10.3 %collective-permute-start.3 = (bf16[128,1536]{1,0:T(8,128)(2,1)S(1)}, bf16[128,1536]{1,0:T(8,128)(2,1)}, u32[]{:S(2)}, u32[]{:S(2)}) collective-permute-start(bf16[128,1536]{1,0:T(8,128)(2,1)S(1)} %collective-permute-done.1), channel_id=1, source_target_pairs={{4,0},{8,4},{12,8},{14,12},{10,14},{6,10},{2,6},{0,2},{5,1},{9,5},... | collective-permute-start | bytes 1179656 | tf_op jit(solution)/shard_map/ppermute | solution.py:52
  47.6 9.9 %collective-permute-start.4 = (bf16[128,1536]{1,0:T(8,128)(2,1)S(1)}, bf16[128,1536]{1,0:T(8,128)(2,1)}, u32[]{:S(2)}, u32[]{:S(2)}) collective-permute-start(bf16[128,1536]{1,0:T(8,128)(2,1)S(1)} %collective-permute-done.2), channel_id=1, source_target_pairs={{0,4},{4,8},{8,12},{12,14},{14,10},{10,6},{6,2},{2,0},{1,5},{5,9},... | collective-permute-start | bytes 1179656 | tf_op jit(solution)/shard_map/ppermute | solution.py:48
  49.4 15.3 %collective-permute-start.5 = (bf16[128,1536]{1,0:T(8,128)(2,1)}, bf16[128,1536]{1,0:T(8,128)(2,1)}, u32[]{:S(2)}, u32[]{:S(2)}) collective-permute-start(bf16[128,1536]{1,0:T(8,128)(2,1)} %collective-permute-done.3), channel_id=1, source_target_pairs={{4,0},{8,4},{12,8},{14,12},{10,14},{6,10},{2,6},{0,2},{5,1},{9,5},... | collective-permute-start | bytes 1179656 | tf_op jit(solution)/shard_map/ppermute | solution.py:52
  57.5 27.9 %collective-permute-start.6 = (bf16[128,1536]{1,0:T(8,128)(2,1)}, bf16[128,1536]{1,0:T(8,128)(2,1)}, u32[]{:S(2)}, u32[]{:S(2)}) collective-permute-start(bf16[128,1536]{1,0:T(8,128)(2,1)} %collective-permute-done.4), channel_id=1, source_target_pairs={{0,4},{4,8},{8,12},{12,14},{14,10},{10,6},{6,2},{2,0},{1,5},{5,9},... | collective-permute-start | bytes 1179656 | tf_op jit(solution)/shard_map/ppermute | solution.py:48
  107.1 0.9 copy-start.9
  107.4 2.8 %copy-start.2 = (bf16[1024,768]{0,1:T(8,128)(2,1)}, bf16[1024,768]{0,1:T(8,128)(2,1)S(1)}, u32[]{:S(2)}) copy-start(bf16[1024,768]{0,1:T(8,128)(2,1)S(1)} %get-tuple-element.103) | copy-start | bytes 4718596
  107.4 2.9 %copy-start.8 = (bf16[1024,768]{0,1:T(8,128)(2,1)}, bf16[1024,768]{0,1:T(8,128)(2,1)S(1)}, u32[]{:S(2)}) copy-start(bf16[1024,768]{0,1:T(8,128)(2,1)S(1)} %get-tuple-element.104) | copy-start | bytes 4718596
  109.3 4.6 %copy-start = (f32[8,1024,128]{2,1,0:T(8,128)}, f32[8,1024,128]{2,1,0:T(8,128)S(1)}, u32[]{:S(2)}) copy-start(f32[8,1024,128]{2,1,0:T(8,128)S(1)} %get-tuple-element.131) | copy-start | bytes 12582916
  110.3 4.5 %copy-start.14 = (bf16[1,128,768]{2,1,0:T(8,128)(2,1)S(1)}, bf16[1,128,768]{2,1,0:T(8,128)(2,1)}, u32[]{:S(2)}) copy-start(bf16[1,128,768]{2,1,0:T(8,128)(2,1)} %param.15) | copy-start | bytes 589828
  110.3 6.8 %copy-start.1 = (bf16[768,1536]{1,0:T(8,128)(2,1)S(1)}, bf16[768,1536]{1,0:T(8,128)(2,1)}, u32[]{:S(2)}) copy-start(bf16[768,1536]{1,0:T(8,128)(2,1)} %param.12) | copy-start | bytes 7077892
  114.8 110.1 %all-gather.4.cloned.1.call-start = ((), (), s32[]{:S(2)}) async-start(), calls=%async_computation.4 | async-start | bytes 3538944 | tf_op jit(solution)/shard_map/all_gather | solution.py:128
  120.5 21.4 %all-to-all-start.2 = ((bf16[8,128,192]{1,2,0:T(8,128)(2,1)}), bf16[8,128,192]{1,2,0:T(8,128)(2,1)S(1)}, u32[]{:S(2)}, u32[]{:S(2)}) async-start(bf16[8,128,192]{1,2,0:T(8,128)(2,1)} %bitcast.164), calls=%async_computation.2 | async-start | bytes 786432 | tf_op jit(solution)/shard_map/all_to_all | solution.py:126
  130.3 19.6 %copy-start.11 = (bf16[128,768]{0,1:T(8,128)(2,1)S(1)}, bf16[128,768]{0,1:T(8,128)(2,1)}, u32[]{:S(2)}) copy-start(bf16[128,768]{0,1:T(8,128)(2,1)} %copy.58) | copy-start | bytes 589828
  130.3 19.6 %copy-start.12 = (f32[8,128,96]{1,2,0:T(8,128)S(1)}, f32[8,128,96]{1,2,0:T(8,128)}, u32[]{:S(2)}) copy-start(f32[8,128,96]{1,2,0:T(8,128)} %get-tuple-element.133) | copy-start | bytes 1179652
  142.7 13.1 %copy-start.3 = (bf16[1024,768]{0,1:T(8,128)(2,1)S(1)}, bf16[1024,768]{0,1:T(8,128)(2,1)}, u32[]{:S(2)}) copy-start(bf16[1024,768]{0,1:T(8,128)(2,1)} %copy-done.2) | copy-start | bytes 4718596
  146.3 5.5 %all-to-all-start = ((f32[2,128,768]{2,1,0:T(8,128)}), f32[2,128,768]{2,1,0:T(8,128)S(1)}, u32[]{:S(2)}, u32[]{:S(2)}) async-start(f32[2,128,768]{2,1,0:T(8,128)} %convolution_bitcast_fusion), calls=%async_computation | async-start | bytes 1572864 | tf_op jit(solution)/shard_map/all_to_all | solution.py:62
  152.4 14.9 %all-to-all-start.1 = ((f32[8,16,128]{2,1,0:T(8,128)}), f32[8,16,128]{2,1,0:T(8,128)S(1)}, u32[]{:S(2)}, u32[]{:S(2)}) async-start(f32[8,16,128]{2,1,0:T(8,128)} %broadcast_in_dim.112), calls=%async_computation.1 | async-start | bytes 131072 | tf_op jit(solution)/shard_map/all_to_all | solution.py:26
  155.9 8.7 %copy-start.13 = (bf16[1024,192]{0,1:T(8,128)(2,1)S(1)}, bf16[1024,192]{0,1:T(8,128)(2,1)}, u32[]{:S(2)}) copy-start(bf16[1024,192]{0,1:T(8,128)(2,1)} %copy_bitcast_fusion.1) | copy-start | bytes 1179652
  161.1 9.8 %copy-start.16 = (bf16[1,128,768]{2,1,0:T(8,128)(2,1)S(1)}, bf16[1,128,768]{2,1,0:T(8,128)(2,1)}, u32[]{:S(2)}) copy-start(bf16[1,128,768]{2,1,0:T(8,128)(2,1)} %param.13) | copy-start | bytes 589828
  167.3 11.6 %all-to-all-start.3 = ((f32[2,768,96]{1,2,0:T(8,128)}), f32[2,768,96]{1,2,0:T(8,128)S(1)}, u32[]{:S(2)}, u32[]{:S(2)}) async-start(f32[2,768,96]{1,2,0:T(8,128)} %fusion.23), calls=%async_computation.3 | async-start | bytes 1179648 | tf_op jit(solution)/shard_map/all_to_all | solution.py:62
  228.2 3.5 %copy-start.10 = (bf16[1,128,768]{1,2,0:T(8,128)(2,1)S(1)}, bf16[1,128,768]{1,2,0:T(8,128)(2,1)}, u32[]{:S(2)}) copy-start(bf16[1,128,768]{1,2,0:T(8,128)(2,1)} %copy.62) | copy-start | bytes 589828
  231.6 1.4 copy-start.7
  231.6 1.4 copy-start.17
  231.6 1.4 copy-start.18
  232.4 2.8 %copy-start.4 = (f32[8,1024,128]{2,1,0:T(8,128)}, f32[8,1024,128]{2,1,0:T(8,128)S(1)}, u32[]{:S(2)}) copy-start(f32[8,1024,128]{2,1,0:T(8,128)S(1)} %fusion.49) | copy-start | bytes 12582916
  233.0 2.2 copy-start.15
Sparse Core Ops, SparseCore 0:
  114.9 49.6 all-gather.5
  166.8 58.0 all-gather.3

commit v2 on v1

--- a/solution.py
+++ b/solution.py
@@ -124,8 +124,7 @@
     g_cols = jnp.transpose(grad_full.reshape(frames_here, n_dp, n_seq, col_width), (2, 0, 1, 3))
     g_cols = g_cols.reshape(n_seq, frames_here, n_dp * col_width)
     g_mine = lax.all_to_all(g_cols, "seq", 0, 0, tiled=True).reshape(-1, n_dp * col_width)
-    qg_rows = jnp.concatenate([own_q, grad_attn], axis=1)
-    qg_all = lax.all_gather(qg_rows, "seq", axis=0, tiled=True)
+    qg_all = ring_gather(jnp.concatenate([own_q, grad_attn], axis=1), "seq").reshape(-1, 2 * width)
     k_all = kv_all[:, :width]
     v_all = kv_all[:, width:]
     run_max, run_sum, total = by_blocks(forward_step, start_state, (k_all, v_all))
@@ -133,9 +132,9 @@
     attn_full = total / run_sum[:, :, None]
     attn = join_heads(attn_full).astype(jnp.bfloat16)
     partial_out = jnp.dot(attn, out_weight, preferred_element_type=jnp.float32)
-    mixed = scatter_sum(partial_out, "tensor", 1)
+    mixed = lax.psum_scatter(partial_out, "tensor", scatter_dimension=1, tiled=True)
     block_out = (residual[0].astype(jnp.float32) + mixed).astype(jnp.bfloat16)
-    attn_all = lax.all_gather(attn, "seq", axis=0, tiled=True)
+    attn_all = ring_gather(attn, "seq").reshape(-1, attn.shape[1])
     weight_term = lax.dot_general(
         attn_all, g_mine, (((0,), (0,)), ((), ())), preferred_element_type=jnp.float32
     )

time: 255 us -> 215 us (0.84); the launches traced: 251 us -> 213 us
  waiting for transfers between devices: 79.8 us -> 35 us
  starting transfers between devices: 23.9 us -> 40.4 us
  local copies, waits for them, and re-layouts: 79.1 us -> 63 us
  matrix products: 26.2 us -> 32.9 us
    all_gather x2 -> x0, waiting for transfers between devices: 48.7 us -> none  [the longest x1 45.2 us: shards_body(): qg_all = lax.all_gather(qg_rows, 'seq', axis=0, tiled=True)]
    ppermute x4 -> x12, waiting for transfers between devices: 12.3 us -> 32 us  [ring_gather(): ahead = lax.ppermute(ahead, axis_name, to_next)]
    ppermute x4 -> x12, starting transfers between devices: 8.33 us -> 23.5 us  [ring_gather(): ahead = lax.ppermute(ahead, axis_name, to_next)]
    dynamic_update_slice x5 -> x11, local copies, waits for them, and re-layouts: 25 us -> 12.4 us  [ring_gather(): gathered = lax.dynamic_update_index_in_dim(gathered, ahead, source, 0)]
    all_to_all x1, waiting for transfers between devices: 11 us -> 0.01 us  [shards_body(): lax.all_to_all(g_cols, 'seq', 0, 0, tiled=True)]
    dynamic_update_slice x3 -> x9, local copies, waits for them, and re-layouts: 20.4 us -> 9.79 us  [ring_gather(): gathered = lax.dynamic_update_index_in_dim(gathered, behind, source, 0)]
    all_to_all x2 -> x1, waiting for transfers between devices: 7.73 us -> 2.46 us  [scatter_sum(): return jnp.sum(lax.all_to_all(pieces, axis_name, 0, 0, tiled=True), axis=0)]
    unnamed x46 -> x39, local copies, waits for them, and re-layouts: 8.97 us -> 14.1 us
  transfers between devices with their start and end apart: 13 -> 25, of which waited for: 7 -> 11; matrix products, arithmetic and copies ran while one was open for 25% -> 32% of each run, Pallas kernels for 0% -> 0%
where the time goes in v2:
time: 215 us; the launch traced here: 213 us
  local copies, waits for them, and re-layouts  63 us (29%)
  starting transfers between devices  40.4 us (19%)
  waiting for transfers between devices  35 us (16%)
  between operations  33.1 us (15%)
  matrix products  32.9 us (15%)
  other arithmetic  6.7 us (3%)
  blocking collectives  2.21 us (1%)
    ppermute x12, waiting for transfers between devices, ring_gather(): ahead = lax.ppermute(ahead, axis_name, to_next)  32 us
    ppermute x12, starting transfers between devices, ring_gather(): ahead = lax.ppermute(ahead, axis_name, to_next)  23.5 us
    unnamed x39, local copies, waits for them, and re-layouts  14.1 us
    dynamic_update_slice x11, local copies, waits for them, and re-layouts, ring_gather(): gathered = lax.dynamic_update_index_in_dim(gathered, ahead, source, 0)  12.4 us
    dynamic_update_slice x9, local copies, waits for them, and re-layouts, ring_gather(): gathered = lax.dynamic_update_index_in_dim(gathered, behind, source, 0)  9.79 us
    dot_general x2, matrix products, masked_scores(): jnp.einsum('ihc,jhc->hij', left, right, preferred_element_type=jnp.float32)  6.92 us
    slice x2, local copies, waits for them, and re-layouts, shards_body(): qg_all[:, width:]  6.3 us
    all_to_all x1, starting transfers between devices, shards_body(): lax.all_to_all(g_cols, 'seq', 0, 0, tiled=True)  6.26 us
  transfers between devices with their start and end apart: 25, of which 11 were waited for; matrix products, arithmetic and copies ran while one was open for 32% of the time, Pallas kernels for 0%

profile of v2, /device:TPU:0, one launch (start us, length us, event | category | flops | bytes accessed | tf_op | source)
XLA Modules:
  0.0 213.3 jit_solution(3108670885306677818)
XLA Ops:
  8.5 2.2 %all-gather = bf16[1,128,1536]{1,2,0:T(8,128)(2,1)S(1)} all-gather(bf16[1,128,768]{1,2,0:T(8,128)(2,1)S(1)} %copy.62), channel_id=2, replica_groups=mesh['dp'=2,'seq'=8,'tensor'=2] {'tensor'}, dimensions={2}, use_global_device_ids=true | all-gather | bytes 589824 | tf_op jit(solution)/shard_map/all_gather | solution.py:114
  12.4 2.9 %collective-permute-start.7 = (bf16[128,1536]{1,0:T(8,128)(2,1)}, bf16[128,1536]{1,0:T(8,128)(2,1)}, u32[]{:S(2)}, u32[]{:S(2)}) collective-permute-start(bf16[128,1536]{1,0:T(8,128)(2,1)} %pad_maximum_fusion.1), channel_id=1, source_target_pairs={{0,4},{4,8},{8,12},{12,14},{14,10},{10,6},{6,2},{2,0},{1,5},{5,9},... | collective-permute-start | bytes 1179656 | tf_op jit(solution)/shard_map/ppermute | solution.py:48
  16.2 2.0 collective-permute-start
  19.0 6.3 %all-to-all-start.1 = ((bf16[8,128,192]{1,2,0:T(8,128)(2,1)}), bf16[8,128,192]{1,2,0:T(8,128)(2,1)S(1)}, u32[]{:S(2)}, u32[]{:S(2)}) async-start(bf16[8,128,192]{1,2,0:T(8,128)(2,1)} %bitcast.180), calls=%async_computation.2 | async-start | bytes 786432 | tf_op jit(solution)/shard_map/all_to_all | solution.py:126
  53.3 2.0 collective-permute-start.9
  55.4 2.0 collective-permute-start.2
  65.6 2.0 collective-permute-start.11
  67.7 6.4 %collective-permute-done.2 = bf16[128,1536]{1,0:T(8,128)(2,1)} collective-permute-done((bf16[128,1536]{1,0:T(8,128)(2,1)}, bf16[128,1536]{1,0:T(8,128)(2,1)}, u32[]{:S(2)}, u32[]{:S(2)}) %collective-permute-start.2) | collective-permute-done | bytes 393248 | tf_op jit(solution)/shard_map/ppermute | solution.py:48
  74.1 2.0 collective-permute-start.4
  84.4 6.5 %collective-permute-done.4 = bf16[128,1536]{1,0:T(8,128)(2,1)S(1)} collective-permute-done((bf16[128,1536]{1,0:T(8,128)(2,1)}, bf16[128,1536]{1,0:T(8,128)(2,1)S(1)}, u32[]{:S(2)}, u32[]{:S(2)}) %collective-permute-start.4) | collective-permute-done | bytes 393248 | tf_op jit(solution)/shard_map/ppermute | solution.py:48
  90.8 2.0 collective-permute-start.6
  95.9 3.3 %collective-permute-done.13 = bf16[128,1536]{1,0:T(8,128)(2,1)S(1)} collective-permute-done((bf16[128,1536]{1,0:T(8,128)(2,1)S(1)}, bf16[128,1536]{1,0:T(8,128)(2,1)S(1)}, u32[]{:S(2)}, u32[]{:S(2)}) %collective-permute-start.13) | collective-permute-done | bytes 393248 | tf_op jit(solution)/shard_map/ppermute | solution.py:48
  99.2 6.2 %collective-permute-done.6 = bf16[128,1536]{1,0:T(8,128)(2,1)S(1)} collective-permute-done((bf16[128,1536]{1,0:T(8,128)(2,1)S(1)}, bf16[128,1536]{1,0:T(8,128)(2,1)S(1)}, u32[]{:S(2)}, u32[]{:S(2)}) %collective-permute-start.6) | collective-permute-done | bytes 393248 | tf_op jit(solution)/shard_map/ppermute | solution.py:48
  106.4 3.8 %fusion.43 = (bf16[1024,768]{1,0:T(8,128)(2,1)}, bf16[1024,768]{1,0:T(8,128)(2,1)}) fusion(bf16[1024,1536]{1,0:T(8,128)(2,1)} %bitcast.26), kind=kLoop, calls=%fused_computation.86 | loop fusion | bytes 6291456 | tf_op jit(solution)/shard_map/slice | solution.py:128
  110.1 2.6 %copy.86 = bf16[1024,768]{0,1:T(8,128)(2,1)} copy(bf16[1024,768]{1,0:T(8,128)(2,1)} %get-tuple-element.103) | data formatting | bytes 3145728
  112.8 2.7 %bitcast_reduce_fusion = (f32[8,128]{1,0:T(8,128)S(1)}, f32[8,1024,128]{2,1,0:T(8,128)S(1)}) fusion(pred[1024]{0:T(1024)(128)(4,1)S(1)} %iota_compare_fusion, bf16[1024,8,96]{0,2,1:T(8,128)(2,1)} %bitcast.165, bf16[128,8,96]{0,2,1:T(8,128)(2,1)S(1)} %bitcast.182), kind=kOutput, calls=%fused_computation.2 | convolution fusion | flops 204471296 | bytes 5968896 | tf_op jit(solution)/shard_map/while/body/eval_jaxpr/ihc,jhc->hij/dot_general | solution.py:92
  118.4 2.6 %copy.87 = bf16[1024,768]{0,1:T(8,128)(2,1)} copy(bf16[1024,768]{1,0:T(8,128)(2,1)} %get-tuple-element.104) | data formatting | bytes 3145728
  121.1 5.5 %fusion.30 = (bf16[128,8,96]{0,2,1:T(8,128)(2,1)S(1)}, f32[8,128,96]{1,2,0:T(8,128)S(1)}) fusion(f32[128,8]{0,1:T(8,128)S(1)} %bitcast_add_fusion.1, f32[128,8]{0,1:T(8,128)S(1)} %get-tuple-element.109, bf16[1024,8,96]{0,2,1:T(8,128)(2,1)} %bitcast.178, f32[8,1024,128]{2,1,0:T(8,128)} %copy-done.1, f32[8,128]{1,0:T(8,128)S(1)} %broadcast_maximum_fusion, ...), kind=kOutput, calls=%fused_computation.48 | convolution fusion | flops 1211400192 | bytes 6370304 | tf_op jit(solution)/shard_map/while/body/eval_jaxpr/hij,jhc->hic/dot_general | solution.py:104
  126.7 5.6 %fusion.21 = bf16[8,128,96]{1,2,0:T(8,128)(2,1)S(1)} fusion(bf16[1024,8,96]{0,2,1:T(8,128)(2,1)} %bitcast.166, f32[8,1024,128]{2,1,0:T(8,128)} %copy-done.1, bf16[128,8,96]{0,2,1:T(8,128)(2,1)S(1)} %bitcast.188, bf16[1024,8,96]{0,2,1:T(8,128)(2,1)} %bitcast.179, f32[8,128]{1,0:T(8,128)S(1)} %fusion.27, f32[8,128]{1,0:T(8,128)S(1)} %get-tuple-element.107, ...), kind=kOutput, calls=%fused_computation.26 | convolution fusion | flops 410091520 | bytes 7742464 | tf_op jit(solution)/shard_map/while/body/eval_jaxpr/hij,jhc->hic/dot_general | solution.py:154
  136.6 3.7 %fusion.42 = (bf16[1024,768]{1,0:T(8,128)(2,1)}, bf16[1024,768]{1,0:T(8,128)(2,1)}) fusion(bf16[1024,1536]{1,0:T(8,128)(2,1)} %bitcast.50), kind=kLoop, calls=%fused_computation.85 | loop fusion | bytes 6291456 | tf_op jit(solution)/shard_map/slice | solution.py:185
  140.3 2.6 %copy.66 = bf16[1024,768]{0,1:T(8,128)(2,1)} copy(bf16[1024,768]{1,0:T(8,128)(2,1)} %get-tuple-element.102) | data formatting | bytes 3145728 | tf_op jit(solution)/shard_map/slice | solution.py:184
  142.9 2.6 %copy.68 = bf16[1024,768]{0,1:T(8,128)(2,1)} copy(bf16[1024,768]{1,0:T(8,128)(2,1)} %get-tuple-element.101) | data formatting | bytes 3145728 | tf_op jit(solution)/shard_map/slice | solution.py:185
  146.1 5.7 %all-to-all-start = ((f32[8,16,128]{2,1,0:T(8,128)}), f32[8,16,128]{2,1,0:T(8,128)S(1)}, u32[]{:S(2)}, u32[]{:S(2)}) async-start(f32[8,16,128]{2,1,0:T(8,128)} %broadcast_in_dim.169), calls=%async_computation.1 | async-start | bytes 131072 | tf_op jit(solution)/shard_map/all_to_all | solution.py:26
  151.9 4.2 %fusion.46 = f32[8,1024,128]{2,1,0:T(8,128)} fusion(bf16[1024,8,96]{0,2,1:T(8,128)(2,1)} %bitcast.167, bf16[128,8,96]{0,2,1:T(8,128)(2,1)S(1)} %bitcast.181), kind=kOutput, calls=%fused_computation.89 | convolution fusion | flops 201326592 | bytes 5963776 | tf_op jit(solution)/shard_map/while/body/eval_jaxpr/ihc,jhc->hij/dot_general | solution.py:92
  159.3 6.2 %fusion.22 = bf16[8,128,96]{1,2,0:T(8,128)(2,1)S(1)} fusion(bf16[1024,8,96]{0,2,1:T(8,128)(2,1)} %bitcast.168, f32[8,1024,128]{2,1,0:T(8,128)} %fusion.46, bf16[1024,8,96]{0,2,1:T(8,128)(2,1)} %bitcast.176, bf16[128,8,96]{0,2,1:T(8,128)(2,1)S(1)} %bitcast.191, f32[8,1024]{1,0:T(8,128)S(1)} %get-tuple-element.106, f32[8,1024]{1,0:T(8,128)S(1)} %get-tuple-element.105, ...), kind=kOutput, calls=%fused_computation.27 | convolution fusion | flops 410091520 | bytes 7798912 | tf_op jit(solution)/shard_map/while/body/eval_jaxpr/hij,ihc->hjc/dot_general | solution.py:172
  171.1 2.4 %collective-permute-done.16 = bf16[128,768]{0,1:T(8,128)(2,1)S(1)} collective-permute-done((bf16[128,768]{0,1:T(8,128)(2,1)}, bf16[128,768]{0,1:T(8,128)(2,1)S(1)}, u32[]{:S(2)}, u32[]{:S(2)}) %collective-permute-start.16) | collective-permute-done | bytes 196640 | tf_op jit(solution)/shard_map/ppermute | solution.py:48
  179.8 4.2 %collective-permute-done.18 = bf16[128,768]{0,1:T(8,128)(2,1)S(1)} collective-permute-done((bf16[128,768]{0,1:T(8,128)(2,1)}, bf16[128,768]{0,1:T(8,128)(2,1)S(1)}, u32[]{:S(2)}, u32[]{:S(2)}) %collective-permute-start.18) | collective-permute-done | bytes 196640 | tf_op jit(solution)/shard_map/ppermute | solution.py:48
  187.4 2.5 %collective-permute-done.20 = bf16[128,768]{0,1:T(8,128)(2,1)S(1)} collective-permute-done((bf16[128,768]{0,1:T(8,128)(2,1)S(1)}, bf16[128,768]{0,1:T(8,128)(2,1)S(1)}, u32[]{:S(2)}, u32[]{:S(2)}) %collective-permute-start.20) | collective-permute-done | bytes 196640 | tf_op jit(solution)/shard_map/ppermute | solution.py:48
  190.9 2.7 %convolution_bitcast_fusion = f32[2,768,96]{1,2,0:T(8,128)} fusion(bf16[1024,768,1]{1,0,2:T(8,128)(2,1)} %bitcast.71, bf16[2,96,1024]{2,1,0:T(8,128)(2,1)S(1)} %bitcast.189), kind=kOutput, calls=%fused_computation.25 | convolution fusion | flops 301989888 | bytes 2555904 | tf_op jit(solution)/shard_map/dot_general | solution.py:138
  193.6 3.5 %all-to-all-start.2 = ((f32[2,768,96]{1,2,0:T(8,128)}), f32[2,768,96]{1,2,0:T(8,128)S(1)}, u32[]{:S(2)}, u32[]{:S(2)}) async-start(f32[2,768,96]{1,2,0:T(8,128)} %convolution_bitcast_fusion), calls=%async_computation.3 | async-start | bytes 1179648 | tf_op jit(solution)/shard_map/all_to_all | solution.py:62
  197.1 3.6 %fusion.23 = bf16[8,128,96]{1,2,0:T(8,128)(2,1)S(1)} fusion(bf16[1024,8,96]{0,2,1:T(8,128)(2,1)} %bitcast.177, f32[8,1024,128]{2,1,0:T(8,128)} %fusion.46, f32[8,1024]{1,0:T(8,128)S(1)} %copy-done.12, pred[128]{0:T(512)(128)(4,1)S(1)} %add_compare_fusion), kind=kOutput, calls=%fused_computation.28 | convolution fusion | flops 205619200 | bytes 5996672 | tf_op jit(solution)/shard_map/while/body/eval_jaxpr/hij,ihc->hjc/dot_general | solution.py:175
  201.5 2.5 %all-to-all-done.2 = f32[2,768,96]{1,2,0:T(8,128)S(1)} async-done(((f32[2,768,96]{1,2,0:T(8,128)}), f32[2,768,96]{1,2,0:T(8,128)S(1)}, u32[]{:S(2)}, u32[]{:S(2)}) %all-to-all-start.2) | async-done | bytes 589856 | tf_op jit(solution)/shard_map/all_to_all | solution.py:62
  (125 shorter events, 65.3 us)
Async XLA Ops:
  7.2 8.1 %copy-start.3 = (bf16[1,128,768]{2,1,0:T(8,128)(2,1)S(1)}, bf16[1,128,768]{2,1,0:T(8,128)(2,1)}, u32[]{:S(2)}) copy-start(bf16[1,128,768]{2,1,0:T(8,128)(2,1)} %param.15) | copy-start | bytes 589828
  7.2 8.1 %copy-start.4 = (bf16[1,128,768]{2,1,0:T(8,128)(2,1)S(1)}, bf16[1,128,768]{2,1,0:T(8,128)(2,1)}, u32[]{:S(2)}) copy-start(bf16[1,128,768]{2,1,0:T(8,128)(2,1)} %param.14) | copy-start | bytes 589828
  12.4 40.9 %collective-permute-start.7 = (bf16[128,1536]{1,0:T(8,128)(2,1)}, bf16[128,1536]{1,0:T(8,128)(2,1)}, u32[]{:S(2)}, u32[]{:S(2)}) collective-permute-start(bf16[128,1536]{1,0:T(8,128)(2,1)} %pad_maximum_fusion.1), channel_id=1, source_target_pairs={{0,4},{4,8},{8,12},{12,14},{14,10},{10,6},{6,2},{2,0},{1,5},{5,9},... | collective-permute-start | bytes 1179656 | tf_op jit(solution)/shard_map/ppermute | solution.py:48
  15.3 40.0 %collective-permute-start.8 = (bf16[128,1536]{1,0:T(8,128)(2,1)}, bf16[128,1536]{1,0:T(8,128)(2,1)}, u32[]{:S(2)}, u32[]{:S(2)}) collective-permute-start(bf16[128,1536]{1,0:T(8,128)(2,1)} %pad_maximum_fusion.1), channel_id=1, source_target_pairs={{4,0},{8,4},{12,8},{14,12},{10,14},{6,10},{2,6},{0,2},{5,1},{9,5},... | collective-permute-start | bytes 1179656 | tf_op jit(solution)/shard_map/ppermute | solution.py:52
  15.3 13.4 %copy-start.14 = (s32[8]{0:T(128)S(1)}, s32[8]{0:T(128)}, u32[]{:S(2)}) copy-start(s32[8]{0:T(128)} %constant.264.clone) | copy-start | bytes 100
  15.3 18.6 %copy-start.13 = (s32[8]{0:T(128)S(1)}, s32[8]{0:T(128)}, u32[]{:S(2)}) copy-start(s32[8]{0:T(128)} %constant.263.clone) | copy-start | bytes 100
  16.2 39.2 %collective-permute-start = (bf16[128,1536]{1,0:T(8,128)(2,1)}, bf16[128,1536]{1,0:T(8,128)(2,1)}, u32[]{:S(2)}, u32[]{:S(2)}) collective-permute-start(bf16[128,1536]{1,0:T(8,128)(2,1)} %pad_maximum_fusion), channel_id=1, source_target_pairs={{0,4},{4,8},{8,12},{12,14},{14,10},{10,6},{6,2},{2,0},{1,5},{5,9},... | collective-permute-start | bytes 1179656 | tf_op jit(solution)/shard_map/ppermute | solution.py:48
  18.2 42.7 %collective-permute-start.1 = (bf16[128,1536]{1,0:T(8,128)(2,1)}, bf16[128,1536]{1,0:T(8,128)(2,1)}, u32[]{:S(2)}, u32[]{:S(2)}) collective-permute-start(bf16[128,1536]{1,0:T(8,128)(2,1)} %pad_maximum_fusion), channel_id=1, source_target_pairs={{4,0},{8,4},{12,8},{14,12},{10,14},{6,10},{2,6},{0,2},{5,1},{9,5},... | collective-permute-start | bytes 1179656 | tf_op jit(solution)/shard_map/ppermute | solution.py:52
  19.0 45.5 %all-to-all-start.1 = ((bf16[8,128,192]{1,2,0:T(8,128)(2,1)}), bf16[8,128,192]{1,2,0:T(8,128)(2,1)S(1)}, u32[]{:S(2)}, u32[]{:S(2)}) async-start(bf16[8,128,192]{1,2,0:T(8,128)(2,1)} %bitcast.180), calls=%async_computation.2 | async-start | bytes 786432 | tf_op jit(solution)/shard_map/all_to_all | solution.py:126
  25.3 179.5 %reduce-scatter.2.cloned.1.call-start = ((), (), s32[]{:S(2)}) async-start(), calls=%async_computation.4 | async-start | bytes 1179648 | tf_op jit(solution)/shard_map/reduce_scatter | solution.py:135
  53.3 12.3 %collective-permute-start.9 = (bf16[128,1536]{1,0:T(8,128)(2,1)}, bf16[128,1536]{1,0:T(8,128)(2,1)}, u32[]{:S(2)}, u32[]{:S(2)}) collective-permute-start(bf16[128,1536]{1,0:T(8,128)(2,1)} %collective-permute-done.7), channel_id=1, source_target_pairs={{0,4},{4,8},{8,12},{12,14},{14,10},{10,6},{6,2},{2,0},{1,5},{5,9},... | collective-permute-start | bytes 1179656 | tf_op jit(solution)/shard_map/ppermute | solution.py:48
  55.3 12.3 %collective-permute-start.10 = (bf16[128,1536]{1,0:T(8,128)(2,1)}, bf16[128,1536]{1,0:T(8,128)(2,1)S(1)}, u32[]{:S(2)}, u32[]{:S(2)}) collective-permute-start(bf16[128,1536]{1,0:T(8,128)(2,1)} %collective-permute-done.8), channel_id=1, source_target_pairs={{4,0},{8,4},{12,8},{14,12},{10,14},{6,10},{2,6},{0,2},{5,1},{9,5},... | collective-permute-start | bytes 1179656 | tf_op jit(solution)/shard_map/ppermute | solution.py:52
  55.4 18.7 %collective-permute-start.2 = (bf16[128,1536]{1,0:T(8,128)(2,1)}, bf16[128,1536]{1,0:T(8,128)(2,1)}, u32[]{:S(2)}, u32[]{:S(2)}) collective-permute-start(bf16[128,1536]{1,0:T(8,128)(2,1)} %collective-permute-done), channel_id=1, source_target_pairs={{0,4},{4,8},{8,12},{12,14},{14,10},{10,6},{6,2},{2,0},{1,5},{5,9},... | collective-permute-start | bytes 1179656 | tf_op jit(solution)/shard_map/ppermute | solution.py:48
  60.9 18.7 %collective-permute-start.3 = (bf16[128,1536]{1,0:T(8,128)(2,1)}, bf16[128,1536]{1,0:T(8,128)(2,1)}, u32[]{:S(2)}, u32[]{:S(2)}) collective-permute-start(bf16[128,1536]{1,0:T(8,128)(2,1)} %collective-permute-done.1), channel_id=1, source_target_pairs={{4,0},{8,4},{12,8},{14,12},{10,14},{6,10},{2,6},{0,2},{5,1},{9,5},... | collective-permute-start | bytes 1179656 | tf_op jit(solution)/shard_map/ppermute | solution.py:52
  65.6 16.7 %collective-permute-start.11 = (bf16[128,1536]{1,0:T(8,128)(2,1)}, bf16[128,1536]{1,0:T(8,128)(2,1)S(1)}, u32[]{:S(2)}, u32[]{:S(2)}) collective-permute-start(bf16[128,1536]{1,0:T(8,128)(2,1)} %collective-permute-done.9), channel_id=1, source_target_pairs={{0,4},{4,8},{8,12},{12,14},{14,10},{10,6},{6,2},{2,0},{1,5},{5,9},... | collective-permute-start | bytes 1179656 | tf_op jit(solution)/shard_map/ppermute | solution.py:48
  67.6 26.7 %collective-permute-start.12 = (bf16[128,1536]{1,0:T(8,128)(2,1)S(1)}, bf16[128,1536]{1,0:T(8,128)(2,1)S(1)}, u32[]{:S(2)}, u32[]{:S(2)}) collective-permute-start(bf16[128,1536]{1,0:T(8,128)(2,1)S(1)} %collective-permute-done.10), channel_id=1, source_target_pairs={{4,0},{8,4},{12,8},{14,12},{10,14},{6,10},{2,6},{0,2},{5,1},{9,5},... | collective-permute-start | bytes 1179656 | tf_op jit(solution)/shard_map/ppermute | solution.py:52
  74.1 16.7 %collective-permute-start.4 = (bf16[128,1536]{1,0:T(8,128)(2,1)}, bf16[128,1536]{1,0:T(8,128)(2,1)S(1)}, u32[]{:S(2)}, u32[]{:S(2)}) collective-permute-start(bf16[128,1536]{1,0:T(8,128)(2,1)} %collective-permute-done.2), channel_id=1, source_target_pairs={{0,4},{4,8},{8,12},{12,14},{14,10},{10,6},{6,2},{2,0},{1,5},{5,9},... | collective-permute-start | bytes 1179656 | tf_op jit(solution)/shard_map/ppermute | solution.py:48
  79.6 15.5 %collective-permute-start.5 = (bf16[128,1536]{1,0:T(8,128)(2,1)}, bf16[128,1536]{1,0:T(8,128)(2,1)S(1)}, u32[]{:S(2)}, u32[]{:S(2)}) collective-permute-start(bf16[128,1536]{1,0:T(8,128)(2,1)} %collective-permute-done.3), channel_id=1, source_target_pairs={{4,0},{8,4},{12,8},{14,12},{10,14},{6,10},{2,6},{0,2},{5,1},{9,5},... | collective-permute-start | bytes 1179656 | tf_op jit(solution)/shard_map/ppermute | solution.py:52
  82.4 16.9 %collective-permute-start.13 = (bf16[128,1536]{1,0:T(8,128)(2,1)S(1)}, bf16[128,1536]{1,0:T(8,128)(2,1)S(1)}, u32[]{:S(2)}, u32[]{:S(2)}) collective-permute-start(bf16[128,1536]{1,0:T(8,128)(2,1)S(1)} %collective-permute-done.11), channel_id=1, source_target_pairs={{0,4},{4,8},{8,12},{12,14},{14,10},{10,6},{6,2},{2,0},{1,5},{5,9},... | collective-permute-start | bytes 1179656 | tf_op jit(solution)/shard_map/ppermute | solution.py:48
  90.8 14.6 %collective-permute-start.6 = (bf16[128,1536]{1,0:T(8,128)(2,1)S(1)}, bf16[128,1536]{1,0:T(8,128)(2,1)S(1)}, u32[]{:S(2)}, u32[]{:S(2)}) collective-permute-start(bf16[128,1536]{1,0:T(8,128)(2,1)S(1)} %collective-permute-done.4), channel_id=1, source_target_pairs={{0,4},{4,8},{8,12},{12,14},{14,10},{10,6},{6,2},{2,0},{1,5},{5,9},... | collective-permute-start | bytes 1179656 | tf_op jit(solution)/shard_map/ppermute | solution.py:48
  133.7 32.6 %collective-permute-start.14 = (bf16[128,768]{0,1:T(8,128)(2,1)S(1)}, bf16[128,768]{0,1:T(8,128)(2,1)}, u32[]{:S(2)}, u32[]{:S(2)}) collective-permute-start(bf16[128,768]{0,1:T(8,128)(2,1)S(1)} %bitcast.184), channel_id=1, source_target_pairs={{0,4},{4,8},{8,12},{12,14},{14,10},{10,6},{6,2},{2,0},{1,5},{5,9},... | collective-permute-start | bytes 589832 | tf_op jit(solution)/shard_map/ppermute | solution.py:48
  135.4 32.0 %collective-permute-start.15 = (bf16[128,768]{0,1:T(8,128)(2,1)S(1)}, bf16[128,768]{0,1:T(8,128)(2,1)S(1)}, u32[]{:S(2)}, u32[]{:S(2)}) collective-permute-start(bf16[128,768]{0,1:T(8,128)(2,1)S(1)} %bitcast.185), channel_id=1, source_target_pairs={{4,0},{8,4},{12,8},{14,12},{10,14},{6,10},{2,6},{0,2},{5,1},{9,5},... | collective-permute-start | bytes 589832 | tf_op jit(solution)/shard_map/ppermute | solution.py:52
  146.1 12.6 %all-to-all-start = ((f32[8,16,128]{2,1,0:T(8,128)}), f32[8,16,128]{2,1,0:T(8,128)S(1)}, u32[]{:S(2)}, u32[]{:S(2)}) async-start(f32[8,16,128]{2,1,0:T(8,128)} %broadcast_in_dim.169), calls=%async_computation.1 | async-start | bytes 131072 | tf_op jit(solution)/shard_map/all_to_all | solution.py:26
  151.9 7.4 %copy-start.8 = (bf16[1,128,768]{1,2,0:T(8,128)(2,1)S(1)}, bf16[1,128,768]{1,2,0:T(8,128)(2,1)}, u32[]{:S(2)}) copy-start(bf16[1,128,768]{1,2,0:T(8,128)(2,1)} %copy.69) | copy-start | bytes 589828
  165.5 25.4 %copy-start.7 = (bf16[1024,192]{0,1:T(8,128)(2,1)S(1)}, bf16[1024,192]{0,1:T(8,128)(2,1)}, u32[]{:S(2)}) copy-start(bf16[1024,192]{0,1:T(8,128)(2,1)} %copy_bitcast_fusion) | copy-start | bytes 1179652
  167.5 5.9 %collective-permute-start.16 = (bf16[128,768]{0,1:T(8,128)(2,1)}, bf16[128,768]{0,1:T(8,128)(2,1)S(1)}, u32[]{:S(2)}, u32[]{:S(2)}) collective-permute-start(bf16[128,768]{0,1:T(8,128)(2,1)} %collective-permute-done.14), channel_id=1, source_target_pairs={{0,4},{4,8},{8,12},{12,14},{14,10},{10,6},{6,2},{2,0},{1,5},{5,9},... | collective-permute-start | bytes 589832 | tf_op jit(solution)/shard_map/ppermute | solution.py:48
  169.2 6.0 %collective-permute-start.17 = (bf16[128,768]{0,1:T(8,128)(2,1)S(1)}, bf16[128,768]{0,1:T(8,128)(2,1)}, u32[]{:S(2)}, u32[]{:S(2)}) collective-permute-start(bf16[128,768]{0,1:T(8,128)(2,1)S(1)} %collective-permute-done.15), channel_id=1, source_target_pairs={{4,0},{8,4},{12,8},{14,12},{10,14},{6,10},{2,6},{0,2},{5,1},{9,5},... | collective-permute-start | bytes 589832 | tf_op jit(solution)/shard_map/ppermute | solution.py:52
  176.3 7.7 %collective-permute-start.18 = (bf16[128,768]{0,1:T(8,128)(2,1)}, bf16[128,768]{0,1:T(8,128)(2,1)S(1)}, u32[]{:S(2)}, u32[]{:S(2)}) collective-permute-start(bf16[128,768]{0,1:T(8,128)(2,1)} %copy-done.9), channel_id=1, source_target_pairs={{0,4},{4,8},{8,12},{12,14},{14,10},{10,6},{6,2},{2,0},{1,5},{5,9},... | collective-permute-start | bytes 589832 | tf_op jit(solution)/shard_map/ppermute | solution.py:48
  177.9 6.2 %collective-permute-start.19 = (bf16[128,768]{0,1:T(8,128)(2,1)}, bf16[128,768]{0,1:T(8,128)(2,1)S(1)}, u32[]{:S(2)}, u32[]{:S(2)}) collective-permute-start(bf16[128,768]{0,1:T(8,128)(2,1)} %collective-permute-done.17), channel_id=1, source_target_pairs={{4,0},{8,4},{12,8},{14,12},{10,14},{6,10},{2,6},{0,2},{5,1},{9,5},... | collective-permute-start | bytes 589832 | tf_op jit(solution)/shard_map/ppermute | solution.py:52
  184.3 5.7 %collective-permute-start.20 = (bf16[128,768]{0,1:T(8,128)(2,1)S(1)}, bf16[128,768]{0,1:T(8,128)(2,1)S(1)}, u32[]{:S(2)}, u32[]{:S(2)}) collective-permute-start(bf16[128,768]{0,1:T(8,128)(2,1)S(1)} %collective-permute-done.18), channel_id=1, source_target_pairs={{0,4},{4,8},{8,12},{12,14},{14,10},{10,6},{6,2},{2,0},{1,5},{5,9},... | collective-permute-start | bytes 589832 | tf_op jit(solution)/shard_map/ppermute | solution.py:48
  193.6 10.4 %all-to-all-start.2 = ((f32[2,768,96]{1,2,0:T(8,128)}), f32[2,768,96]{1,2,0:T(8,128)S(1)}, u32[]{:S(2)}, u32[]{:S(2)}) async-start(f32[2,768,96]{1,2,0:T(8,128)} %convolution_bitcast_fusion), calls=%async_computation.3 | async-start | bytes 1179648 | tf_op jit(solution)/shard_map/all_to_all | solution.py:62
  197.1 7.7 %copy-start.10 = (bf16[1,128,768]{2,1,0:T(8,128)(2,1)S(1)}, bf16[1,128,768]{2,1,0:T(8,128)(2,1)}, u32[]{:S(2)}) copy-start(bf16[1,128,768]{2,1,0:T(8,128)(2,1)} %param.17) | copy-start | bytes 589828
  (8 other events, 26.3 us)
Sparse Core Ops, SparseCore 0:
  135.9 9.2 reduce-scatter.1

commit v3 on v1

--- a/solution.py
+++ b/solution.py
@@ -26,7 +26,7 @@
     return lax.all_to_all(spread, axis_name, 0, 0, tiled=True)
 
 
-def ring_gather(x, axis_name):
+def ring_gather(x, axis_name, lead=()):
     n = lax.axis_size(axis_name)
     me = lax.axis_index(axis_name)
     if n % 2 == 0:
@@ -40,6 +40,7 @@
     here = jnp.array(place, jnp.int32)[me]
     to_next = [(ring[i], ring[(i + 1) % n]) for i in range(n)]
     to_prev = [(ring[(i + 1) % n], ring[i]) for i in range(n)]
+    x = x.reshape(lead + x.shape)
     gathered = jnp.zeros((n,) + x.shape, x.dtype)
     gathered = lax.dynamic_update_index_in_dim(gathered, x, me, 0)
     ahead = x
@@ -125,7 +126,7 @@
     g_cols = g_cols.reshape(n_seq, frames_here, n_dp * col_width)
     g_mine = lax.all_to_all(g_cols, "seq", 0, 0, tiled=True).reshape(-1, n_dp * col_width)
     qg_rows = jnp.concatenate([own_q, grad_attn], axis=1)
-    qg_all = lax.all_gather(qg_rows, "seq", axis=0, tiled=True)
+    qg_all = ring_gather(qg_rows, "seq", lead=(1,)).reshape(-1, 2 * width)
     k_all = kv_all[:, :width]
     v_all = kv_all[:, width:]
     run_max, run_sum, total = by_blocks(forward_step, start_state, (k_all, v_all))
@@ -133,7 +134,7 @@
     attn_full = total / run_sum[:, :, None]
     attn = join_heads(attn_full).astype(jnp.bfloat16)
     partial_out = jnp.dot(attn, out_weight, preferred_element_type=jnp.float32)
-    mixed = scatter_sum(partial_out, "tensor", 1)
+    mixed = lax.psum_scatter(partial_out, "tensor", scatter_dimension=1, tiled=True)
     block_out = (residual[0].astype(jnp.float32) + mixed).astype(jnp.bfloat16)
     attn_all = lax.all_gather(attn, "seq", axis=0, tiled=True)
     weight_term = lax.dot_general(

time: 255 us -> 220 us (0.86)
  waiting for transfers between devices: 79.8 us -> 15.6 us
  local copies, waits for them, and re-layouts: 79.1 us -> 96.7 us
  starting transfers between devices: 23.9 us -> 30.5 us
  matrix products: 26.2 us -> 30 us
    all_gather x1 -> x0, waiting for transfers between devices: 45.2 us -> none  [shards_body(): qg_all = lax.all_gather(qg_rows, 'seq', axis=0, tiled=True)]
    dynamic_update_slice x5 -> x9, local copies, waits for them, and re-layouts: 25 us -> 36.1 us  [ring_gather(): gathered = lax.dynamic_update_index_in_dim(gathered, ahead, source, 0)]
    all_to_all x1, waiting for transfers between devices: 11 us -> 0.01 us  [shards_body(): lax.all_to_all(g_cols, 'seq', 0, 0, tiled=True)]
    ppermute x4 -> x8, starting transfers between devices: 8.33 us -> 16.6 us  [ring_gather(): ahead = lax.ppermute(ahead, axis_name, to_next)]
    dynamic_update_slice x3 -> x6, local copies, waits for them, and re-layouts: 20.4 us -> 28.6 us  [ring_gather(): gathered = lax.dynamic_update_index_in_dim(gathered, behind, source, 0)]
    all_to_all x2 -> x1, waiting for transfers between devices: 7.73 us -> 0.93 us  [scatter_sum(): return jnp.sum(lax.all_to_all(pieces, axis_name, 0, 0, tiled=True), axis=0)]
    ppermute x4 -> x8, waiting for transfers between devices: 12.3 us -> 7.95 us  [ring_gather(): ahead = lax.ppermute(ahead, axis_name, to_next)]
    all_to_all x2 -> x1, starting transfers between devices: 7.03 us -> 3.5 us  [scatter_sum(): return jnp.sum(lax.all_to_all(pieces, axis_name, 0, 0, tiled=True), axis=0)]
  transfers between devices with their start and end apart: 13 -> 19, of which waited for: 7 -> 5; matrix products, arithmetic and copies ran while one was open for 25% -> 61% of each run, Pallas kernels for 0% -> 0%
where the time goes in v3:
time: 220 us; the launch traced here: 217 us
  local copies, waits for them, and re-layouts  96.7 us (44%)
  between operations  34.2 us (16%)
  starting transfers between devices  30.5 us (14%)
  matrix products  30 us (14%)
  waiting for transfers between devices  15.6 us (7%)
  other arithmetic  8.38 us (4%)
    dynamic_update_slice x9, local copies, waits for them, and re-layouts, ring_gather(): gathered = lax.dynamic_update_index_in_dim(gathered, ahead, source, 0)  36.1 us
    dynamic_update_slice x6, local copies, waits for them, and re-layouts, ring_gather(): gathered = lax.dynamic_update_index_in_dim(gathered, behind, source, 0)  28.6 us
    ppermute x8, starting transfers between devices, ring_gather(): ahead = lax.ppermute(ahead, axis_name, to_next)  16.6 us
    unnamed x40, local copies, waits for them, and re-layouts  9.38 us
    ppermute x8, waiting for transfers between devices, ring_gather(): ahead = lax.ppermute(ahead, axis_name, to_next)  7.95 us
    all_gather x1, waiting for transfers between devices, shards_body(): attn_all = lax.all_gather(attn, 'seq', axis=0, tiled=True)  6.69 us
    dot_general x1, matrix products, key_step(): jnp.einsum('hij,ihc->hjc', dscores, q_part, preferred_element_type=jnp.fl...  6.56 us
    slice x2, local copies, waits for them, and re-layouts, shards_body(): qg_all[:, width:]  6.41 us
  transfers between devices with their start and end apart: 19, of which 5 were waited for; matrix products, arithmetic and copies ran while one was open for 61% of the time, Pallas kernels for 0%

profile of v3, /device:TPU:0, one launch (start us, length us, event | category | flops | bytes accessed | tf_op | source)
XLA Modules:
  0.0 217.5 jit_solution(12134203779306624459)
XLA Ops:
  8.0 2.0 pad_maximum_fusion
  10.0 3.1 %collective-permute-start = (bf16[128,1536]{1,0:T(8,128)(2,1)}, bf16[128,1536]{1,0:T(8,128)(2,1)}, u32[]{:S(2)}, u32[]{:S(2)}) collective-permute-start(bf16[128,1536]{1,0:T(8,128)(2,1)} %pad_maximum_fusion), channel_id=1, source_target_pairs={{0,4},{4,8},{8,12},{12,14},{14,10},{10,6},{6,2},{2,0},{1,5},{5,9},... | collective-permute-start | bytes 1179656 | tf_op jit(solution)/shard_map/ppermute | solution.py:49
  14.1 2.1 all-gather
  18.0 2.0 collective-permute-start.7
  20.8 6.3 %all-to-all-start.1 = ((bf16[8,128,192]{1,2,0:T(8,128)(2,1)}), bf16[8,128,192]{1,2,0:T(8,128)(2,1)S(1)}, u32[]{:S(2)}, u32[]{:S(2)}) async-start(bf16[8,128,192]{1,2,0:T(8,128)(2,1)} %bitcast.194), calls=%async_computation.2 | async-start | bytes 786432 | tf_op jit(solution)/shard_map/all_to_all | solution.py:127
  27.8 1.9 broadcast_in_dim.131
  53.3 1.9 broadcast_in_dim.143
  56.0 2.0 collective-permute-start.2
  58.1 2.0 collective-permute-start.9
  68.2 2.0 collective-permute-start.4
  70.3 6.5 %collective-permute-done.9 = bf16[1,128,1536]{2,1,0:T(8,128)(2,1)} collective-permute-done((bf16[1,128,1536]{2,1,0:T(8,128)(2,1)}, bf16[1,128,1536]{2,1,0:T(8,128)(2,1)}, u32[]{:S(2)}, u32[]{:S(2)}) %collective-permute-start.9) | collective-permute-done | bytes 393248 | tf_op jit(solution)/shard_map/ppermute | solution.py:49
  76.7 2.0 collective-permute-start.11
  85.2 2.0 collective-permute-start.6
  87.2 1.8 bitcast_dynamic-update-slice_fusion.8
  89.0 5.0 %copy.53 = bf16[8,128,1536]{1,0,2:T(8,128)(2,1)} copy(bf16[8,128,1536]{2,1,0:T(8,128)(2,1)} %bitcast_dynamic-update-slice_fusion.8) | data formatting | bytes 6291456 | tf_op jit(solution)/shard_map/jit(dynamic_update_index_in_dim)/dynamic_update_slice | solution.py:51
  94.0 2.2 copy.54
  96.1 20.7 %dynamic_update_slice.56 = bf16[8,128,1536]{1,0,2:T(8,128)(2,1)} dynamic-update-slice(bf16[8,128,1536]{1,0,2:T(8,128)(2,1)} %copy.53, bf16[1,128,1536]{1,0,2:T(2,128)(2,1)S(1)} %copy.54, s32[]{:T(128)S(6)} %select_n.195, s32[]{:T(128)} %constant.191.clone.1, s32[]{:T(128)} %constant.191.clone.1) | dynamic-update-slice | bytes 786436 | tf_op jit(solution)/shard_map/jit(dynamic_update_index_in_dim)/dynamic_update_slice | solution.py:55
  118.3 2.2 copy.55
  120.5 20.7 %dynamic_update_slice.57 = bf16[8,128,1536]{1,0,2:T(8,128)(2,1)} dynamic-update-slice(bf16[8,128,1536]{1,0,2:T(8,128)(2,1)} %dynamic_update_slice.56, bf16[1,128,1536]{1,0,2:T(2,128)(2,1)S(1)} %copy.55, s32[]{:T(128)S(6)} %select_n.198, s32[]{:T(128)} %constant.191.clone.1, s32[]{:T(128)} %constant.191.clone.1) | dynamic-update-slice | bytes 786436 | tf_op jit(solution)/shard_map/jit(dynamic_update_index_in_dim)/dynamic_update_slice | solution.py:51
  141.1 2.7 %copy.87 = bf16[192,8,8,128]{3,1,2,0:T(8,128)(2,1)S(1)} copy(bf16[192,8,8,128]{3,2,1,0:T(8,128)(2,1)} %bitcast.179) | data formatting | bytes 6291456
  147.1 3.7 %fusion.35 = (bf16[128,8,96]{0,2,1:T(8,128)(2,1)S(1)}, f32[8,128,96]{1,2,0:T(8,128)S(1)}) fusion(f32[128,8]{0,1:T(8,128)S(1)} %bitcast_add_fusion.1, f32[128,8]{0,1:T(8,128)S(1)} %get-tuple-element.109, bf16[1024,8,96]{0,2,1:T(8,128)(2,1)S(1)} %bitcast.195, f32[8,1024,128]{2,1,0:T(8,128)S(1)} %get-tuple-element.131, ...), kind=kOutput, calls=%fused_computation.51 | convolution fusion | flops 1211400192 | bytes 6370304 | tf_op jit(solution)/shard_map/while/body/eval_jaxpr/hij,jhc->hic/dot_general | solution.py:105
  154.3 5.6 %fusion.26 = bf16[8,128,96]{1,2,0:T(8,128)(2,1)S(1)} fusion(bf16[1024,8,96]{0,2,1:T(8,128)(2,1)} %bitcast.184, f32[8,1024,128]{2,1,0:T(8,128)} %copy-done.1, bf16[128,8,96]{0,2,1:T(8,128)(2,1)S(1)} %bitcast.202, bf16[1024,8,96]{0,2,1:T(8,128)(2,1)} %bitcast.196, f32[8,128]{1,0:T(8,128)S(1)} %fusion.32, f32[8,128]{1,0:T(8,128)S(1)} %get-tuple-element.107, ...), kind=kOutput, calls=%fused_computation.29 | convolution fusion | flops 410091520 | bytes 7742464 | tf_op jit(solution)/shard_map/while/body/eval_jaxpr/hij,jhc->hic/dot_general | solution.py:156
  162.5 3.8 %fusion.48 = (bf16[1024,768]{1,0:T(8,128)(2,1)}, bf16[1024,768]{1,0:T(8,128)(2,1)}) fusion(bf16[1024,1536]{1,0:T(8,128)(2,1)} %bitcast.58), kind=kLoop, calls=%fused_computation.79 | loop fusion | bytes 6291456 | tf_op jit(solution)/shard_map/slice | solution.py:187
  166.3 2.6 %copy.70 = bf16[1024,768]{0,1:T(8,128)(2,1)} copy(bf16[1024,768]{1,0:T(8,128)(2,1)} %get-tuple-element.102) | data formatting | bytes 3145728 | tf_op jit(solution)/shard_map/slice | solution.py:186
  169.6 3.7 %all-to-all-start = ((f32[8,16,128]{2,1,0:T(8,128)}), f32[8,16,128]{2,1,0:T(8,128)S(1)}, u32[]{:S(2)}, u32[]{:S(2)}) async-start(f32[8,16,128]{2,1,0:T(8,128)} %broadcast_in_dim.152), calls=%async_computation.1 | async-start | bytes 131072 | tf_op jit(solution)/shard_map/all_to_all | solution.py:26
  175.0 4.3 %fusion.52 = f32[8,1024,128]{2,1,0:T(8,128)} fusion(bf16[1024,8,96]{0,2,1:T(8,128)(2,1)} %bitcast.181, bf16[128,8,96]{0,2,1:T(8,128)(2,1)S(1)} %bitcast.197), kind=kOutput, calls=%fused_computation.83 | convolution fusion | flops 201326592 | bytes 5963776 | tf_op jit(solution)/shard_map/while/body/eval_jaxpr/ihc,jhc->hij/dot_general | solution.py:93
  179.3 2.6 %copy.72 = bf16[1024,768]{0,1:T(8,128)(2,1)} copy(bf16[1024,768]{1,0:T(8,128)(2,1)} %get-tuple-element.101) | data formatting | bytes 3145728 | tf_op jit(solution)/shard_map/slice | solution.py:187
  181.9 6.6 %fusion.27 = bf16[8,128,96]{1,2,0:T(8,128)(2,1)S(1)} fusion(bf16[1024,8,96]{0,2,1:T(8,128)(2,1)} %bitcast.182, f32[8,1024,128]{2,1,0:T(8,128)} %fusion.52, bf16[1024,8,96]{0,2,1:T(8,128)(2,1)} %bitcast.192, bf16[128,8,96]{0,2,1:T(8,128)(2,1)S(1)} %bitcast.205, f32[8,1024]{1,0:T(8,128)S(1)} %get-tuple-element.106, f32[8,1024]{1,0:T(8,128)S(1)} %get-tuple-element.105, ...), kind=kOutput, calls=%fused_computation.30 | convolution fusion | flops 410091520 | bytes 7798912 | tf_op jit(solution)/shard_map/while/body/eval_jaxpr/hij,ihc->hjc/dot_general | solution.py:174
  188.5 6.7 %all-gather.3.cloned.1.call-done = bf16[1024,768]{1,0:T(8,128)(2,1)} async-done(((bf16[128,768]{1,0:T(8,128)(2,1)}), bf16[1024,768]{1,0:T(8,128)(2,1)}) %all-gather.3.cloned.1.call-update) | async-done | bytes 1572880 | tf_op jit(solution)/shard_map/all_gather | solution.py:139
  195.2 2.7 %fusion.23 = f32[2,768,96]{1,2,0:T(8,128)} fusion(bf16[2,96,1024]{2,1,0:T(8,128)(2,1)S(1)} %bitcast.203, bf16[1024,768]{1,0:T(8,128)(2,1)} %all-gather.3.cloned.1.call-done), kind=kOutput, calls=%fused_computation.28 | convolution fusion | flops 301989888 | bytes 2555904 | tf_op jit(solution)/shard_map/dot_general | solution.py:140
  197.9 3.5 %all-to-all-start.2 = ((f32[2,768,96]{1,2,0:T(8,128)}), f32[2,768,96]{1,2,0:T(8,128)S(1)}, u32[]{:S(2)}, u32[]{:S(2)}) async-start(f32[2,768,96]{1,2,0:T(8,128)} %fusion.23), calls=%async_computation.3 | async-start | bytes 1179648 | tf_op jit(solution)/shard_map/all_to_all | solution.py:63
  201.4 3.6 %fusion.28 = bf16[8,128,96]{1,2,0:T(8,128)(2,1)S(1)} fusion(bf16[1024,8,96]{0,2,1:T(8,128)(2,1)} %bitcast.193, f32[8,1024,128]{2,1,0:T(8,128)} %fusion.52, f32[8,1024]{1,0:T(8,128)S(1)} %get-tuple-element.105, pred[128]{0:T(512)(128)(4,1)S(1)} %copy-done.14), kind=kOutput, calls=%fused_computation.31 | convolution fusion | flops 205619200 | bytes 5996672 | tf_op jit(solution)/shard_map/while/body/eval_jaxpr/hij,ihc->hjc/dot_general | solution.py:177
  (103 shorter events, 43.0 us)
Async XLA Ops:
  8.0 8.2 %copy-start = (bf16[768,1536]{1,0:T(8,128)(2,1)S(1)}, bf16[768,1536]{1,0:T(8,128)(2,1)}, u32[]{:S(2)}) copy-start(bf16[768,1536]{1,0:T(8,128)(2,1)} %param.14) | copy-start | bytes 7077892
  8.0 9.2 %copy-start.5 = (bf16[1,128,768]{2,1,0:T(8,128)(2,1)S(1)}, bf16[1,128,768]{2,1,0:T(8,128)(2,1)}, u32[]{:S(2)}) copy-start(bf16[1,128,768]{2,1,0:T(8,128)(2,1)} %param.11) | copy-start | bytes 589828
  10.0 46.0 %collective-permute-start = (bf16[128,1536]{1,0:T(8,128)(2,1)}, bf16[128,1536]{1,0:T(8,128)(2,1)}, u32[]{:S(2)}, u32[]{:S(2)}) collective-permute-start(bf16[128,1536]{1,0:T(8,128)(2,1)} %pad_maximum_fusion), channel_id=1, source_target_pairs={{0,4},{4,8},{8,12},{12,14},{14,10},{10,6},{6,2},{2,0},{1,5},{5,9},... | collective-permute-start | bytes 1179656 | tf_op jit(solution)/shard_map/ppermute | solution.py:49
  13.1 45.0 %collective-permute-start.1 = (bf16[128,1536]{1,0:T(8,128)(2,1)}, bf16[128,1536]{1,0:T(8,128)(2,1)}, u32[]{:S(2)}, u32[]{:S(2)}) collective-permute-start(bf16[128,1536]{1,0:T(8,128)(2,1)} %pad_maximum_fusion), channel_id=1, source_target_pairs={{4,0},{8,4},{12,8},{14,12},{10,14},{6,10},{2,6},{0,2},{5,1},{9,5},... | collective-permute-start | bytes 1179656 | tf_op jit(solution)/shard_map/ppermute | solution.py:53
  17.2 12.5 %copy-start.3 = (bf16[1,128,768]{2,1,0:T(8,128)(2,1)S(1)}, bf16[1,128,768]{2,1,0:T(8,128)(2,1)}, u32[]{:S(2)}) copy-start(bf16[1,128,768]{2,1,0:T(8,128)(2,1)} %param.12) | copy-start | bytes 589828
  17.2 12.5 %copy-start.4 = (bf16[1,128,768]{2,1,0:T(8,128)(2,1)S(1)}, bf16[1,128,768]{2,1,0:T(8,128)(2,1)}, u32[]{:S(2)}) copy-start(bf16[1,128,768]{2,1,0:T(8,128)(2,1)} %param.13) | copy-start | bytes 589828
  17.2 13.8 %copy-start.15 = (s32[8]{0:T(128)S(1)}, s32[8]{0:T(128)}, u32[]{:S(2)}) copy-start(s32[8]{0:T(128)} %constant.205.clone) | copy-start | bytes 100
  17.2 19.1 %copy-start.12 = (s32[8]{0:T(128)S(1)}, s32[8]{0:T(128)}, u32[]{:S(2)}) copy-start(s32[8]{0:T(128)} %constant.204.clone) | copy-start | bytes 100
  18.0 40.1 %collective-permute-start.7 = (bf16[1,128,1536]{2,1,0:T(8,128)(2,1)}, bf16[1,128,1536]{2,1,0:T(8,128)(2,1)}, u32[]{:S(2)}, u32[]{:S(2)}) collective-permute-start(bf16[1,128,1536]{2,1,0:T(8,128)(2,1)} %fusion.36), channel_id=1, source_target_pairs={{0,4},{4,8},{8,12},{12,14},{14,10},{10,6},{6,2},{2,0},{1,5},{5,9},... | collective-permute-start | bytes 1179656 | tf_op jit(solution)/shard_map/ppermute | solution.py:49
  20.0 43.6 %collective-permute-start.8 = (bf16[1,128,1536]{2,1,0:T(8,128)(2,1)}, bf16[1,128,1536]{2,1,0:T(8,128)(2,1)}, u32[]{:S(2)}, u32[]{:S(2)}) collective-permute-start(bf16[1,128,1536]{2,1,0:T(8,128)(2,1)} %fusion.36), channel_id=1, source_target_pairs={{4,0},{8,4},{12,8},{14,12},{10,14},{6,10},{2,6},{0,2},{5,1},{9,5},... | collective-permute-start | bytes 1179656 | tf_op jit(solution)/shard_map/ppermute | solution.py:53
  20.8 46.4 %all-to-all-start.1 = ((bf16[8,128,192]{1,2,0:T(8,128)(2,1)}), bf16[8,128,192]{1,2,0:T(8,128)(2,1)S(1)}, u32[]{:S(2)}, u32[]{:S(2)}) async-start(bf16[8,128,192]{1,2,0:T(8,128)(2,1)} %bitcast.194), calls=%async_computation.2 | async-start | bytes 786432 | tf_op jit(solution)/shard_map/all_to_all | solution.py:127
  27.1 168.1 %all-gather.3.cloned.1.call-start = ((), (), s32[]{:S(2)}) async-start(), calls=%async_computation.5 | async-start | bytes 1769472 | tf_op jit(solution)/shard_map/all_gather | solution.py:139
  53.3 92.8 %copy-start.13 = (pred[1024]{0:T(1024)(128)(4,1)}, pred[1024]{0:T(1024)(128)(4,1)S(1)}, u32[]{:S(2)}) copy-start(pred[1024]{0:T(1024)(128)(4,1)S(1)} %iota_compare_fusion) | copy-start | bytes 3076
  56.0 12.2 %collective-permute-start.2 = (bf16[128,1536]{1,0:T(8,128)(2,1)}, bf16[128,1536]{1,0:T(8,128)(2,1)S(1)}, u32[]{:S(2)}, u32[]{:S(2)}) collective-permute-start(bf16[128,1536]{1,0:T(8,128)(2,1)} %collective-permute-done), channel_id=1, source_target_pairs={{0,4},{4,8},{8,12},{12,14},{14,10},{10,6},{6,2},{2,0},{1,5},{5,9},... | collective-permute-start | bytes 1179656 | tf_op jit(solution)/shard_map/ppermute | solution.py:49
  58.0 12.2 %collective-permute-start.3 = (bf16[128,1536]{1,0:T(8,128)(2,1)}, bf16[128,1536]{1,0:T(8,128)(2,1)S(1)}, u32[]{:S(2)}, u32[]{:S(2)}) collective-permute-start(bf16[128,1536]{1,0:T(8,128)(2,1)} %collective-permute-done.1), channel_id=1, source_target_pairs={{4,0},{8,4},{12,8},{14,12},{10,14},{6,10},{2,6},{0,2},{5,1},{9,5},... | collective-permute-start | bytes 1179656 | tf_op jit(solution)/shard_map/ppermute | solution.py:53
  58.1 18.7 %collective-permute-start.9 = (bf16[1,128,1536]{2,1,0:T(8,128)(2,1)}, bf16[1,128,1536]{2,1,0:T(8,128)(2,1)}, u32[]{:S(2)}, u32[]{:S(2)}) collective-permute-start(bf16[1,128,1536]{2,1,0:T(8,128)(2,1)} %collective-permute-done.7), channel_id=1, source_target_pairs={{0,4},{4,8},{8,12},{12,14},{14,10},{10,6},{6,2},{2,0},{1,5},{5,9},... | collective-permute-start | bytes 1179656 | tf_op jit(solution)/shard_map/ppermute | solution.py:49
  63.6 17.7 %collective-permute-start.10 = (bf16[1,128,1536]{2,1,0:T(8,128)(2,1)}, bf16[1,128,1536]{2,1,0:T(8,128)(2,1)}, u32[]{:S(2)}, u32[]{:S(2)}) collective-permute-start(bf16[1,128,1536]{2,1,0:T(8,128)(2,1)} %collective-permute-done.8), channel_id=1, source_target_pairs={{4,0},{8,4},{12,8},{14,12},{10,14},{6,10},{2,6},{0,2},{5,1},{9,5},... | collective-permute-start | bytes 1179656 | tf_op jit(solution)/shard_map/ppermute | solution.py:53
  68.2 17.0 %collective-permute-start.4 = (bf16[128,1536]{1,0:T(8,128)(2,1)S(1)}, bf16[128,1536]{1,0:T(8,128)(2,1)}, u32[]{:S(2)}, u32[]{:S(2)}) collective-permute-start(bf16[128,1536]{1,0:T(8,128)(2,1)S(1)} %collective-permute-done.2), channel_id=1, source_target_pairs={{0,4},{4,8},{8,12},{12,14},{14,10},{10,6},{6,2},{2,0},{1,5},{5,9},... | collective-permute-start | bytes 1179656 | tf_op jit(solution)/shard_map/ppermute | solution.py:49
  70.2 23.7 %collective-permute-start.5 = (bf16[128,1536]{1,0:T(8,128)(2,1)S(1)}, bf16[128,1536]{1,0:T(8,128)(2,1)}, u32[]{:S(2)}, u32[]{:S(2)}) collective-permute-start(bf16[128,1536]{1,0:T(8,128)(2,1)S(1)} %collective-permute-done.3), channel_id=1, source_target_pairs={{4,0},{8,4},{12,8},{14,12},{10,14},{6,10},{2,6},{0,2},{5,1},{9,5},... | collective-permute-start | bytes 1179656 | tf_op jit(solution)/shard_map/ppermute | solution.py:53
  76.7 40.1 %collective-permute-start.11 = (bf16[1,128,1536]{2,1,0:T(8,128)(2,1)}, bf16[1,128,1536]{2,1,0:T(8,128)(2,1)S(1)}, u32[]{:S(2)}, u32[]{:S(2)}) collective-permute-start(bf16[1,128,1536]{2,1,0:T(8,128)(2,1)} %collective-permute-done.9), channel_id=1, source_target_pairs={{0,4},{4,8},{8,12},{12,14},{14,10},{10,6},{6,2},{2,0},{1,5},{5,9},... | collective-permute-start | bytes 1179656 | tf_op jit(solution)/shard_map/ppermute | solution.py:49
  81.3 71.1 %collective-permute-start.12 = (bf16[1,128,1536]{2,1,0:T(8,128)(2,1)}, bf16[1,128,1536]{2,1,0:T(8,128)(2,1)}, u32[]{:S(2)}, u32[]{:S(2)}) collective-permute-start(bf16[1,128,1536]{2,1,0:T(8,128)(2,1)} %collective-permute-done.10), channel_id=1, source_target_pairs={{4,0},{8,4},{12,8},{14,12},{10,14},{6,10},{2,6},{0,2},{5,1},{9,5},... | collective-permute-start | bytes 1179656 | tf_op jit(solution)/shard_map/ppermute | solution.py:53
  85.2 33.1 %collective-permute-start.6 = (bf16[128,1536]{1,0:T(8,128)(2,1)}, bf16[128,1536]{1,0:T(8,128)(2,1)}, u32[]{:S(2)}, u32[]{:S(2)}) collective-permute-start(bf16[128,1536]{1,0:T(8,128)(2,1)} %collective-permute-done.4), channel_id=1, source_target_pairs={{0,4},{4,8},{8,12},{12,14},{14,10},{10,6},{6,2},{2,0},{1,5},{5,9},... | collective-permute-start | bytes 1179656 | tf_op jit(solution)/shard_map/ppermute | solution.py:49
  116.8 43.9 %collective-permute-start.13 = (bf16[1,128,1536]{2,1,0:T(8,128)(2,1)S(1)}, bf16[1,128,1536]{2,1,0:T(8,128)(2,1)}, u32[]{:S(2)}, u32[]{:S(2)}) collective-permute-start(bf16[1,128,1536]{2,1,0:T(8,128)(2,1)S(1)} %collective-permute-done.11), channel_id=1, source_target_pairs={{0,4},{4,8},{8,12},{12,14},{14,10},{10,6},{6,2},{2,0},{1,5},{5,9},... | collective-permute-start | bytes 1179656 | tf_op jit(solution)/shard_map/ppermute | solution.py:49
  146.1 4.7 %copy-start.1 = (f32[8,1024,128]{2,1,0:T(8,128)}, f32[8,1024,128]{2,1,0:T(8,128)S(1)}, u32[]{:S(2)}) copy-start(f32[8,1024,128]{2,1,0:T(8,128)S(1)} %get-tuple-element.131) | copy-start | bytes 12582916
  147.1 7.1 %copy-start.9 = (bf16[128,768]{0,1:T(8,128)(2,1)S(1)}, bf16[128,768]{0,1:T(8,128)(2,1)}, u32[]{:S(2)}) copy-start(bf16[128,768]{0,1:T(8,128)(2,1)} %copy.59) | copy-start | bytes 589828
  166.3 8.6 %copy-start.7 = (bf16[1,128,768]{1,2,0:T(8,128)(2,1)S(1)}, bf16[1,128,768]{1,2,0:T(8,128)(2,1)}, u32[]{:S(2)}) copy-start(bf16[1,128,768]{1,2,0:T(8,128)(2,1)} %copy.71) | copy-start | bytes 589828
  169.6 12.3 %all-to-all-start = ((f32[8,16,128]{2,1,0:T(8,128)}), f32[8,16,128]{2,1,0:T(8,128)S(1)}, u32[]{:S(2)}, u32[]{:S(2)}) async-start(f32[8,16,128]{2,1,0:T(8,128)} %broadcast_in_dim.152), calls=%async_computation.1 | async-start | bytes 131072 | tf_op jit(solution)/shard_map/all_to_all | solution.py:26
  173.2 33.4 %reduce-scatter.2.cloned.1.call-start = ((), (), s32[]{:S(2)}) async-start(), calls=%async_computation.4 | async-start | bytes 1179648 | tf_op jit(solution)/shard_map/reduce_scatter | solution.py:137
  174.9 6.9 %copy-start.11 = (bf16[1,128,768]{1,2,0:T(8,128)(2,1)S(1)}, bf16[1,128,768]{1,2,0:T(8,128)(2,1)}, u32[]{:S(2)}) copy-start(bf16[1,128,768]{1,2,0:T(8,128)(2,1)} %copy.73) | copy-start | bytes 589828
  174.9 6.9 %copy-start.14 = (pred[128]{0:T(512)(128)(4,1)S(1)}, pred[128]{0:T(512)(128)(4,1)}, u32[]{:S(2)}) copy-start(pred[128]{0:T(512)(128)(4,1)} %add_compare_fusion) | copy-start | bytes 388
  181.9 13.3 %copy-start.10 = (bf16[1024,192]{0,1:T(8,128)(2,1)S(1)}, bf16[1024,192]{0,1:T(8,128)(2,1)}, u32[]{:S(2)}) copy-start(bf16[1024,192]{0,1:T(8,128)(2,1)} %copy_bitcast_fusion.1) | copy-start | bytes 1179652
  197.9 11.4 %all-to-all-start.2 = ((f32[2,768,96]{1,2,0:T(8,128)}), f32[2,768,96]{1,2,0:T(8,128)S(1)}, u32[]{:S(2)}, u32[]{:S(2)}) async-start(f32[2,768,96]{1,2,0:T(8,128)} %fusion.23), calls=%async_computation.3 | async-start | bytes 1179648 | tf_op jit(solution)/shard_map/all_to_all | solution.py:63
  (3 other events, 6.6 us)
Sparse Core Ops, SparseCore 0:
  151.7 43.3 all-gather.2
Sparse Core Ops, SparseCore 1:
  176.0 9.5 reduce-scatter.1

commit v4 on v1

--- a/solution.py
+++ b/solution.py
@@ -117,15 +117,17 @@
     ).astype(jnp.bfloat16)
     width = own_k.shape[1]
     kv_rows = jnp.concatenate([own_k, own_v], axis=1)
-    kv_all = ring_gather(kv_rows, "seq").reshape(-1, 2 * width)
+    everything = ring_gather(
+        jnp.concatenate([kv_rows, own_q, grad_attn], axis=1), "seq"
+    ).reshape(-1, 4 * width)
+    kv_all = everything[:, : 2 * width]
+    qg_all = everything[:, 2 * width :]
     n_seq = lax.axis_size("seq")
     n_dp = lax.axis_size("dp")
     col_width = grad_full.shape[1] // (n_dp * n_seq)
     g_cols = jnp.transpose(grad_full.reshape(frames_here, n_dp, n_seq, col_width), (2, 0, 1, 3))
     g_cols = g_cols.reshape(n_seq, frames_here, n_dp * col_width)
     g_mine = lax.all_to_all(g_cols, "seq", 0, 0, tiled=True).reshape(-1, n_dp * col_width)
-    qg_rows = jnp.concatenate([own_q, grad_attn], axis=1)
-    qg_all = lax.all_gather(qg_rows, "seq", axis=0, tiled=True)
     k_all = kv_all[:, :width]
     v_all = kv_all[:, width:]
     run_max, run_sum, total = by_blocks(forward_step, start_state, (k_all, v_all))

time: 255 us -> 193 us (0.76); the launches traced: 251 us -> 192 us
  local copies, waits for them, and re-layouts: 79.1 us -> 29.4 us
  waiting for transfers between devices: 79.8 us -> 61.7 us
  matrix products: 26.2 us -> 34.5 us
  starting transfers between devices: 23.9 us -> 27.3 us
    all_gather x1 -> x0, waiting for transfers between devices: 45.2 us -> none  [shards_body(): qg_all = lax.all_gather(qg_rows, 'seq', axis=0, tiled=True)]
    ppermute x4, waiting for transfers between devices: 12.3 us -> 45.5 us  [ring_gather(): ahead = lax.ppermute(ahead, axis_name, to_next)]
    dynamic_update_slice x5 -> x4, local copies, waits for them, and re-layouts: 25 us -> 1.4 us  [ring_gather(): gathered = lax.dynamic_update_index_in_dim(gathered, ahead, source, 0)]
    dynamic_update_slice x3, local copies, waits for them, and re-layouts: 20.4 us -> 1.35 us  [ring_gather(): gathered = lax.dynamic_update_index_in_dim(gathered, behind, source, 0)]
    all_to_all x1, waiting for transfers between devices: 11 us -> 0.01 us  [shards_body(): lax.all_to_all(g_cols, 'seq', 0, 0, tiled=True)]
    all_gather x1, waiting for transfers between devices: 3.51 us -> 12.4 us  [shards_body(): attn_all = lax.all_gather(attn, 'seq', axis=0, tiled=True)]
    broadcast_in_dim x2 -> x0, local copies, waits for them, and re-layouts: 5.91 us -> none  [the longest x1 2.96 us: ring_gather(): gathered = lax.dynamic_update_index_in_dim(gathered, behind, source, 0)]
    all_to_all x2, waiting for transfers between devices: 7.73 us -> 3.85 us  [scatter_sum(): return jnp.sum(lax.all_to_all(pieces, axis_name, 0, 0, tiled=True), axis=0)]
  transfers between devices with their start and end apart: 13 -> 12, of which waited for: 7 -> 6; matrix products, arithmetic and copies ran while one was open for 25% -> 30% of each run, Pallas kernels for 0% -> 0%
where the time goes in v4:
time: 193 us; the launch traced here: 192 us
  waiting for transfers between devices  61.7 us (32%)
  matrix products  34.5 us (18%)
  between operations  32.4 us (17%)
  local copies, waits for them, and re-layouts  29.4 us (15%)
  starting transfers between devices  27.3 us (14%)
  other arithmetic  4.72 us (2%)
  blocking collectives  2.34 us (1%)
    ppermute x4, waiting for transfers between devices, ring_gather(): ahead = lax.ppermute(ahead, axis_name, to_next)  45.5 us
    all_gather x1, waiting for transfers between devices, shards_body(): attn_all = lax.all_gather(attn, 'seq', axis=0, tiled=True)  12.4 us
    ppermute x4, starting transfers between devices, ring_gather(): ahead = lax.ppermute(ahead, axis_name, to_next)  8.17 us
    unnamed x43, local copies, waits for them, and re-layouts  8.1 us
    all_to_all x2, starting transfers between devices, scatter_sum(): return jnp.sum(lax.all_to_all(pieces, axis_name, 0, 0, tiled=True), axis=0)  7.16 us
    dot_general x1, matrix products, key_step(): jnp.einsum('hij,ihc->hjc', dscores, q_part, preferred_element_type=jnp.fl...  6.41 us
    dot_general x1, matrix products, forward_step(): jnp.einsum('hij,jhc->hic', weights, split_heads(v_rows).astype(jnp.float3...  6.39 us
    all_to_all x1, starting transfers between devices, shards_body(): lax.all_to_all(g_cols, 'seq', 0, 0, tiled=True)  6.28 us
  transfers between devices with their start and end apart: 12, of which 6 were waited for; matrix products, arithmetic and copies ran while one was open for 30% of the time, Pallas kernels for 0%

profile of v4, /device:TPU:0, one launch (start us, length us, event | category | flops | bytes accessed | tf_op | source)
XLA Modules:
  0.0 192.4 jit_solution(10118557304337042216)
XLA Ops:
  8.4 2.3 %all-gather = bf16[1,128,1536]{1,2,0:T(8,128)(2,1)S(1)} all-gather(bf16[1,128,768]{1,2,0:T(8,128)(2,1)S(1)} %copy.43), channel_id=2, replica_groups=mesh['dp'=2,'seq'=8,'tensor'=2] {'tensor'}, dimensions={2}, use_global_device_ids=true | all-gather | bytes 589824 | tf_op jit(solution)/shard_map/all_gather | solution.py:114
  10.7 2.6 %convolution_convert_fusion = bf16[128,768]{1,0:T(8,128)(2,1)S(1)} fusion(bf16[768,1536]{1,0:T(8,128)(2,1)} %param.12, bf16[1,128,1536]{1,2,0:T(8,128)(2,1)S(1)} %all-gather), kind=kOutput, calls=%fused_computation.32 | convolution fusion | flops 302088192 | bytes 2949120 | tf_op jit(solution)/shard_map/dot_general | solution.py:115
  13.3 2.1 %pad_maximum_fusion = bf16[128,3072]{1,0:T(8,128)(2,1)} fusion(bf16[128,768]{1,0:T(8,128)(2,1)S(1)} %convolution_convert_fusion, bf16[128,768]{1,0:T(8,128)(2,1)} %bitcast.154, bf16[128,768]{1,0:T(8,128)(2,1)} %bitcast.156, bf16[128,768]{1,0:T(8,128)(2,1)} %bitcast.158), kind=kLoop, calls=%fused_computation.33 | loop fusion | flops 3145728 | bytes 1572864 | tf_op jit(solution)/shard_map/concatenate | solution.py:121
  15.4 2.9 %collective-permute-start = (bf16[128,3072]{1,0:T(8,128)(2,1)}, bf16[128,3072]{1,0:T(8,128)(2,1)}, u32[]{:S(2)}, u32[]{:S(2)}) collective-permute-start(bf16[128,3072]{1,0:T(8,128)(2,1)} %pad_maximum_fusion), channel_id=1, source_target_pairs={{0,4},{4,8},{8,12},{12,14},{14,10},{10,6},{6,2},{2,0},{1,5},{5,9},... | collective-permute-start | bytes 2359304 | tf_op jit(solution)/shard_map/ppermute | solution.py:48
  19.1 6.3 %all-to-all-start.2 = ((bf16[8,128,192]{1,2,0:T(8,128)(2,1)}), bf16[8,128,192]{1,2,0:T(8,128)(2,1)S(1)}, u32[]{:S(2)}, u32[]{:S(2)}) async-start(bf16[8,128,192]{1,2,0:T(8,128)(2,1)} %bitcast.164), calls=%async_computation.2 | async-start | bytes 786432 | tf_op jit(solution)/shard_map/all_to_all | solution.py:130
  43.8 2.5 %copy.68 = bf16[1536,768]{1,0:T(8,128)(2,1)} copy(bf16[1536,768]{0,1:T(8,128)(2,1)S(1)} %bitcast.147) | data formatting | bytes 4718592 | tf_op jit(solution)/shard_map/dot_general | solution.py:137
  51.4 2.0 %collective-permute-start.2 = (bf16[128,3072]{1,0:T(8,128)(2,1)}, bf16[128,3072]{1,0:T(8,128)(2,1)S(1)}, u32[]{:S(2)}, u32[]{:S(2)}) collective-permute-start(bf16[128,3072]{1,0:T(8,128)(2,1)} %collective-permute-done), channel_id=1, source_target_pairs={{0,4},{4,8},{8,12},{12,14},{14,10},{10,6},{6,2},{2,0},{1,5},{5,9},... | collective-permute-start | bytes 2359304 | tf_op jit(solution)/shard_map/ppermute | solution.py:48
  54.7 1.2 bitcast_dynamic-update-slice_fusion.5
  55.9 14.5 %collective-permute-done.2 = bf16[128,3072]{1,0:T(8,128)(2,1)S(1)} collective-permute-done((bf16[128,3072]{1,0:T(8,128)(2,1)}, bf16[128,3072]{1,0:T(8,128)(2,1)S(1)}, u32[]{:S(2)}, u32[]{:S(2)}) %collective-permute-start.2) | collective-permute-done | bytes 786464 | tf_op jit(solution)/shard_map/ppermute | solution.py:48
  70.4 1.7 collective-permute-start.4
  72.6 15.7 %collective-permute-done.4 = bf16[128,3072]{1,0:T(8,128)(2,1)S(1)} collective-permute-done((bf16[128,3072]{1,0:T(8,128)(2,1)S(1)}, bf16[128,3072]{1,0:T(8,128)(2,1)S(1)}, u32[]{:S(2)}, u32[]{:S(2)}) %collective-permute-start.4) | collective-permute-done | bytes 786464 | tf_op jit(solution)/shard_map/ppermute | solution.py:48
  88.2 1.5 collective-permute-start.6
  89.9 15.3 %collective-permute-done.6 = bf16[128,3072]{1,0:T(8,128)(2,1)S(1)} collective-permute-done((bf16[128,3072]{1,0:T(8,128)(2,1)S(1)}, bf16[128,3072]{1,0:T(8,128)(2,1)S(1)}, u32[]{:S(2)}, u32[]{:S(2)}) %collective-permute-start.6) | collective-permute-done | bytes 786464 | tf_op jit(solution)/shard_map/ppermute | solution.py:48
  105.4 2.3 %fusion.46 = (bf16[1024,768]{1,0:T(8,128)(2,1)}, bf16[1024,768]{1,0:T(8,128)(2,1)}, bf16[1024,768]{1,0:T(8,128)(2,1)S(1)}, bf16[1024,768]{1,0:T(8,128)(2,1)}) fusion(bf16[1024,3072]{1,0:T(8,128)(2,1)S(1)} %bitcast.146), kind=kLoop, calls=%fused_computation.70 | loop fusion | bytes 12582912 | tf_op jit(solution)/shard_map/slice | solution.py:188
  107.7 2.6 %copy.44 = bf16[1024,768]{0,1:T(8,128)(2,1)} copy(bf16[1024,768]{1,0:T(8,128)(2,1)} %get-tuple-element.104) | data formatting | bytes 3145728 | tf_op jit(solution)/shard_map/slice | solution.py:131
  110.3 2.7 %bitcast_reduce_fusion = (f32[8,128]{1,0:T(8,128)S(1)}, f32[8,1024,128]{2,1,0:T(8,128)S(1)}) fusion(pred[1024]{0:T(1024)(128)(4,1)S(1)} %iota_compare_fusion, bf16[1024,8,96]{0,2,1:T(8,128)(2,1)} %bitcast.149, bf16[128,8,96]{0,2,1:T(8,128)(2,1)S(1)} %bitcast.166), kind=kOutput, calls=%fused_computation.2 | convolution fusion | flops 204471296 | bytes 5968896 | tf_op jit(solution)/shard_map/while/body/eval_jaxpr/ihc,jhc->hij/dot_general | solution.py:92
  113.0 1.9 %copy-done = f32[8,1024,128]{2,1,0:T(8,128)} copy-done((f32[8,1024,128]{2,1,0:T(8,128)}, f32[8,1024,128]{2,1,0:T(8,128)S(1)}, u32[]{:S(2)}) %copy-start) | copy-done | bytes 4194328
  115.9 1.6 copy.46
  117.6 6.4 %fusion.34 = (bf16[128,8,96]{0,2,1:T(8,128)(2,1)S(1)}, f32[8,128,96]{1,2,0:T(8,128)}) fusion(f32[128,8]{0,1:T(8,128)S(1)} %bitcast_add_fusion.2, f32[128,8]{0,1:T(8,128)S(1)} %get-tuple-element.109, bf16[1024,8,96]{0,2,1:T(8,128)(2,1)} %bitcast.160, f32[8,1024,128]{2,1,0:T(8,128)} %copy-done, f32[8,128]{1,0:T(8,128)S(1)} %broadcast_maximum_fusion, ...), kind=kOutput, calls=%fused_computation.49 | convolution fusion | flops 1211400192 | bytes 6370304 | tf_op jit(solution)/shard_map/while/body/eval_jaxpr/hij,jhc->hic/dot_general | solution.py:104
  125.6 1.8 convolution_bitcast_fusion
  127.4 3.7 %all-to-all-start = ((f32[2,128,768]{2,1,0:T(8,128)}), f32[2,128,768]{2,1,0:T(8,128)S(1)}, u32[]{:S(2)}, u32[]{:S(2)}) async-start(f32[2,128,768]{2,1,0:T(8,128)} %convolution_bitcast_fusion), calls=%async_computation | async-start | bytes 1572864 | tf_op jit(solution)/shard_map/all_to_all | solution.py:62
  131.1 1.7 copy.53
  133.9 5.2 %all-to-all-start.1 = ((f32[8,16,128]{2,1,0:T(8,128)}), f32[8,16,128]{2,1,0:T(8,128)S(1)}, u32[]{:S(2)}, u32[]{:S(2)}) async-start(f32[8,16,128]{2,1,0:T(8,128)} %broadcast_in_dim.112), calls=%async_computation.1 | async-start | bytes 131072 | tf_op jit(solution)/shard_map/all_to_all | solution.py:26
  139.2 2.8 %fusion.48 = f32[8,1024,128]{2,1,0:T(8,128)} fusion(bf16[1024,8,96]{0,2,1:T(8,128)(2,1)S(1)} %bitcast.151, bf16[128,8,96]{0,2,1:T(8,128)(2,1)S(1)} %bitcast.165), kind=kOutput, calls=%fused_computation.72 | convolution fusion | flops 201326592 | bytes 5963776 | tf_op jit(solution)/shard_map/while/body/eval_jaxpr/ihc,jhc->hij/dot_general | solution.py:92
  142.0 5.7 %fusion.26 = bf16[8,128,96]{1,2,0:T(8,128)(2,1)S(1)} fusion(bf16[1024,8,96]{0,2,1:T(8,128)(2,1)} %bitcast.150, f32[8,1024,128]{2,1,0:T(8,128)} %copy-done, bf16[128,8,96]{0,2,1:T(8,128)(2,1)S(1)} %bitcast.170, bf16[1024,8,96]{0,2,1:T(8,128)(2,1)} %bitcast.161, f32[8,128]{1,0:T(8,128)S(1)} %fusion.31, f32[8,128]{1,0:T(8,128)S(1)} %get-tuple-element.107, ...), kind=kOutput, calls=%fused_computation.29 | convolution fusion | flops 410091520 | bytes 7742464 | tf_op jit(solution)/shard_map/while/body/eval_jaxpr/hij,jhc->hic/dot_general | solution.py:157
  149.3 1.6 copy.55
  151.0 6.4 %fusion.27 = bf16[8,128,96]{1,2,0:T(8,128)(2,1)S(1)} fusion(bf16[1024,8,96]{0,2,1:T(8,128)(2,1)} %bitcast.152, f32[8,1024,128]{2,1,0:T(8,128)} %fusion.48, bf16[1024,8,96]{0,2,1:T(8,128)(2,1)} %bitcast.162, bf16[128,8,96]{0,2,1:T(8,128)(2,1)S(1)} %bitcast.173, f32[8,1024]{1,0:T(8,128)S(1)} %get-tuple-element.106, f32[8,1024]{1,0:T(8,128)S(1)} %get-tuple-element.105, ...), kind=kOutput, calls=%fused_computation.30 | convolution fusion | flops 410091520 | bytes 7798912 | tf_op jit(solution)/shard_map/while/body/eval_jaxpr/hij,ihc->hjc/dot_general | solution.py:175
  158.3 12.4 %all-gather.3.cloned.1.call-done = bf16[1024,768]{1,0:T(8,128)(2,1)} async-done(((bf16[128,768]{1,0:T(8,128)(2,1)}), bf16[1024,768]{1,0:T(8,128)(2,1)}) %all-gather.3.cloned.1.call-update) | async-done | bytes 1572880 | tf_op jit(solution)/shard_map/all_gather | solution.py:140
  170.6 2.7 %fusion.23 = f32[2,768,96]{1,2,0:T(8,128)} fusion(bf16[2,96,1024]{2,1,0:T(8,128)(2,1)S(1)} %bitcast.171, bf16[1024,768]{1,0:T(8,128)(2,1)} %all-gather.3.cloned.1.call-done), kind=kOutput, calls=%fused_computation.28 | convolution fusion | flops 301989888 | bytes 2555904 | tf_op jit(solution)/shard_map/dot_general | solution.py:141
  173.4 3.5 %all-to-all-start.3 = ((f32[2,768,96]{1,2,0:T(8,128)}), f32[2,768,96]{1,2,0:T(8,128)S(1)}, u32[]{:S(2)}, u32[]{:S(2)}) async-start(f32[2,768,96]{1,2,0:T(8,128)} %fusion.23), calls=%async_computation.3 | async-start | bytes 1179648 | tf_op jit(solution)/shard_map/all_to_all | solution.py:62
  176.9 3.3 %fusion.28 = bf16[8,128,96]{1,2,0:T(8,128)(2,1)S(1)} fusion(bf16[1024,8,96]{0,2,1:T(8,128)(2,1)S(1)} %bitcast.163, f32[8,1024,128]{2,1,0:T(8,128)} %fusion.48, f32[8,1024]{1,0:T(8,128)S(1)} %get-tuple-element.105, pred[128]{0:T(512)(128)(4,1)S(1)} %add_compare_fusion), kind=kOutput, calls=%fused_computation.31 | convolution fusion | flops 205619200 | bytes 5996672 | tf_op jit(solution)/shard_map/while/body/eval_jaxpr/hij,ihc->hjc/dot_general | solution.py:178
  181.0 3.8 %all-to-all-done.3 = f32[2,768,96]{1,2,0:T(8,128)S(1)} async-done(((f32[2,768,96]{1,2,0:T(8,128)}), f32[2,768,96]{1,2,0:T(8,128)S(1)}, u32[]{:S(2)}, u32[]{:S(2)}) %all-to-all-start.3) | async-done | bytes 589856 | tf_op jit(solution)/shard_map/all_to_all | solution.py:62
  (81 shorter events, 17.0 us)
Async XLA Ops:
  7.2 18.3 %copy-start.17 = (s32[8]{0:T(128)S(1)}, s32[8]{0:T(128)}, u32[]{:S(2)}) copy-start(s32[8]{0:T(128)} %constant.143.clone) | copy-start | bytes 100
  7.2 23.6 %copy-start.16 = (s32[8]{0:T(128)S(1)}, s32[8]{0:T(128)}, u32[]{:S(2)}) copy-start(s32[8]{0:T(128)} %constant.142.clone) | copy-start | bytes 100
  7.2 32.7 %copy-start.5 = (bf16[1,128,768]{2,1,0:T(8,128)(2,1)S(1)}, bf16[1,128,768]{2,1,0:T(8,128)(2,1)}, u32[]{:S(2)}) copy-start(bf16[1,128,768]{2,1,0:T(8,128)(2,1)} %param.9) | copy-start | bytes 589828
  7.2 35.1 %copy-start.6 = (bf16[1,128,768]{2,1,0:T(8,128)(2,1)S(1)}, bf16[1,128,768]{2,1,0:T(8,128)(2,1)}, u32[]{:S(2)}) copy-start(bf16[1,128,768]{2,1,0:T(8,128)(2,1)} %param.11) | copy-start | bytes 589828
  7.2 34.3 %copy-start.7 = (bf16[1,128,768]{2,1,0:T(8,128)(2,1)S(1)}, bf16[1,128,768]{2,1,0:T(8,128)(2,1)}, u32[]{:S(2)}) copy-start(bf16[1,128,768]{2,1,0:T(8,128)(2,1)} %param.10) | copy-start | bytes 589828
  8.4 35.4 %copy-start.1 = (bf16[768,1536]{1,0:T(8,128)(2,1)S(1)}, bf16[768,1536]{1,0:T(8,128)(2,1)}, u32[]{:S(2)}) copy-start(bf16[768,1536]{1,0:T(8,128)(2,1)} %param.12) | copy-start | bytes 7077892
  15.4 35.9 %collective-permute-start = (bf16[128,3072]{1,0:T(8,128)(2,1)}, bf16[128,3072]{1,0:T(8,128)(2,1)}, u32[]{:S(2)}, u32[]{:S(2)}) collective-permute-start(bf16[128,3072]{1,0:T(8,128)(2,1)} %pad_maximum_fusion), channel_id=1, source_target_pairs={{0,4},{4,8},{8,12},{12,14},{14,10},{10,6},{6,2},{2,0},{1,5},{5,9},... | collective-permute-start | bytes 2359304 | tf_op jit(solution)/shard_map/ppermute | solution.py:48
  18.4 35.0 %collective-permute-start.1 = (bf16[128,3072]{1,0:T(8,128)(2,1)}, bf16[128,3072]{1,0:T(8,128)(2,1)}, u32[]{:S(2)}, u32[]{:S(2)}) collective-permute-start(bf16[128,3072]{1,0:T(8,128)(2,1)} %pad_maximum_fusion), channel_id=1, source_target_pairs={{4,0},{8,4},{12,8},{14,12},{10,14},{6,10},{2,6},{0,2},{5,1},{9,5},... | collective-permute-start | bytes 2359304 | tf_op jit(solution)/shard_map/ppermute | solution.py:52
  19.1 105.7 %all-to-all-start.2 = ((bf16[8,128,192]{1,2,0:T(8,128)(2,1)}), bf16[8,128,192]{1,2,0:T(8,128)(2,1)S(1)}, u32[]{:S(2)}, u32[]{:S(2)}) async-start(bf16[8,128,192]{1,2,0:T(8,128)(2,1)} %bitcast.164), calls=%async_computation.2 | async-start | bytes 786432 | tf_op jit(solution)/shard_map/all_to_all | solution.py:130
  25.4 145.2 %all-gather.3.cloned.1.call-start = ((), (), s32[]{:S(2)}) async-start(), calls=%async_computation.4 | async-start | bytes 1769472 | tf_op jit(solution)/shard_map/all_gather | solution.py:140
  51.4 19.0 %collective-permute-start.2 = (bf16[128,3072]{1,0:T(8,128)(2,1)}, bf16[128,3072]{1,0:T(8,128)(2,1)S(1)}, u32[]{:S(2)}, u32[]{:S(2)}) collective-permute-start(bf16[128,3072]{1,0:T(8,128)(2,1)} %collective-permute-done), channel_id=1, source_target_pairs={{0,4},{4,8},{8,12},{12,14},{14,10},{10,6},{6,2},{2,0},{1,5},{5,9},... | collective-permute-start | bytes 2359304 | tf_op jit(solution)/shard_map/ppermute | solution.py:48
  53.4 18.7 %collective-permute-start.3 = (bf16[128,3072]{1,0:T(8,128)(2,1)}, bf16[128,3072]{1,0:T(8,128)(2,1)S(1)}, u32[]{:S(2)}, u32[]{:S(2)}) collective-permute-start(bf16[128,3072]{1,0:T(8,128)(2,1)} %collective-permute-done.1), channel_id=1, source_target_pairs={{4,0},{8,4},{12,8},{14,12},{10,14},{6,10},{2,6},{0,2},{5,1},{9,5},... | collective-permute-start | bytes 2359304 | tf_op jit(solution)/shard_map/ppermute | solution.py:52
  70.4 17.9 %collective-permute-start.4 = (bf16[128,3072]{1,0:T(8,128)(2,1)S(1)}, bf16[128,3072]{1,0:T(8,128)(2,1)S(1)}, u32[]{:S(2)}, u32[]{:S(2)}) collective-permute-start(bf16[128,3072]{1,0:T(8,128)(2,1)S(1)} %collective-permute-done.2), channel_id=1, source_target_pairs={{0,4},{4,8},{8,12},{12,14},{14,10},{10,6},{6,2},{2,0},{1,5},{5,9},... | collective-permute-start | bytes 2359304 | tf_op jit(solution)/shard_map/ppermute | solution.py:48
  72.1 17.8 %collective-permute-start.5 = (bf16[128,3072]{1,0:T(8,128)(2,1)S(1)}, bf16[128,3072]{1,0:T(8,128)(2,1)S(1)}, u32[]{:S(2)}, u32[]{:S(2)}) collective-permute-start(bf16[128,3072]{1,0:T(8,128)(2,1)S(1)} %collective-permute-done.3), channel_id=1, source_target_pairs={{4,0},{8,4},{12,8},{14,12},{10,14},{6,10},{2,6},{0,2},{5,1},{9,5},... | collective-permute-start | bytes 2359304 | tf_op jit(solution)/shard_map/ppermute | solution.py:52
  88.2 17.0 %collective-permute-start.6 = (bf16[128,3072]{1,0:T(8,128)(2,1)S(1)}, bf16[128,3072]{1,0:T(8,128)(2,1)S(1)}, u32[]{:S(2)}, u32[]{:S(2)}) collective-permute-start(bf16[128,3072]{1,0:T(8,128)(2,1)S(1)} %collective-permute-done.4), channel_id=1, source_target_pairs={{0,4},{4,8},{8,12},{12,14},{14,10},{10,6},{6,2},{2,0},{1,5},{5,9},... | collective-permute-start | bytes 2359304 | tf_op jit(solution)/shard_map/ppermute | solution.py:48
  105.3 5.0 %copy-start.10 = (bf16[1,128,768]{1,2,0:T(8,128)(2,1)S(1)}, bf16[1,128,768]{1,2,0:T(8,128)(2,1)}, u32[]{:S(2)}) copy-start(bf16[1,128,768]{1,2,0:T(8,128)(2,1)} %copy.45) | copy-start | bytes 589828
  113.0 2.0 %copy-start = (f32[8,1024,128]{2,1,0:T(8,128)}, f32[8,1024,128]{2,1,0:T(8,128)S(1)}, u32[]{:S(2)}) copy-start(f32[8,1024,128]{2,1,0:T(8,128)S(1)} %get-tuple-element.131) | copy-start | bytes 12582916
  117.6 8.1 %copy-start.2 = (bf16[1536,768]{1,0:T(8,128)(2,1)S(1)}, bf16[1536,768]{1,0:T(8,128)(2,1)}, u32[]{:S(2)}) copy-start(bf16[1536,768]{1,0:T(8,128)(2,1)} %copy.68) | copy-start | bytes 7077892
  125.6 7.2 %copy-start.11 = (bf16[128,768]{0,1:T(8,128)(2,1)S(1)}, bf16[128,768]{0,1:T(8,128)(2,1)}, u32[]{:S(2)}) copy-start(bf16[128,768]{0,1:T(8,128)(2,1)} %copy.50) | copy-start | bytes 589828
  125.6 7.2 %copy-start.13 = (f32[8,128,96]{1,2,0:T(8,128)S(1)}, f32[8,128,96]{1,2,0:T(8,128)}, u32[]{:S(2)}) copy-start(f32[8,128,96]{1,2,0:T(8,128)} %get-tuple-element.133) | copy-start | bytes 1179652
  127.4 11.7 %copy-start.9 = (bf16[1,128,768]{1,2,0:T(8,128)(2,1)S(1)}, bf16[1,128,768]{1,2,0:T(8,128)(2,1)}, u32[]{:S(2)}) copy-start(bf16[1,128,768]{1,2,0:T(8,128)(2,1)} %copy.54) | copy-start | bytes 589828
  127.4 5.6 %all-to-all-start = ((f32[2,128,768]{2,1,0:T(8,128)}), f32[2,128,768]{2,1,0:T(8,128)S(1)}, u32[]{:S(2)}, u32[]{:S(2)}) async-start(f32[2,128,768]{2,1,0:T(8,128)} %convolution_bitcast_fusion), calls=%async_computation | async-start | bytes 1572864 | tf_op jit(solution)/shard_map/all_to_all | solution.py:62
  132.8 6.3 %copy-start.4 = (bf16[1024,768]{0,1:T(8,128)(2,1)}, bf16[1024,768]{0,1:T(8,128)(2,1)S(1)}, u32[]{:S(2)}) copy-start(bf16[1024,768]{0,1:T(8,128)(2,1)S(1)} %copy.53) | copy-start | bytes 4718596
  133.9 17.1 %all-to-all-start.1 = ((f32[8,16,128]{2,1,0:T(8,128)}), f32[8,16,128]{2,1,0:T(8,128)S(1)}, u32[]{:S(2)}, u32[]{:S(2)}) async-start(f32[8,16,128]{2,1,0:T(8,128)} %broadcast_in_dim.112), calls=%async_computation.1 | async-start | bytes 131072 | tf_op jit(solution)/shard_map/all_to_all | solution.py:26
  142.0 5.8 %copy-start.15 = (bf16[1,128,768]{2,1,0:T(8,128)(2,1)S(1)}, bf16[1,128,768]{2,1,0:T(8,128)(2,1)}, u32[]{:S(2)}) copy-start(bf16[1,128,768]{2,1,0:T(8,128)(2,1)} %param.13) | copy-start | bytes 589828
  142.0 7.3 %copy-start.3 = (bf16[1024,768]{1,0:T(8,128)(2,1)S(1)}, bf16[1024,768]{1,0:T(8,128)(2,1)}, u32[]{:S(2)}) copy-start(bf16[1024,768]{1,0:T(8,128)(2,1)} %get-tuple-element.101) | copy-start | bytes 4718596
  147.8 3.2 %copy-start.14 = (bf16[1,128,768]{1,2,0:T(8,128)(2,1)S(1)}, bf16[1,128,768]{1,2,0:T(8,128)(2,1)}, u32[]{:S(2)}) copy-start(bf16[1,128,768]{1,2,0:T(8,128)(2,1)} %copy.56) | copy-start | bytes 589828
  151.0 19.6 %copy-start.12 = (bf16[1024,192]{0,1:T(8,128)(2,1)S(1)}, bf16[1024,192]{0,1:T(8,128)(2,1)}, u32[]{:S(2)}) copy-start(bf16[1024,192]{0,1:T(8,128)(2,1)} %copy_bitcast_fusion) | copy-start | bytes 1179652
  157.4 19.4 %copy-start.8 = (bf16[1024,768]{0,1:T(8,128)(2,1)S(1)}, bf16[1024,768]{0,1:T(8,128)(2,1)}, u32[]{:S(2)}) copy-start(bf16[1024,768]{0,1:T(8,128)(2,1)} %copy.55) | copy-start | bytes 4718596
  173.4 11.4 %all-to-all-start.3 = ((f32[2,768,96]{1,2,0:T(8,128)}), f32[2,768,96]{1,2,0:T(8,128)S(1)}, u32[]{:S(2)}, u32[]{:S(2)}) async-start(f32[2,768,96]{1,2,0:T(8,128)} %fusion.23), calls=%async_computation.3 | async-start | bytes 1179648 | tf_op jit(solution)/shard_map/all_to_all | solution.py:62
Sparse Core Ops, SparseCore 0:
  124.9 45.6 all-gather.2

commit v5 on v1

--- a/solution.py
+++ b/solution.py
@@ -76,7 +76,7 @@
 
 def shards_body(queries, keys, values, out_weight, residual, lengths, grad_out):
     scale = 1.0 / math.sqrt(HEAD_DIM)
-    highest = lax.Precision.HIGHEST
+    highest = lax.Precision.HIGH
     own_q = queries[0]
     own_k = keys[0]
     own_v = values[0]
@@ -124,8 +124,7 @@
     g_cols = jnp.transpose(grad_full.reshape(frames_here, n_dp, n_seq, col_width), (2, 0, 1, 3))
     g_cols = g_cols.reshape(n_seq, frames_here, n_dp * col_width)
     g_mine = lax.all_to_all(g_cols, "seq", 0, 0, tiled=True).reshape(-1, n_dp * col_width)
-    qg_rows = jnp.concatenate([own_q, grad_attn], axis=1)
-    qg_all = lax.all_gather(qg_rows, "seq", axis=0, tiled=True)
+    qg_all = ring_gather(jnp.concatenate([own_q, grad_attn], axis=1), "seq").reshape(-1, 2 * width)
     k_all = kv_all[:, :width]
     v_all = kv_all[:, width:]
     run_max, run_sum, total = by_blocks(forward_step, start_state, (k_all, v_all))

time: 255 us -> 193 us (0.76); the launches traced: 251 us -> 192 us
  waiting for transfers between devices: 79.8 us -> 32.7 us
  local copies, waits for them, and re-layouts: 79.1 us -> 45.9 us
  starting transfers between devices: 23.9 us -> 37.2 us
  matrix products: 26.2 us -> 33.2 us
    all_gather x1 -> x0, waiting for transfers between devices: 45.2 us -> none  [shards_body(): qg_all = lax.all_gather(qg_rows, 'seq', axis=0, tiled=True)]
    dynamic_update_slice x5 -> x7, local copies, waits for them, and re-layouts: 25 us -> 7.21 us  [ring_gather(): gathered = lax.dynamic_update_index_in_dim(gathered, ahead, source, 0)]
    dynamic_update_slice x3 -> x6, local copies, waits for them, and re-layouts: 20.4 us -> 5.45 us  [ring_gather(): gathered = lax.dynamic_update_index_in_dim(gathered, behind, source, 0)]
    ppermute x4 -> x8, waiting for transfers between devices: 12.3 us -> 26 us  [ring_gather(): ahead = lax.ppermute(ahead, axis_name, to_next)]
    all_to_all x1, waiting for transfers between devices: 11 us -> 0.01 us  [shards_body(): lax.all_to_all(g_cols, 'seq', 0, 0, tiled=True)]
    ppermute x4 -> x8, starting transfers between devices: 8.33 us -> 17 us  [ring_gather(): ahead = lax.ppermute(ahead, axis_name, to_next)]
    broadcast_in_dim x3 -> x0, local copies, waits for them, and re-layouts: 7.82 us -> none  [the longest x1 2.96 us: ring_gather(): gathered = lax.dynamic_update_index_in_dim(gathered, behind, source, 0)]
    unnamed x46 -> x39, local copies, waits for them, and re-layouts: 8.97 us -> 13.5 us
  transfers between devices with their start and end apart: 13 -> 19, of which waited for: 7 -> 8; matrix products, arithmetic and copies ran while one was open for 25% -> 32% of each run, Pallas kernels for 0% -> 0%
where the time goes in v5:
time: 193 us; the launch traced here: 192 us
  local copies, waits for them, and re-layouts  45.9 us (24%)
  starting transfers between devices  37.2 us (19%)
  matrix products  33.2 us (17%)
  waiting for transfers between devices  32.7 us (17%)
  between operations  32.6 us (17%)
  other arithmetic  8.02 us (4%)
  blocking collectives  2.21 us (1%)
    ppermute x8, waiting for transfers between devices, ring_gather(): ahead = lax.ppermute(ahead, axis_name, to_next)  26 us
    ppermute x8, starting transfers between devices, ring_gather(): ahead = lax.ppermute(ahead, axis_name, to_next)  17 us
    unnamed x39, local copies, waits for them, and re-layouts  13.5 us
    all_to_all x2, starting transfers between devices, scatter_sum(): return jnp.sum(lax.all_to_all(pieces, axis_name, 0, 0, tiled=True), axis=0)  7.81 us
    dynamic_update_slice x7, local copies, waits for them, and re-layouts, ring_gather(): gathered = lax.dynamic_update_index_in_dim(gathered, ahead, source, 0)  7.21 us
    all_to_all x1, starting transfers between devices, shards_body(): lax.all_to_all(g_cols, 'seq', 0, 0, tiled=True)  6.39 us
    dot_general x1, matrix products, key_step(): jnp.einsum('hij,ihc->hjc', dscores, q_part, preferred_element_type=jnp.fl...  5.96 us
    dot_general x1, matrix products, query_step(): jnp.einsum('hij,jhc->hic', dscores, split_heads(k_rows), preferred_elemen...  5.88 us
  transfers between devices with their start and end apart: 19, of which 8 were waited for; matrix products, arithmetic and copies ran while one was open for 32% of the time, Pallas kernels for 0%

profile of v5, /device:TPU:0, one launch (start us, length us, event | category | flops | bytes accessed | tf_op | source)
XLA Modules:
  0.0 191.9 jit_solution(12081124121676223496)
XLA Ops:
  8.3 2.2 %all-gather = bf16[1,128,1536]{1,2,0:T(8,128)(2,1)S(1)} all-gather(bf16[1,128,768]{1,2,0:T(8,128)(2,1)S(1)} %copy.52), channel_id=2, replica_groups=mesh['dp'=2,'seq'=8,'tensor'=2] {'tensor'}, dimensions={2}, use_global_device_ids=true | all-gather | bytes 589824 | tf_op jit(solution)/shard_map/all_gather | solution.py:114
  10.6 2.6 %convolution_convert_fusion = bf16[128,768]{1,0:T(8,128)(2,1)S(1)} fusion(bf16[768,1536]{1,0:T(8,128)(2,1)} %param.14, bf16[1,128,1536]{1,2,0:T(8,128)(2,1)S(1)} %all-gather), kind=kOutput, calls=%fused_computation.32 | convolution fusion | flops 302088192 | bytes 2949120 | tf_op jit(solution)/shard_map/dot_general | solution.py:115
  13.9 2.9 %collective-permute-start.7 = (bf16[128,1536]{1,0:T(8,128)(2,1)}, bf16[128,1536]{1,0:T(8,128)(2,1)}, u32[]{:S(2)}, u32[]{:S(2)}) collective-permute-start(bf16[128,1536]{1,0:T(8,128)(2,1)} %pad_maximum_fusion.1), channel_id=1, source_target_pairs={{0,4},{4,8},{8,12},{12,14},{14,10},{10,6},{6,2},{2,0},{1,5},{5,9},... | collective-permute-start | bytes 1179656 | tf_op jit(solution)/shard_map/ppermute | solution.py:48
  17.7 2.0 %collective-permute-start = (bf16[128,1536]{1,0:T(8,128)(2,1)}, bf16[128,1536]{1,0:T(8,128)(2,1)}, u32[]{:S(2)}, u32[]{:S(2)}) collective-permute-start(bf16[128,1536]{1,0:T(8,128)(2,1)} %pad_maximum_fusion), channel_id=1, source_target_pairs={{0,4},{4,8},{8,12},{12,14},{14,10},{10,6},{6,2},{2,0},{1,5},{5,9},... | collective-permute-start | bytes 1179656 | tf_op jit(solution)/shard_map/ppermute | solution.py:48
  20.5 6.4 %all-to-all-start.2 = ((bf16[8,128,192]{1,2,0:T(8,128)(2,1)}), bf16[8,128,192]{1,2,0:T(8,128)(2,1)}, u32[]{:S(2)}, u32[]{:S(2)}) async-start(bf16[8,128,192]{1,2,0:T(8,128)(2,1)} %bitcast.68), calls=%async_computation.2 | async-start | bytes 786432 | tf_op jit(solution)/shard_map/all_to_all | solution.py:126
  27.6 1.9 %broadcast.96.clone = bf16[8,128,1536]{2,1,0:T(8,128)(2,1)} broadcast(bf16[]{:T(256)} %constant.185.clone.1), dimensions={} | broadcast | bytes 3145730 | tf_op jit(solution)/shard_map/broadcast.8
  48.1 2.5 %copy.71 = bf16[1536,768]{1,0:T(8,128)(2,1)} copy(bf16[1536,768]{0,1:T(8,128)(2,1)S(1)} %bitcast.164) | data formatting | bytes 4718592 | tf_op jit(solution)/shard_map/dot_general | solution.py:134
  55.3 2.1 %collective-permute-start.9 = (bf16[128,1536]{1,0:T(8,128)(2,1)}, bf16[128,1536]{1,0:T(8,128)(2,1)}, u32[]{:S(2)}, u32[]{:S(2)}) collective-permute-start(bf16[128,1536]{1,0:T(8,128)(2,1)} %collective-permute-done.7), channel_id=1, source_target_pairs={{0,4},{4,8},{8,12},{12,14},{14,10},{10,6},{6,2},{2,0},{1,5},{5,9},... | collective-permute-start | bytes 1179656 | tf_op jit(solution)/shard_map/ppermute | solution.py:48
  57.4 2.0 %collective-permute-start.2 = (bf16[128,1536]{1,0:T(8,128)(2,1)}, bf16[128,1536]{1,0:T(8,128)(2,1)}, u32[]{:S(2)}, u32[]{:S(2)}) collective-permute-start(bf16[128,1536]{1,0:T(8,128)(2,1)} %collective-permute-done), channel_id=1, source_target_pairs={{0,4},{4,8},{8,12},{12,14},{14,10},{10,6},{6,2},{2,0},{1,5},{5,9},... | collective-permute-start | bytes 1179656 | tf_op jit(solution)/shard_map/ppermute | solution.py:48
  67.6 2.0 %collective-permute-start.11 = (bf16[128,1536]{1,0:T(8,128)(2,1)}, bf16[128,1536]{1,0:T(8,128)(2,1)S(1)}, u32[]{:S(2)}, u32[]{:S(2)}) collective-permute-start(bf16[128,1536]{1,0:T(8,128)(2,1)} %collective-permute-done.9), channel_id=1, source_target_pairs={{0,4},{4,8},{8,12},{12,14},{14,10},{10,6},{6,2},{2,0},{1,5},{5,9},... | collective-permute-start | bytes 1179656 | tf_op jit(solution)/shard_map/ppermute | solution.py:48
  69.7 6.4 %collective-permute-done.2 = bf16[128,1536]{1,0:T(8,128)(2,1)} collective-permute-done((bf16[128,1536]{1,0:T(8,128)(2,1)}, bf16[128,1536]{1,0:T(8,128)(2,1)}, u32[]{:S(2)}, u32[]{:S(2)}) %collective-permute-start.2) | collective-permute-done | bytes 393248 | tf_op jit(solution)/shard_map/ppermute | solution.py:48
  76.0 2.0 %collective-permute-start.4 = (bf16[128,1536]{1,0:T(8,128)(2,1)}, bf16[128,1536]{1,0:T(8,128)(2,1)S(1)}, u32[]{:S(2)}, u32[]{:S(2)}) collective-permute-start(bf16[128,1536]{1,0:T(8,128)(2,1)} %collective-permute-done.2), channel_id=1, source_target_pairs={{0,4},{4,8},{8,12},{12,14},{14,10},{10,6},{6,2},{2,0},{1,5},{5,9},... | collective-permute-start | bytes 1179656 | tf_op jit(solution)/shard_map/ppermute | solution.py:48
  84.4 2.0 %collective-permute-start.13 = (bf16[128,1536]{1,0:T(8,128)(2,1)S(1)}, bf16[128,1536]{1,0:T(8,128)(2,1)S(1)}, u32[]{:S(2)}, u32[]{:S(2)}) collective-permute-start(bf16[128,1536]{1,0:T(8,128)(2,1)S(1)} %collective-permute-done.11), channel_id=1, source_target_pairs={{0,4},{4,8},{8,12},{12,14},{14,10},{10,6},{6,2},{2,0},{1,5},{5,9},... | collective-permute-start | bytes 1179656 | tf_op jit(solution)/shard_map/ppermute | solution.py:48
  86.4 6.4 %collective-permute-done.4 = bf16[128,1536]{1,0:T(8,128)(2,1)S(1)} collective-permute-done((bf16[128,1536]{1,0:T(8,128)(2,1)}, bf16[128,1536]{1,0:T(8,128)(2,1)S(1)}, u32[]{:S(2)}, u32[]{:S(2)}) %collective-permute-start.4) | collective-permute-done | bytes 393248 | tf_op jit(solution)/shard_map/ppermute | solution.py:48
  92.8 2.0 %collective-permute-start.6 = (bf16[128,1536]{1,0:T(8,128)(2,1)S(1)}, bf16[128,1536]{1,0:T(8,128)(2,1)S(1)}, u32[]{:S(2)}, u32[]{:S(2)}) collective-permute-start(bf16[128,1536]{1,0:T(8,128)(2,1)S(1)} %collective-permute-done.4), channel_id=1, source_target_pairs={{0,4},{4,8},{8,12},{12,14},{14,10},{10,6},{6,2},{2,0},{1,5},{5,9},... | collective-permute-start | bytes 1179656 | tf_op jit(solution)/shard_map/ppermute | solution.py:48
  96.5 4.8 %collective-permute-done.13 = bf16[128,1536]{1,0:T(8,128)(2,1)S(1)} collective-permute-done((bf16[128,1536]{1,0:T(8,128)(2,1)S(1)}, bf16[128,1536]{1,0:T(8,128)(2,1)S(1)}, u32[]{:S(2)}, u32[]{:S(2)}) %collective-permute-start.13) | collective-permute-done | bytes 393248 | tf_op jit(solution)/shard_map/ppermute | solution.py:48
  101.2 6.2 %collective-permute-done.6 = bf16[128,1536]{1,0:T(8,128)(2,1)S(1)} collective-permute-done((bf16[128,1536]{1,0:T(8,128)(2,1)S(1)}, bf16[128,1536]{1,0:T(8,128)(2,1)S(1)}, u32[]{:S(2)}, u32[]{:S(2)}) %collective-permute-start.6) | collective-permute-done | bytes 393248 | tf_op jit(solution)/shard_map/ppermute | solution.py:48
  108.2 1.8 fusion.47
  113.2 1.9 %copy-done = f32[8,1024,128]{2,1,0:T(8,128)} copy-done((f32[8,1024,128]{2,1,0:T(8,128)}, f32[8,1024,128]{2,1,0:T(8,128)S(1)}, u32[]{:S(2)}) %copy-start) | copy-done | bytes 4194328
  117.7 5.7 %fusion.35 = (bf16[128,8,96]{0,2,1:T(8,128)(2,1)S(1)}, f32[8,128,96]{1,2,0:T(8,128)}) fusion(f32[128,8]{0,1:T(8,128)S(1)} %bitcast_add_fusion.2, f32[128,8]{0,1:T(8,128)S(1)} %get-tuple-element.109, bf16[1024,8,96]{0,2,1:T(8,128)(2,1)} %bitcast.177, f32[8,1024,128]{2,1,0:T(8,128)} %copy-done, f32[8,128]{1,0:T(8,128)S(1)} %broadcast_maximum_fusion, ...), kind=kOutput, calls=%fused_computation.51 | convolution fusion | flops 607420416 | bytes 6370304 | tf_op jit(solution)/shard_map/while/body/eval_jaxpr/hij,jhc->hic/dot_general | solution.py:104
  124.2 1.9 convolution_bitcast_fusion
  126.1 4.3 %all-to-all-start = ((f32[2,128,768]{2,1,0:T(8,128)}), f32[2,128,768]{2,1,0:T(8,128)}, u32[]{:S(2)}, u32[]{:S(2)}) async-start(f32[2,128,768]{2,1,0:T(8,128)} %convolution_bitcast_fusion), calls=%async_computation | async-start | bytes 1572864 | tf_op jit(solution)/shard_map/all_to_all | solution.py:62
  130.4 3.3 %fusion.46 = (bf16[1024,768]{1,0:T(8,128)(2,1)}, bf16[1024,768]{1,0:T(8,128)(2,1)S(1)}) fusion(bf16[1024,1536]{1,0:T(8,128)(2,1)} %bitcast.53), kind=kLoop, calls=%fused_computation.79 | loop fusion | bytes 6291456 | tf_op jit(solution)/shard_map/slice | solution.py:185
  136.3 5.7 %all-to-all-start.1 = ((f32[8,16,128]{2,1,0:T(8,128)}), f32[8,16,128]{2,1,0:T(8,128)}, u32[]{:S(2)}, u32[]{:S(2)}) async-start(f32[8,16,128]{2,1,0:T(8,128)} %broadcast_in_dim.140), calls=%async_computation.1 | async-start | bytes 131072 | tf_op jit(solution)/shard_map/all_to_all | solution.py:26
  143.3 3.9 %fusion.49 = f32[8,1024,128]{2,1,0:T(8,128)} fusion(bf16[1024,8,96]{0,2,1:T(8,128)(2,1)S(1)} %bitcast.168, bf16[128,8,96]{0,2,1:T(8,128)(2,1)} %bitcast.181), kind=kOutput, calls=%fused_computation.82 | convolution fusion | flops 201326592 | bytes 5963776 | tf_op jit(solution)/shard_map/while/body/eval_jaxpr/ihc,jhc->hij/dot_general | solution.py:92
  147.1 5.9 %fusion.26 = bf16[8,128,96]{1,2,0:T(8,128)(2,1)} fusion(bf16[1024,8,96]{0,2,1:T(8,128)(2,1)S(1)} %bitcast.167, f32[8,1024,128]{2,1,0:T(8,128)} %copy-done, bf16[128,8,96]{0,2,1:T(8,128)(2,1)} %bitcast.185, bf16[1024,8,96]{0,2,1:T(8,128)(2,1)} %bitcast.178, f32[8,128]{1,0:T(8,128)S(1)} %fusion.31, f32[8,128]{1,0:T(8,128)S(1)} %get-tuple-element.107, ...), kind=kOutput, calls=%fused_computation.29 | convolution fusion | flops 410091520 | bytes 7742464 | tf_op jit(solution)/shard_map/while/body/eval_jaxpr/hij,jhc->hic/dot_general | solution.py:154
  159.5 6.0 %fusion.27 = bf16[8,128,96]{1,2,0:T(8,128)(2,1)} fusion(bf16[1024,8,96]{0,2,1:T(8,128)(2,1)S(1)} %bitcast.169, f32[8,1024,128]{2,1,0:T(8,128)} %fusion.49, bf16[1024,8,96]{0,2,1:T(8,128)(2,1)S(1)} %bitcast.179, bf16[128,8,96]{0,2,1:T(8,128)(2,1)} %bitcast.188, f32[8,1024]{1,0:T(8,128)} %get-tuple-element.106, f32[8,1024]{1,0:T(8,128)} %get-tuple-element.105, ...), kind=kOutput, calls=%fused_computation.30 | convolution fusion | flops 410091520 | bytes 7798912 | tf_op jit(solution)/shard_map/while/body/eval_jaxpr/hij,ihc->hjc/dot_general | solution.py:172
  167.3 2.9 %all-gather.3.cloned.1.call-done = bf16[1024,768]{1,0:T(8,128)(2,1)} async-done(((bf16[128,768]{1,0:T(8,128)(2,1)}), bf16[1024,768]{1,0:T(8,128)(2,1)}) %all-gather.3.cloned.1.call-update) | async-done | bytes 1572880 | tf_op jit(solution)/shard_map/all_gather | solution.py:137
  170.1 2.8 %fusion.23 = f32[2,768,96]{1,2,0:T(8,128)} fusion(bf16[2,96,1024]{2,1,0:T(8,128)(2,1)S(1)} %bitcast.187, bf16[1024,768]{1,0:T(8,128)(2,1)} %all-gather.3.cloned.1.call-done), kind=kOutput, calls=%fused_computation.28 | convolution fusion | flops 301989888 | bytes 2555904 | tf_op jit(solution)/shard_map/dot_general | solution.py:138
  172.9 3.5 %all-to-all-start.3 = ((f32[2,768,96]{1,2,0:T(8,128)}), f32[2,768,96]{1,2,0:T(8,128)S(1)}, u32[]{:S(2)}, u32[]{:S(2)}) async-start(f32[2,768,96]{1,2,0:T(8,128)} %fusion.23), calls=%async_computation.3 | async-start | bytes 1179648 | tf_op jit(solution)/shard_map/all_to_all | solution.py:62
  176.4 3.3 %fusion.28 = bf16[8,128,96]{1,2,0:T(8,128)(2,1)S(1)} fusion(bf16[1024,8,96]{0,2,1:T(8,128)(2,1)S(1)} %bitcast.180, f32[8,1024,128]{2,1,0:T(8,128)} %fusion.49, f32[8,1024]{1,0:T(8,128)S(1)} %copy-done.12, pred[128]{0:T(512)(128)(4,1)S(1)} %add_compare_fusion), kind=kOutput, calls=%fused_computation.31 | convolution fusion | flops 205619200 | bytes 5996672 | tf_op jit(solution)/shard_map/while/body/eval_jaxpr/hij,ihc->hjc/dot_general | solution.py:175
  180.5 3.8 %all-to-all-done.3 = f32[2,768,96]{1,2,0:T(8,128)S(1)} async-done(((f32[2,768,96]{1,2,0:T(8,128)}), f32[2,768,96]{1,2,0:T(8,128)S(1)}, u32[]{:S(2)}, u32[]{:S(2)}) %all-to-all-start.3) | async-done | bytes 589856 | tf_op jit(solution)/shard_map/all_to_all | solution.py:62
  (99 shorter events, 46.4 us)
Async XLA Ops:
  7.2 6.0 %copy-start.6 = (bf16[1,128,768]{2,1,0:T(8,128)(2,1)S(1)}, bf16[1,128,768]{2,1,0:T(8,128)(2,1)}, u32[]{:S(2)}) copy-start(bf16[1,128,768]{2,1,0:T(8,128)(2,1)} %param.11) | copy-start | bytes 589828
  7.2 9.7 %copy-start.7 = (bf16[1,128,768]{2,1,0:T(8,128)(2,1)S(1)}, bf16[1,128,768]{2,1,0:T(8,128)(2,1)}, u32[]{:S(2)}) copy-start(bf16[1,128,768]{2,1,0:T(8,128)(2,1)} %param.13) | copy-start | bytes 589828
  7.2 9.7 %copy-start.8 = (bf16[1,128,768]{2,1,0:T(8,128)(2,1)S(1)}, bf16[1,128,768]{2,1,0:T(8,128)(2,1)}, u32[]{:S(2)}) copy-start(bf16[1,128,768]{2,1,0:T(8,128)(2,1)} %param.12) | copy-start | bytes 589828
  13.9 41.3 %collective-permute-start.7 = (bf16[128,1536]{1,0:T(8,128)(2,1)}, bf16[128,1536]{1,0:T(8,128)(2,1)}, u32[]{:S(2)}, u32[]{:S(2)}) collective-permute-start(bf16[128,1536]{1,0:T(8,128)(2,1)} %pad_maximum_fusion.1), channel_id=1, source_target_pairs={{0,4},{4,8},{8,12},{12,14},{14,10},{10,6},{6,2},{2,0},{1,5},{5,9},... | collective-permute-start | bytes 1179656 | tf_op jit(solution)/shard_map/ppermute | solution.py:48
  16.9 40.5 %collective-permute-start.8 = (bf16[128,1536]{1,0:T(8,128)(2,1)}, bf16[128,1536]{1,0:T(8,128)(2,1)}, u32[]{:S(2)}, u32[]{:S(2)}) collective-permute-start(bf16[128,1536]{1,0:T(8,128)(2,1)} %pad_maximum_fusion.1), channel_id=1, source_target_pairs={{4,0},{8,4},{12,8},{14,12},{10,14},{6,10},{2,6},{0,2},{5,1},{9,5},... | collective-permute-start | bytes 1179656 | tf_op jit(solution)/shard_map/ppermute | solution.py:52
  16.9 13.4 %copy-start.14 = (s32[8]{0:T(128)S(1)}, s32[8]{0:T(128)}, u32[]{:S(2)}) copy-start(s32[8]{0:T(128)} %constant.202.clone) | copy-start | bytes 100
  16.9 18.7 %copy-start.13 = (s32[8]{0:T(128)S(1)}, s32[8]{0:T(128)}, u32[]{:S(2)}) copy-start(s32[8]{0:T(128)} %constant.201.clone) | copy-start | bytes 100
  17.7 39.7 %collective-permute-start = (bf16[128,1536]{1,0:T(8,128)(2,1)}, bf16[128,1536]{1,0:T(8,128)(2,1)}, u32[]{:S(2)}, u32[]{:S(2)}) collective-permute-start(bf16[128,1536]{1,0:T(8,128)(2,1)} %pad_maximum_fusion), channel_id=1, source_target_pairs={{0,4},{4,8},{8,12},{12,14},{14,10},{10,6},{6,2},{2,0},{1,5},{5,9},... | collective-permute-start | bytes 1179656 | tf_op jit(solution)/shard_map/ppermute | solution.py:48
  19.7 42.5 %collective-permute-start.1 = (bf16[128,1536]{1,0:T(8,128)(2,1)}, bf16[128,1536]{1,0:T(8,128)(2,1)}, u32[]{:S(2)}, u32[]{:S(2)}) collective-permute-start(bf16[128,1536]{1,0:T(8,128)(2,1)} %pad_maximum_fusion), channel_id=1, source_target_pairs={{4,0},{8,4},{12,8},{14,12},{10,14},{6,10},{2,6},{0,2},{5,1},{9,5},... | collective-permute-start | bytes 1179656 | tf_op jit(solution)/shard_map/ppermute | solution.py:52
  20.5 27.6 %copy-start.1 = (bf16[768,1536]{1,0:T(8,128)(2,1)S(1)}, bf16[768,1536]{1,0:T(8,128)(2,1)}, u32[]{:S(2)}) copy-start(bf16[768,1536]{1,0:T(8,128)(2,1)} %param.14) | copy-start | bytes 7077892
  20.5 44.6 %all-to-all-start.2 = ((bf16[8,128,192]{1,2,0:T(8,128)(2,1)}), bf16[8,128,192]{1,2,0:T(8,128)(2,1)}, u32[]{:S(2)}, u32[]{:S(2)}) async-start(bf16[8,128,192]{1,2,0:T(8,128)(2,1)} %bitcast.68), calls=%async_computation.2 | async-start | bytes 786432 | tf_op jit(solution)/shard_map/all_to_all | solution.py:126
  26.9 143.2 %all-gather.3.cloned.1.call-start = ((), (), s32[]{:S(2)}) async-start(), calls=%async_computation.4 | async-start | bytes 1769472 | tf_op jit(solution)/shard_map/all_gather | solution.py:137
  55.3 12.4 %collective-permute-start.9 = (bf16[128,1536]{1,0:T(8,128)(2,1)}, bf16[128,1536]{1,0:T(8,128)(2,1)}, u32[]{:S(2)}, u32[]{:S(2)}) collective-permute-start(bf16[128,1536]{1,0:T(8,128)(2,1)} %collective-permute-done.7), channel_id=1, source_target_pairs={{0,4},{4,8},{8,12},{12,14},{14,10},{10,6},{6,2},{2,0},{1,5},{5,9},... | collective-permute-start | bytes 1179656 | tf_op jit(solution)/shard_map/ppermute | solution.py:48
  57.3 12.3 %collective-permute-start.10 = (bf16[128,1536]{1,0:T(8,128)(2,1)}, bf16[128,1536]{1,0:T(8,128)(2,1)S(1)}, u32[]{:S(2)}, u32[]{:S(2)}) collective-permute-start(bf16[128,1536]{1,0:T(8,128)(2,1)} %collective-permute-done.8), channel_id=1, source_target_pairs={{4,0},{8,4},{12,8},{14,12},{10,14},{6,10},{2,6},{0,2},{5,1},{9,5},... | collective-permute-start | bytes 1179656 | tf_op jit(solution)/shard_map/ppermute | solution.py:52
  57.4 18.7 %collective-permute-start.2 = (bf16[128,1536]{1,0:T(8,128)(2,1)}, bf16[128,1536]{1,0:T(8,128)(2,1)}, u32[]{:S(2)}, u32[]{:S(2)}) collective-permute-start(bf16[128,1536]{1,0:T(8,128)(2,1)} %collective-permute-done), channel_id=1, source_target_pairs={{0,4},{4,8},{8,12},{12,14},{14,10},{10,6},{6,2},{2,0},{1,5},{5,9},... | collective-permute-start | bytes 1179656 | tf_op jit(solution)/shard_map/ppermute | solution.py:48
  62.2 18.7 %collective-permute-start.3 = (bf16[128,1536]{1,0:T(8,128)(2,1)}, bf16[128,1536]{1,0:T(8,128)(2,1)}, u32[]{:S(2)}, u32[]{:S(2)}) collective-permute-start(bf16[128,1536]{1,0:T(8,128)(2,1)} %collective-permute-done.1), channel_id=1, source_target_pairs={{4,0},{8,4},{12,8},{14,12},{10,14},{6,10},{2,6},{0,2},{5,1},{9,5},... | collective-permute-start | bytes 1179656 | tf_op jit(solution)/shard_map/ppermute | solution.py:52
  67.6 16.7 %collective-permute-start.11 = (bf16[128,1536]{1,0:T(8,128)(2,1)}, bf16[128,1536]{1,0:T(8,128)(2,1)S(1)}, u32[]{:S(2)}, u32[]{:S(2)}) collective-permute-start(bf16[128,1536]{1,0:T(8,128)(2,1)} %collective-permute-done.9), channel_id=1, source_target_pairs={{0,4},{4,8},{8,12},{12,14},{14,10},{10,6},{6,2},{2,0},{1,5},{5,9},... | collective-permute-start | bytes 1179656 | tf_op jit(solution)/shard_map/ppermute | solution.py:48
  69.6 26.0 %collective-permute-start.12 = (bf16[128,1536]{1,0:T(8,128)(2,1)S(1)}, bf16[128,1536]{1,0:T(8,128)(2,1)S(1)}, u32[]{:S(2)}, u32[]{:S(2)}) collective-permute-start(bf16[128,1536]{1,0:T(8,128)(2,1)S(1)} %collective-permute-done.10), channel_id=1, source_target_pairs={{4,0},{8,4},{12,8},{14,12},{10,14},{6,10},{2,6},{0,2},{5,1},{9,5},... | collective-permute-start | bytes 1179656 | tf_op jit(solution)/shard_map/ppermute | solution.py:52
  76.0 16.7 %collective-permute-start.4 = (bf16[128,1536]{1,0:T(8,128)(2,1)}, bf16[128,1536]{1,0:T(8,128)(2,1)S(1)}, u32[]{:S(2)}, u32[]{:S(2)}) collective-permute-start(bf16[128,1536]{1,0:T(8,128)(2,1)} %collective-permute-done.2), channel_id=1, source_target_pairs={{0,4},{4,8},{8,12},{12,14},{14,10},{10,6},{6,2},{2,0},{1,5},{5,9},... | collective-permute-start | bytes 1179656 | tf_op jit(solution)/shard_map/ppermute | solution.py:48
  80.9 15.6 %collective-permute-start.5 = (bf16[128,1536]{1,0:T(8,128)(2,1)}, bf16[128,1536]{1,0:T(8,128)(2,1)S(1)}, u32[]{:S(2)}, u32[]{:S(2)}) collective-permute-start(bf16[128,1536]{1,0:T(8,128)(2,1)} %collective-permute-done.3), channel_id=1, source_target_pairs={{4,0},{8,4},{12,8},{14,12},{10,14},{6,10},{2,6},{0,2},{5,1},{9,5},... | collective-permute-start | bytes 1179656 | tf_op jit(solution)/shard_map/ppermute | solution.py:52
  84.4 16.9 %collective-permute-start.13 = (bf16[128,1536]{1,0:T(8,128)(2,1)S(1)}, bf16[128,1536]{1,0:T(8,128)(2,1)S(1)}, u32[]{:S(2)}, u32[]{:S(2)}) collective-permute-start(bf16[128,1536]{1,0:T(8,128)(2,1)S(1)} %collective-permute-done.11), channel_id=1, source_target_pairs={{0,4},{4,8},{8,12},{12,14},{14,10},{10,6},{6,2},{2,0},{1,5},{5,9},... | collective-permute-start | bytes 1179656 | tf_op jit(solution)/shard_map/ppermute | solution.py:48
  92.8 14.6 %collective-permute-start.6 = (bf16[128,1536]{1,0:T(8,128)(2,1)S(1)}, bf16[128,1536]{1,0:T(8,128)(2,1)S(1)}, u32[]{:S(2)}, u32[]{:S(2)}) collective-permute-start(bf16[128,1536]{1,0:T(8,128)(2,1)S(1)} %collective-permute-done.4), channel_id=1, source_target_pairs={{0,4},{4,8},{8,12},{12,14},{14,10},{10,6},{6,2},{2,0},{1,5},{5,9},... | collective-permute-start | bytes 1179656 | tf_op jit(solution)/shard_map/ppermute | solution.py:48
  111.8 4.2 %copy-start.3 = (bf16[1024,768]{0,1:T(8,128)(2,1)}, bf16[1024,768]{0,1:T(8,128)(2,1)S(1)}, u32[]{:S(2)}) copy-start(bf16[1024,768]{0,1:T(8,128)(2,1)S(1)} %copy.72) | copy-start | bytes 4718596
  113.1 2.0 %copy-start = (f32[8,1024,128]{2,1,0:T(8,128)}, f32[8,1024,128]{2,1,0:T(8,128)S(1)}, u32[]{:S(2)}) copy-start(f32[8,1024,128]{2,1,0:T(8,128)S(1)} %get-tuple-element.131) | copy-start | bytes 12582916
  113.1 2.9 %copy-start.5 = (bf16[1024,768]{1,0:T(8,128)(2,1)S(1)}, bf16[1024,768]{1,0:T(8,128)(2,1)}, u32[]{:S(2)}) copy-start(bf16[1024,768]{1,0:T(8,128)(2,1)} %get-tuple-element.104) | copy-start | bytes 4718596
  117.7 6.5 %copy-start.2 = (bf16[1536,768]{1,0:T(8,128)(2,1)S(1)}, bf16[1536,768]{1,0:T(8,128)(2,1)}, u32[]{:S(2)}) copy-start(bf16[1536,768]{1,0:T(8,128)(2,1)} %copy.71) | copy-start | bytes 7077892
  126.1 9.6 %all-to-all-start = ((f32[2,128,768]{2,1,0:T(8,128)}), f32[2,128,768]{2,1,0:T(8,128)}, u32[]{:S(2)}, u32[]{:S(2)}) async-start(f32[2,128,768]{2,1,0:T(8,128)} %convolution_bitcast_fusion), calls=%async_computation | async-start | bytes 1572864 | tf_op jit(solution)/shard_map/all_to_all | solution.py:62
  136.3 21.8 %all-to-all-start.1 = ((f32[8,16,128]{2,1,0:T(8,128)}), f32[8,16,128]{2,1,0:T(8,128)}, u32[]{:S(2)}, u32[]{:S(2)}) async-start(f32[8,16,128]{2,1,0:T(8,128)} %broadcast_in_dim.140), calls=%async_computation.1 | async-start | bytes 131072 | tf_op jit(solution)/shard_map/all_to_all | solution.py:26
  143.2 3.9 %copy-start.4 = (bf16[1024,768]{0,1:T(8,128)(2,1)S(1)}, bf16[1024,768]{0,1:T(8,128)(2,1)}, u32[]{:S(2)}) copy-start(bf16[1024,768]{0,1:T(8,128)(2,1)} %copy-done.3) | copy-start | bytes 4718596
  159.5 10.6 %copy-start.11 = (bf16[1024,192]{0,1:T(8,128)(2,1)S(1)}, bf16[1024,192]{0,1:T(8,128)(2,1)}, u32[]{:S(2)}) copy-start(bf16[1024,192]{0,1:T(8,128)(2,1)} %copy_bitcast_fusion) | copy-start | bytes 1179652
  165.5 10.9 %copy-start.12 = (f32[8,1024]{1,0:T(8,128)S(1)}, f32[8,1024]{1,0:T(8,128)}, u32[]{:S(2)}) copy-start(f32[8,1024]{1,0:T(8,128)} %get-tuple-element.105) | copy-start | bytes 98308
  172.9 11.4 %all-to-all-start.3 = ((f32[2,768,96]{1,2,0:T(8,128)}), f32[2,768,96]{1,2,0:T(8,128)S(1)}, u32[]{:S(2)}, u32[]{:S(2)}) async-start(f32[2,768,96]{1,2,0:T(8,128)} %fusion.23), calls=%async_computation.3 | async-start | bytes 1179648 | tf_op jit(solution)/shard_map/all_to_all | solution.py:62
  (2 other events, 2.7 us)
Sparse Core Ops, SparseCore 0:
  124.3 45.7 all-gather.2
